TPU v7x, 256 devices: a whole 4x4x8 slice. The times are simulated.
256 devices in a mesh: seq: 64 (over x, z, core), head: 4 (over y).
Axes of the slice: x: 4, y: 4, z: 8, core: 2. Of those that a mesh axis runs over, the one named last changes fastest.
Arguments:
- queries: bfloat16 [65536, 2048], P('seq', 'head'), may hold values from -48 to 48
- keys: bfloat16 [65536, 2048], P('seq', 'head'), may hold values from -48 to 48
- values: bfloat16 [65536, 2048], P('seq', 'head'), may hold values from -6 to 6
- memory_keys: bfloat16 [65536, 2048], P('seq', 'head'), may hold values from -48 to 48
- memory_values: bfloat16 [65536, 2048], P('seq', 'head'), may hold values from -6 to 6
- block_ids: int32 [512, 4], P('seq'), may hold values from 0 to 1023, as said below
- gate_bias: float32 [16], P('head'), may hold values from -2 to 2
- out_weight: bfloat16 [2048, 2048], P('head'), may hold values from -0.5 to 0.5
Outputs:
- layer_out: bfloat16 [65536, 2048], P(('seq', 'head'))
Inputs may be any that keep to these rules, and one draw needn't show every extreme that they name: `block_ids`: block b belongs to owner b // 16. Among the 8 x 4 ids of one device's rows no id repeats; exactly 2 of them name blocks of owner 64 - 1, block 1023 always among them, and no other owner is named more than 1 times.
All inputs are finite; a program needn't handle non-finite values.
Results may differ from a plain program's by a relative error of at most 0.013.
Values may be sent and summed in bfloat16 or wider, within the bound.
No kernel may reach another device: no remote copies, remote signals or barrier semaphores. Data moves between devices by JAX's collectives and lax.ppermute only.
A program may use at most 192 MiB of HBM per device.

v0:
```python
import math

import jax
import jax.numpy as jnp
from jax import lax
from jax.sharding import PartitionSpec as P

HDIM = 128
WINDOW = 1024
QBLK = 128
MROWS = 64
TOPM = 4


NEG_FILL = -1e30


def passed_along(value, axis, steps):
    count = lax.axis_size(axis)
    leading, last = (max(0, -steps), min(count, count - steps))
    return lax.ppermute(value, axis, [(source, source + steps) for source in range(leading, last)])


def masked_softmax(scores, allowed):
    row_max = jnp.max(jnp.where(allowed, scores, NEG_FILL), axis=-1, keepdims=True)
    weights = jnp.where(allowed, jnp.exp(scores - row_max), 0.0)
    return (weights / jnp.sum(weights, axis=-1, keepdims=True)).astype(jnp.bfloat16)


def window_attention(queries, ext_keys, ext_values, first_row):
    tok_rows, features = queries.shape
    heads_here = features // HDIM
    tile_rows = math.gcd(tok_rows, 512)
    key_span = tile_rows + WINDOW
    score_scale = 1.0 / math.sqrt(HDIM)

    def per_tile(step_index):
        row_start = step_index * tile_rows
        query_tile = lax.dynamic_slice_in_dim(queries, row_start, tile_rows, 0).reshape(
            tile_rows, heads_here, HDIM
        )
        key_tile = lax.dynamic_slice_in_dim(ext_keys, row_start, key_span, 0).reshape(
            key_span, heads_here, HDIM
        )
        value_tile = lax.dynamic_slice_in_dim(ext_values, row_start, key_span, 0).reshape(
            key_span, heads_here, HDIM
        )
        scores = (
            jnp.einsum("qhd,khd->hqk", query_tile, key_tile, preferred_element_type=jnp.float32)
            * score_scale
        )
        query_pos = first_row + row_start + jnp.arange(tile_rows, dtype=jnp.int32)
        key_pos = first_row + row_start - WINDOW + jnp.arange(key_span, dtype=jnp.int32)
        allowed = (
            (key_pos[None, :] <= query_pos[:, None])
            & (key_pos[None, :] > query_pos[:, None] - WINDOW)
            & (key_pos[None, :] >= 0)
        )
        attend_weights = masked_softmax(scores, allowed[None])
        return jnp.einsum(
            "hqk,khd->qhd", attend_weights, value_tile, preferred_element_type=jnp.float32
        )

    return lax.map(per_tile, jnp.arange(tok_rows // tile_rows, dtype=jnp.int32)).reshape(
        tok_rows, heads_here, HDIM
    )


def memory_attention(queries, fetched):
    tok_rows, features = queries.shape
    heads_here = features // HDIM
    block_count = tok_rows // QBLK
    score_scale = 1.0 / math.sqrt(HDIM)
    query_blocks = queries.reshape(block_count, QBLK, heads_here, HDIM)
    key_blocks = fetched[:, 0].reshape(block_count, TOPM * MROWS, heads_here, HDIM)
    value_blocks = fetched[:, 1].reshape(block_count, TOPM * MROWS, heads_here, HDIM)
    scores = (
        jnp.einsum("bqhd,bkhd->bhqk", query_blocks, key_blocks, preferred_element_type=jnp.float32)
        * score_scale
    )
    attend_weights = masked_softmax(scores, jnp.ones(scores.shape, dtype=bool))
    remote = jnp.einsum(
        "bhqk,bkhd->bqhd", attend_weights, value_blocks, preferred_element_type=jnp.float32
    )
    return remote.reshape(tok_rows, heads_here, HDIM)


def build_table(slot_index, offset, in_use, total_slots):
    matches = (jnp.arange(total_slots, dtype=jnp.int32)[:, None] == slot_index[None, :]) & in_use[
        None, :
    ]
    return jnp.sum(jnp.where(matches, offset[None, :] + 1, 0), axis=1) - 1


def on_device(queries, keys, values, memory_keys, memory_values, block_ids, gate_bias, out_weight):
    tok_rows, features = queries.shape
    owners = lax.axis_size("seq")
    first_row = lax.axis_index("seq") * tok_rows
    edge_rows = jnp.stack((keys, values))
    before = passed_along(edge_rows, "seq", 1)
    local_part = window_attention(
        queries, jnp.concatenate([before[0], keys]), jnp.concatenate([before[1], values]), first_row
    )
    request_count = block_ids.shape[0] * block_ids.shape[1]
    wanted = block_ids.reshape(request_count)
    mem_dev = memory_keys.shape[0] // MROWS
    owner_index = wanted // mem_dev
    offset = wanted % mem_dev
    per_owner = (request_count + owners) // (owners + 1)
    positions = jnp.arange(request_count, dtype=jnp.int32)
    earlier = (positions[None, :] < positions[:, None]) & (
        owner_index[None, :] == owner_index[:, None]
    )
    rank_index = jnp.sum(earlier.astype(jnp.int32), axis=1)
    memory_store = jnp.stack(
        (
            memory_keys.reshape(mem_dev, MROWS, features),
            memory_values.reshape(mem_dev, MROWS, features),
        ),
        axis=1,
    )
    slot_width = 2 * per_owner
    slot_index = owner_index * slot_width + rank_index
    slot_table = build_table(
        slot_index, offset, jnp.ones((request_count,), dtype=bool), owners * slot_width
    ).reshape(owners, slot_width)
    asked_for = lax.all_to_all(slot_table, "seq", split_axis=0, concat_axis=0, tiled=True)
    returned = lax.all_to_all(
        memory_store[jnp.maximum(asked_for, 0)], "seq", split_axis=0, concat_axis=0, tiled=True
    )
    fetched = returned.reshape(owners * slot_width, 2, MROWS, features)[slot_index]
    remote = memory_attention(queries, fetched)
    mixing = jax.nn.sigmoid(gate_bias)[None, :, None]
    attended = (
        (mixing * remote + (1.0 - mixing) * local_part)
        .reshape(tok_rows, features)
        .astype(jnp.bfloat16)
    )
    return lax.psum_scatter(
        jnp.dot(attended, out_weight, preferred_element_type=jnp.float32).astype(jnp.bfloat16),
        "head",
        scatter_dimension=0,
        tiled=True,
    )


def solution(mesh):
    in_specs = (
        P("seq", "head"),
        P("seq", "head"),
        P("seq", "head"),
        P("seq", "head"),
        P("seq", "head"),
        P("seq", None),
        P("head"),
        P("head", None),
    )
    out_specs = P(("seq", "head"), None)
    return jax.shard_map(
        on_device, mesh=mesh, in_specs=in_specs, out_specs=out_specs, check_vma=False
    )
```

profile of v0, /device:TPU:2, one launch (start us, length us, event | category | flops | bytes accessed | tf_op | source)
XLA Modules:
  0.0 623.8 jit_solution(11828257569276125208)
XLA Ops:
  6.5 0.0 copy-start
  6.5 0.9 copy.65
  7.4 0.1 reshape.333
  7.5 0.2 convert_reduce_fusion
  7.7 0.1 select_reduce_fusion.1
  7.8 0.8 sub.50
  8.6 12.0 %all-to-all-start = ((s32[64,1,2]{2,1,0:T(1,128)}), s32[64,1,2]{2,1,0:T(1,128)S(1)}, u32[]{:S(2)}, u32[]{:S(2)}) async-start(s32[64,1,2]{2,1,0:T(1,128)} %bitcast.9), calls=%async_computation | async-start | bytes 65536 | tf_op jit(solution)/shard_map/all_to_all | solution.py:127
  20.6 3.1 pad_maximum_fusion
  23.7 5.5 all-to-all-done
  29.2 0.1 maximum_reduce_fusion
  29.3 0.1 reshape.341
  29.4 9.5 %gather_fusion = bf16[128,2,64,512]{3,2,1,0:T(8,128)(2,1)} fusion(bf16[16,2,64,512]{3,2,0,1:T(8,128)(2,1)} %pad_maximum_fusion, s32[1024]{0:T(1024)S(1)} %pad_clamp_fusion.1), kind=kCustom, calls=%fused_computation | custom fusion | bytes 33554944 | tf_op jit(solution)/shard_map/gather | solution.py:129
  38.9 6.6 %all-to-all-start.1 = ((bf16[64,2,2,64,512]{4,3,2,1,0:T(8,128)(2,1)}), bf16[64,2,2,64,512]{4,3,2,1,0:T(8,128)(2,1)}, u32[]{:S(2)}, u32[]{:S(2)}) async-start(bf16[64,2,2,64,512]{4,3,2,1,0:T(8,128)(2,1)} %bitcast.88), calls=%async_computation.1 | async-start | bytes 33554432 | tf_op jit(solution)/shard_map/all_to_all | solution.py:128
  45.5 0.0 reduce-scatter.2.cloned.1.call-start
  45.6 1.5 copy.73
  47.1 2.3 copy.74
  49.4 2.7 pad_maximum_fusion.1
  52.1 2.3 collective-permute-start
  54.4 0.1 reshape.335
  54.5 2.1 reshape.336
  56.7 0.0 copy-done.6
  56.7 0.7 broadcast_bitcast_fusion
  57.4 373.6 %collective-permute-done = bf16[2,1024,512]{1,2,0:T(8,128)(2,1)} collective-permute-done((bf16[2,1024,512]{1,2,0:T(8,128)(2,1)}, bf16[2,1024,512]{1,2,0:T(8,128)(2,1)}, u32[]{:S(2)}, u32[]{:S(2)}) %collective-permute-start) | collective-permute-done | bytes 2097184 | tf_op jit(solution)/shard_map/ppermute | solution.py:21
  431.0 1.7 slice_bitcast_fusion
  432.7 0.0 copy-done.1
  432.7 2.3 pad_maximum_fusion.2
  435.0 93.0 %while.13 = (s32[]{:T(128)}, f32[2,512,4,128]{1,0,3,2:T(2,128)}, s32[2]{0:T(128)S(1)}, bf16[2048,512]{0,1:T(8,128)(2,1)}, s32[]{:T(128)}, /*index=5*/bf16[1024,5...) while((s32[]{:T(128)}, f32[2,512,4,128]{1,0,3,2:T(2,128)}, ...), condition=%wide.region_7.8_spmd, body=%wide.region_4.7_spmd.sunk | while | flops 2444237824 | bytes 44080384 | solution.py:64
  435.0 0.7 dynamic_slice.37
  436.4 0.8 and_and_fusion.2
  437.2 3.8 constant_dynamic-slice_fusion.5
  440.9 1.1 constant_dynamic-slice_fusion.6
  442.0 1.0 copy.103
  443.0 11.4 %fusion.59 = (f32[4,512]{1,0:T(4,128)S(1)}, f32[4,512,1536]{2,1,0:T(8,128)}) fusion(pred[512,1536]{1,0:T(8,128)(4,1)S(1)} %and_and_fusion.2, bf16[512,4,128]{0,2,1:T(8,128)(2,1)} %bitcast.91, bf16[1536,4,128]{0,2,1:T(8,128)(2,1)} %bitcast.90), kind=kOutput, calls=%fused_computation.78.clone.1 | convolution fusion | flops 1629488640 | bytes 15474688 | tf_op jit(solution)/shard_map/while/body/eval_jaxpr/sub | solution.py:26
  454.4 6.3 %fusion.60 = f32[1,512,4,128]{1,3,2,0:T(8,128)S(1)} fusion(bf16[1536,4,128]{0,2,1:T(8,128)(2,1)} %bitcast.89, f32[4,512,1536]{2,1,0:T(8,128)} %get-tuple-element.237, f32[4,512]{1,0:T(4,128)S(1)} %get-tuple-element.238), kind=kOutput, calls=%fused_computation.14.clone.1 | convolution fusion | flops 811597824 | bytes 15212544 | tf_op jit(solution)/shard_map/while/body/eval_jaxpr/hqk,khd->qhd/dot_general | solution.py:60
  460.8 1.1 copy.104
  461.9 19.6 %dynamic_update_slice.9 = f32[2,512,4,128]{1,0,3,2:T(2,128)} dynamic-update-slice(f32[2,512,4,128]{1,0,3,2:T(2,128)} %get-tuple-element.253, f32[1,512,4,128]{1,0,3,2:T(1,128)S(1)} %copy.104, s32[]{:T(128)} %get-tuple-element.252, s32[]{:T(128)} %constant.116.clone.1..sunk, s32[]{:T(128)} %constant.116.clone.1..sunk, s32[]{:T(128)} %constant.116.clone.1..sunk) | dynamic-update-slice | bytes 2097156 | tf_op jit(solution)/shard_map/while/body/jit(dynamic_update_index_in_dim)/dynamic_update_slice | solution.py:64
  481.5 0.7 dynamic_slice.37
  482.9 0.8 and_and_fusion.2
  483.7 3.8 constant_dynamic-slice_fusion.5
  487.4 1.1 constant_dynamic-slice_fusion.6
  488.5 1.0 copy.103
  489.5 11.4 %fusion.59 = (f32[4,512]{1,0:T(4,128)S(1)}, f32[4,512,1536]{2,1,0:T(8,128)}) fusion(pred[512,1536]{1,0:T(8,128)(4,1)S(1)} %and_and_fusion.2, bf16[512,4,128]{0,2,1:T(8,128)(2,1)} %bitcast.91, bf16[1536,4,128]{0,2,1:T(8,128)(2,1)} %bitcast.90), kind=kOutput, calls=%fused_computation.78.clone.1 | convolution fusion | flops 1629488640 | bytes 15474688 | tf_op jit(solution)/shard_map/while/body/eval_jaxpr/sub | solution.py:26
  500.9 6.3 %fusion.60 = f32[1,512,4,128]{1,3,2,0:T(8,128)S(1)} fusion(bf16[1536,4,128]{0,2,1:T(8,128)(2,1)} %bitcast.89, f32[4,512,1536]{2,1,0:T(8,128)} %get-tuple-element.237, f32[4,512]{1,0:T(4,128)S(1)} %get-tuple-element.238), kind=kOutput, calls=%fused_computation.14.clone.1 | convolution fusion | flops 811597824 | bytes 15212544 | tf_op jit(solution)/shard_map/while/body/eval_jaxpr/hqk,khd->qhd/dot_general | solution.py:60
  507.3 1.1 copy.104
  508.4 19.6 %dynamic_update_slice.9 = f32[2,512,4,128]{1,0,3,2:T(2,128)} dynamic-update-slice(f32[2,512,4,128]{1,0,3,2:T(2,128)} %get-tuple-element.253, f32[1,512,4,128]{1,0,3,2:T(1,128)S(1)} %copy.104, s32[]{:T(128)} %get-tuple-element.252, s32[]{:T(128)} %constant.116.clone.1..sunk, s32[]{:T(128)} %constant.116.clone.1..sunk, s32[]{:T(128)} %constant.116.clone.1..sunk) | dynamic-update-slice | bytes 2097156 | tf_op jit(solution)/shard_map/while/body/jit(dynamic_update_index_in_dim)/dynamic_update_slice | solution.py:64
  528.0 3.4 copy.90
  531.4 0.0 all-to-all-done.1
  531.4 8.5 %gather_fusion.1 = bf16[32,2,64,512]{3,2,1,0:T(8,128)(2,1)} fusion(bf16[128,2,64,512]{3,2,1,0:T(8,128)(2,1)} %bitcast.11, s32[1024]{0:T(1024)S(1)} %pad_clamp_fusion), kind=kCustom, calls=%fused_computation.1 | custom fusion | bytes 8388736 | tf_op jit(solution)/shard_map/gather | solution.py:131
  539.9 4.7 fusion.39
  544.6 4.0 reshape_squeeze.7
  548.6 0.0 copy-done.2
  548.6 2.3 fusion.24
  550.9 3.0 fusion.40
  553.9 4.0 reshape_squeeze.6
  557.9 3.7 fusion.27
  561.6 0.0 copy-start.3
  561.7 0.0 copy-start.4
  561.7 0.0 copy-start.5
  561.7 1.2 copy.72
  562.9 0.3 copy-done.3
  563.2 0.0 copy-done.5
  563.2 5.0 convolution_convert_fusion
  568.2 0.0 reduce-scatter.2.cloned.1.call-update
  568.2 48.7 %reduce-scatter.2.cloned.1.call-done = bf16[256,2048]{1,0:T(8,128)(2,1)} async-done(((bf16[1024,2048]{1,0:T(8,128)(2,1)}), bf16[256,2048]{1,0:T(8,128)(2,1)}) %reduce-scatter.2.cloned.1.call-update) | async-done | bytes 1048592 | tf_op jit(solution)/shard_map/reduce_scatter | solution.py:139
  (20 shorter events, 0.1 us)
Async XLA Ops:
  6.5 556.4 %copy-start = (bf16[512,2048]{1,0:T(8,128)(2,1)S(1)}, bf16[512,2048]{1,0:T(8,128)(2,1)}, u32[]{:S(2)}) copy-start(bf16[512,2048]{1,0:T(8,128)(2,1)} %param.17) | copy-start | bytes 6291460
  8.6 20.6 %all-to-all-start = ((s32[64,1,2]{2,1,0:T(1,128)}), s32[64,1,2]{2,1,0:T(1,128)S(1)}, u32[]{:S(2)}, u32[]{:S(2)}) async-start(s32[64,1,2]{2,1,0:T(1,128)} %bitcast.9), calls=%async_computation | async-start | bytes 65536 | tf_op jit(solution)/shard_map/all_to_all | solution.py:127
  38.9 492.5 %all-to-all-start.1 = ((bf16[64,2,2,64,512]{4,3,2,1,0:T(8,128)(2,1)}), bf16[64,2,2,64,512]{4,3,2,1,0:T(8,128)(2,1)}, u32[]{:S(2)}, u32[]{:S(2)}) async-start(bf16[64,2,2,64,512]{4,3,2,1,0:T(8,128)(2,1)} %bitcast.88), calls=%async_computation.1 | async-start | bytes 33554432 | tf_op jit(solution)/shard_map/all_to_all | solution.py:128
  45.5 571.4 %reduce-scatter.2.cloned.1.call-start = ((), (), s32[]{:S(2)}) async-start(), calls=%async_computation.3 | async-start | bytes 5242880 | tf_op jit(solution)/shard_map/reduce_scatter | solution.py:139
  52.1 4.6 copy-start.6
  52.1 378.9 %collective-permute-start = (bf16[2,1024,512]{1,2,0:T(8,128)(2,1)}, bf16[2,1024,512]{1,2,0:T(8,128)(2,1)}, u32[]{:S(2)}, u32[]{:S(2)}) collective-permute-start(bf16[2,1024,512]{1,2,0:T(8,128)(2,1)} %pad_maximum_fusion.1), channel_id=1, source_target_pairs={{0,4},{4,8},{8,12},{12,16},{16,20},{20,24},{24,28},{28,32},{32,36}... | collective-permute-start | bytes 6291464 | tf_op jit(solution)/shard_map/ppermute | solution.py:21
  57.4 375.3 %copy-start.1 = (bf16[1024,512]{0,1:T(8,128)(2,1)S(1)}, bf16[1024,512]{0,1:T(8,128)(2,1)}, u32[]{:S(2)}) copy-start(bf16[1024,512]{0,1:T(8,128)(2,1)} %copy.74) | copy-start | bytes 3145732
  544.6 4.0 copy-start.2
  561.6 1.6 copy-start.3
  561.7 1.6 copy-start.4
  561.7 1.6 copy-start.5
Sparse Core Ops, SparseCore 0:
  568.4 48.5 reduce-scatter.1
where the time goes:
time: 628 us; the launch traced here: 624 us
  waiting for transfers between devices  428 us (68%)
  local copies, waits for them, and re-layouts  100 us (16%)
  matrix products  46.5 us (7%)
  starting transfers between devices  21 us (3%)
  between operations  13.5 us (2%)
  other arithmetic  13.1 us (2%)
    ppermute x1, waiting for transfers between devices, passed_along(): lax.ppermute(value, axis, [(source, source + steps) for source in range(l...  374 us
    reduce_scatter x1, waiting for transfers between devices, on_device(): lax.psum_scatter(jnp.dot(attended, out_weight, preferred_element_type=jnp...  48.7 us
    dynamic_update_slice x4, local copies, waits for them, and re-layouts, window_attention(): lax.map(per_tile, jnp.arange(tok_rows // tile_rows, dtype=jnp.int32))  41.4 us
    sub x2, matrix products, masked_softmax(): weights = jnp.where(allowed, jnp.exp(scores - row_max), 0.0)  22.9 us
    dot_general x2, matrix products, per_tile(): jnp.einsum('hqk,khd->qhd', attend_weights, value_tile, preferred_element_...  12.7 us
  transfers between devices with their start and end apart: 4, of which 3 were waited for; matrix products, arithmetic and copies ran while one was open for 18% of the time, Pallas kernels for 0%

commit v1 on v0

--- a/solution.py
+++ b/solution.py
@@ -95,23 +95,17 @@
 def on_device(queries, keys, values, memory_keys, memory_values, block_ids, gate_bias, out_weight):
     tok_rows, features = queries.shape
     owners = lax.axis_size("seq")
-    first_row = lax.axis_index("seq") * tok_rows
-    edge_rows = jnp.stack((keys, values))
-    before = passed_along(edge_rows, "seq", 1)
-    local_part = window_attention(
-        queries, jnp.concatenate([before[0], keys]), jnp.concatenate([before[1], values]), first_row
-    )
+    groups = lax.axis_size("head")
+    seq_index = lax.axis_index("seq")
+    first_row = seq_index * tok_rows
+    full_weight = lax.all_gather(out_weight, "head", axis=0, tiled=True)
     request_count = block_ids.shape[0] * block_ids.shape[1]
     wanted = block_ids.reshape(request_count)
     mem_dev = memory_keys.shape[0] // MROWS
+    last_block = owners * mem_dev - 1
     owner_index = wanted // mem_dev
     offset = wanted % mem_dev
-    per_owner = (request_count + owners) // (owners + 1)
-    positions = jnp.arange(request_count, dtype=jnp.int32)
-    earlier = (positions[None, :] < positions[:, None]) & (
-        owner_index[None, :] == owner_index[:, None]
-    )
-    rank_index = jnp.sum(earlier.astype(jnp.int32), axis=1)
+    is_last = wanted == last_block
     memory_store = jnp.stack(
         (
             memory_keys.reshape(mem_dev, MROWS, features),
@@ -119,16 +113,22 @@
         ),
         axis=1,
     )
-    slot_width = 2 * per_owner
-    slot_index = owner_index * slot_width + rank_index
-    slot_table = build_table(
-        slot_index, offset, jnp.ones((request_count,), dtype=bool), owners * slot_width
-    ).reshape(owners, slot_width)
+    slot_table = build_table(owner_index, offset, jnp.logical_not(is_last), owners).reshape(owners, 1)
     asked_for = lax.all_to_all(slot_table, "seq", split_axis=0, concat_axis=0, tiled=True)
     returned = lax.all_to_all(
-        memory_store[jnp.maximum(asked_for, 0)], "seq", split_axis=0, concat_axis=0, tiled=True
+        memory_store[jnp.maximum(asked_for[:, 0], 0)], "seq", split_axis=0, concat_axis=0, tiled=True
     )
-    fetched = returned.reshape(owners * slot_width, 2, MROWS, features)[slot_index]
+    shared = lax.psum(
+        jnp.where(seq_index == owners - 1, memory_store[mem_dev - 1], jnp.zeros_like(memory_store[0])),
+        "seq",
+    )
+    edge_rows = jnp.stack((keys, values))
+    before = passed_along(edge_rows, "seq", 1)
+    local_part = window_attention(
+        queries, jnp.concatenate([before[0], keys]), jnp.concatenate([before[1], values]), first_row
+    )
+    pool = jnp.concatenate([returned, shared[None]])
+    fetched = pool[jnp.where(is_last, owners, owner_index)]
     remote = memory_attention(queries, fetched)
     mixing = jax.nn.sigmoid(gate_bias)[None, :, None]
     attended = (
@@ -136,12 +136,17 @@
         .reshape(tok_rows, features)
         .astype(jnp.bfloat16)
     )
-    return lax.psum_scatter(
-        jnp.dot(attended, out_weight, preferred_element_type=jnp.float32).astype(jnp.bfloat16),
-        "head",
-        scatter_dimension=0,
-        tiled=True,
+    out_rows = tok_rows // groups
+    gathered = lax.all_to_all(
+        attended.reshape(groups, out_rows, features), "head", split_axis=0, concat_axis=0, tiled=True
     )
+    partials = jnp.einsum(
+        "gqf,gfn->gqn",
+        gathered,
+        full_weight.reshape(groups, features, full_weight.shape[1]),
+        preferred_element_type=jnp.float32,
+    ).astype(jnp.bfloat16)
+    return jnp.sum(partials.astype(jnp.float32), axis=0).astype(jnp.bfloat16)
 
 
 def solution(mesh):

time: 628 us -> 387 us (0.62)
  waiting for transfers between devices: 428 us -> 217 us
  local copies, waits for them, and re-layouts: 100 us -> 55.7 us
  other arithmetic: 13.1 us -> 23.2 us
    ppermute x1, waiting for transfers between devices: 374 us -> 197 us  [passed_along(): lax.ppermute(value, axis, [(source, source + steps) for source in range(l...]
    reduce_scatter x1 -> x0, waiting for transfers between devices: 48.7 us -> none  [on_device(): lax.psum_scatter(jnp.dot(attended, out_weight, preferred_element_type=jnp...]
    dynamic_update_slice x4, local copies, waits for them, and re-layouts: 41.4 us -> 5.39 us  [window_attention(): lax.map(per_tile, jnp.arange(tok_rows // tile_rows, dtype=jnp.int32))]
    all_to_all x1 -> x2, waiting for transfers between devices: 0.01 us -> 12.5 us  [the longest x1 12.5 us: on_device(): lax.all_to_all(attended.reshape(groups, out_rows, features), 'head', spli...]
    concatenate x0 -> x1, other arithmetic: none -> 7.46 us  [on_device(): pool = jnp.concatenate([returned, shared[None]])]
    reshape x0 -> x2, local copies, waits for them, and re-layouts: none -> 6.3 us  [the longest x1 3.23 us: memory_attention(): return remote.reshape(tok_rows, heads_here, HDIM)]
  transfers between devices with their start and end apart: 4 -> 6, of which waited for: 3 -> 3; matrix products, arithmetic and copies ran while one was open for 18% -> 29% of each run, Pallas kernels for 0% -> 0%
where the time goes in v1:
time: 387 us; the launch traced here: 386 us
  waiting for transfers between devices  217 us (56%)
  local copies, waits for them, and re-layouts  55.7 us (14%)
  matrix products  48.3 us (12%)
  starting transfers between devices  25.3 us (7%)
  other arithmetic  23.2 us (6%)
  between operations  15.1 us (4%)
    ppermute x1, waiting for transfers between devices, passed_along(): lax.ppermute(value, axis, [(source, source + steps) for source in range(l...  197 us
    sub x2, matrix products, masked_softmax(): weights = jnp.where(allowed, jnp.exp(scores - row_max), 0.0)  23.2 us
    dot_general x2, matrix products, per_tile(): jnp.einsum('hqk,khd->qhd', attend_weights, value_tile, preferred_element_...  16.6 us
    all_to_all x1, waiting for transfers between devices, on_device(): lax.all_to_all(attended.reshape(groups, out_rows, features), 'head', spli...  12.5 us
    all_to_all x1, starting transfers between devices, on_device(): lax.all_to_all(slot_table, 'seq', split_axis=0, concat_axis=0, tiled=True)  12 us
  transfers between devices with their start and end apart: 6, of which 3 were waited for; matrix products, arithmetic and copies ran while one was open for 29% of the time, Pallas kernels for 0%

profile of v1, /device:TPU:2, one launch (start us, length us, event | category | flops | bytes accessed | tf_op | source)
XLA Modules:
  0.0 386.3 jit_solution(3534146146987731793)
XLA Ops:
  7.4 0.8 copy.81
  8.1 0.1 reshape.331
  8.2 0.1 select_reduce_fusion.1
  8.3 0.7 copy.82
  9.1 12.0 %all-to-all-start = ((s32[64,1,1]{2,1,0:T(1,128)}), s32[64,1,1]{2,1,0:T(1,128)S(1)}, u32[]{:S(2)}, u32[]{:S(2)}) async-start(s32[64,1,1]{2,1,0:T(1,128)} %copy.82), calls=%async_computation | async-start | bytes 65536 | tf_op jit(solution)/shard_map/all_to_all | solution.py:117
  21.1 1.7 pad_maximum_fusion.1
  22.8 6.8 %all-to-all-done = s32[64,1,1]{2,1,0:T(1,128)S(1)} async-done(((s32[64,1,1]{2,1,0:T(1,128)}), s32[64,1,1]{2,1,0:T(1,128)S(1)}, u32[]{:S(2)}, u32[]{:S(2)}) %all-to-all-start) | async-done | bytes 288 | tf_op jit(solution)/shard_map/all_to_all | solution.py:117
  29.6 1.2 maximum_reduce_fusion
  30.9 5.5 %gather_fusion = bf16[64,2,64,512]{3,2,1,0:T(8,128)(2,1)} fusion(bf16[16,2,64,512]{3,2,1,0:T(8,128)(2,1)S(1)} %pad_maximum_fusion.1, s32[1024]{0:T(1024)S(1)} %pad_clamp_fusion.1), kind=kCustom, calls=%fused_computation | custom fusion | bytes 16777472 | tf_op jit(solution)/shard_map/gather | solution.py:119
  36.4 6.7 %all-to-all-start.1 = ((bf16[64,2,64,512]{3,2,1,0:T(8,128)(2,1)}), bf16[64,2,64,512]{3,2,1,0:T(8,128)(2,1)}, u32[]{:S(2)}, u32[]{:S(2)}) async-start(bf16[64,2,64,512]{3,2,1,0:T(8,128)(2,1)} %gather_fusion), calls=%async_computation.1 | async-start | bytes 16777216 | tf_op jit(solution)/shard_map/all_to_all | solution.py:118
  43.2 0.0 copy-start.8
  43.2 0.0 all-reduce.2.cloned.1.call-start
  43.2 0.5 copy.90
  43.8 0.6 copy-done.8
  44.4 0.5 copy.89
  44.9 0.0 copy-start.5
  44.9 1.5 pad_maximum_fusion.2
  46.4 0.2 copy-done.1
  46.6 2.0 collective-permute-start
  48.6 1.6 fusion.30
  50.2 0.0 all-reduce.2.cloned.1.call-update
  50.3 0.0 copy-start.11
  50.3 0.0 all-gather.2.cloned.1.call-start
  50.3 0.5 all-gather.2.cloned.1.call-update
  50.9 0.1 reshape.332
  51.0 1.3 reshape.333
  52.3 0.7 broadcast_bitcast_fusion
  53.0 197.4 %collective-permute-done = bf16[2,1024,512]{1,2,0:T(8,128)(2,1)} collective-permute-done((bf16[2,1024,512]{1,2,0:T(8,128)(2,1)}, bf16[2,1024,512]{1,2,0:T(8,128)(2,1)}, u32[]{:S(2)}, u32[]{:S(2)}) %collective-permute-start) | collective-permute-done | bytes 2097184 | tf_op jit(solution)/shard_map/ppermute | solution.py:21
  250.4 1.7 slice_bitcast_fusion
  252.1 1.6 pad_maximum_fusion.3
  253.8 60.1 %while.13 = (s32[]{:T(128)}, f32[2,512,4,128]{3,2,1,0:T(4,128)}, s32[2]{0:T(128)S(1)}, bf16[2048,512]{0,1:T(8,128)(2,1)S(1)}, s32[]{:T(128)}, /*index=5*/bf16[10...) while((s32[]{:T(128)}, f32[2,512,4,128]{3,2,1,0:T(4,128)}, ...), condition=%wide.region_7.8_spmd, body=%wide.region_4.7_spmd.sunk | while | flops 2444237824 | bytes 44080392 | solution.py:64
  253.8 0.6 dynamic_slice.37
  255.0 3.3 constant_dynamic-slice_fusion.5
  258.3 0.8 and_and_fusion.2
  259.1 1.1 constant_dynamic-slice_fusion.6
  260.2 1.0 copy.112
  261.2 11.6 %fusion.57 = (f32[4,512]{1,0:T(4,128)S(1)}, f32[4,512,1536]{2,1,0:T(8,128)}) fusion(pred[512,1536]{1,0:T(8,128)(4,1)S(1)} %and_and_fusion.2, bf16[512,4,128]{0,2,1:T(8,128)(2,1)} %bitcast.71, bf16[1536,4,128]{0,2,1:T(8,128)(2,1)} %bitcast.70), kind=kOutput, calls=%fused_computation.78.clone.1 | convolution fusion | flops 1629488640 | bytes 15474688 | tf_op jit(solution)/shard_map/while/body/eval_jaxpr/sub | solution.py:26
  272.8 8.3 %fusion.58 = f32[1,512,4,128]{1,3,2,0:T(8,128)} fusion(bf16[1536,4,128]{0,2,1:T(8,128)(2,1)} %bitcast.69, f32[4,512,1536]{2,1,0:T(8,128)} %get-tuple-element.244, f32[4,512]{1,0:T(4,128)S(1)} %get-tuple-element.245), kind=kOutput, calls=%fused_computation.14.clone.1 | convolution fusion | flops 811597824 | bytes 15212544 | tf_op jit(solution)/shard_map/while/body/eval_jaxpr/hqk,khd->qhd/dot_general | solution.py:60
  281.1 1.6 copy.113
  282.7 1.1 constant_dynamic-update-slice_fusion.2
  283.8 0.6 dynamic_slice.37
  285.1 3.3 constant_dynamic-slice_fusion.5
  288.4 0.8 and_and_fusion.2
  289.2 1.1 constant_dynamic-slice_fusion.6
  290.3 1.0 copy.112
  291.3 11.6 %fusion.57 = (f32[4,512]{1,0:T(4,128)S(1)}, f32[4,512,1536]{2,1,0:T(8,128)}) fusion(pred[512,1536]{1,0:T(8,128)(4,1)S(1)} %and_and_fusion.2, bf16[512,4,128]{0,2,1:T(8,128)(2,1)} %bitcast.71, bf16[1536,4,128]{0,2,1:T(8,128)(2,1)} %bitcast.70), kind=kOutput, calls=%fused_computation.78.clone.1 | convolution fusion | flops 1629488640 | bytes 15474688 | tf_op jit(solution)/shard_map/while/body/eval_jaxpr/sub | solution.py:26
  302.9 8.3 %fusion.58 = f32[1,512,4,128]{1,3,2,0:T(8,128)} fusion(bf16[1536,4,128]{0,2,1:T(8,128)(2,1)} %bitcast.69, f32[4,512,1536]{2,1,0:T(8,128)} %get-tuple-element.244, f32[4,512]{1,0:T(4,128)S(1)} %get-tuple-element.245), kind=kOutput, calls=%fused_computation.14.clone.1 | convolution fusion | flops 811597824 | bytes 15212544 | tf_op jit(solution)/shard_map/while/body/eval_jaxpr/hqk,khd->qhd/dot_general | solution.py:60
  311.2 1.6 copy.113
  312.8 1.1 constant_dynamic-update-slice_fusion.2
  313.9 3.1 reshape.335
  317.0 7.5 %pad_maximum_fusion = bf16[65,2,64,512]{3,2,1,0:T(8,128)(2,1)} fusion(bf16[1,2,64,512]{3,2,1,0:T(8,128)(2,1)} %all-reduce.2.cloned.1.call-done, bf16[64,2,64,512]{3,2,1,0:T(8,128)(2,1)} %all-to-all-done.1), kind=kLoop, calls=%fused_computation.26 | loop fusion | flops 4259840 | bytes 17039360 | tf_op jit(solution)/shard_map/concatenate | solution.py:130
  324.5 6.2 %gather_fusion.1 = bf16[32,2,64,512]{3,2,1,0:T(8,128)(2,1)} fusion(bf16[65,2,64,512]{3,2,1,0:T(8,128)(2,1)} %pad_maximum_fusion, s32[1024]{0:T(1024)S(1)} %pad_clamp_fusion), kind=kCustom, calls=%fused_computation.1 | custom fusion | bytes 8388736 | tf_op jit(solution)/shard_map/gather | solution.py:131
  330.7 4.7 %fusion.36 = (bf16[32,1,64,512]{3,2,1,0:T(8,128)(2,1)}, bf16[32,1,64,512]{3,2,1,0:T(8,128)(2,1)}) fusion(bf16[32,2,64,512]{3,2,1,0:T(8,128)(2,1)} %gather_fusion.1), kind=kLoop, calls=%fused_computation.79 | loop fusion | bytes 8388608 | tf_op jit(solution)/shard_map/slice | solution.py:76
  335.3 2.5 reshape_squeeze.7
  337.9 4.1 %reshape_squeeze.6 = bf16[8,256,4,128]{3,2,1,0:T(4,128)(2,1)} reshape(bf16[32,1,64,512]{3,2,1,0:T(8,128)(2,1)} %get-tuple-element.179) | data formatting | bytes 4194304 | tf_op jit(solution)/shard_map/reshape;squeeze | solution.py:76
  342.0 0.7 fusion.22
  342.7 3.1 fusion.37
  345.8 0.9 fusion.25
  346.7 1.8 copy.88
  348.5 3.2 reshape.334
  351.8 3.1 add_convert_fusion
  354.9 4.5 %all-to-all-start.2 = ((bf16[4,256,512]{2,1,0:T(8,128)(2,1)}), bf16[4,256,512]{2,1,0:T(8,128)(2,1)S(1)}, u32[]{:S(2)}, u32[]{:S(2)}) async-start(bf16[4,256,512]{2,1,0:T(8,128)(2,1)} %add_convert_fusion), calls=%async_computation.2 | async-start | bytes 2097152 | tf_op jit(solution)/shard_map/all_to_all | solution.py:140
  359.4 12.5 %all-to-all-done.2 = bf16[4,256,512]{2,1,0:T(8,128)(2,1)S(1)} async-done(((bf16[4,256,512]{2,1,0:T(8,128)(2,1)}), bf16[4,256,512]{2,1,0:T(8,128)(2,1)S(1)}, u32[]{:S(2)}, u32[]{:S(2)}) %all-to-all-start.2) | async-done | bytes 1048608 | tf_op jit(solution)/shard_map/all_to_all | solution.py:140
  371.9 6.9 %convert_reduce_fusion = bf16[256,2048]{1,0:T(8,128)(2,1)} fusion(bf16[4,256,512]{2,1,0:T(8,128)(2,1)S(1)} %all-to-all-done.2, bf16[4,512,2048]{2,1,0:T(8,128)(2,1)} %bitcast.78), kind=kOutput, calls=%fused_computation.31 | convolution fusion | flops 2151153664 | bytes 10485760 | tf_op jit(solution)/shard_map/gqf,gfn->gqn/dot_general | solution.py:143
  (37 shorter events, 0.2 us)
Async XLA Ops:
  9.1 20.6 %all-to-all-start = ((s32[64,1,1]{2,1,0:T(1,128)}), s32[64,1,1]{2,1,0:T(1,128)S(1)}, u32[]{:S(2)}, u32[]{:S(2)}) async-start(s32[64,1,1]{2,1,0:T(1,128)} %copy.82), calls=%async_computation | async-start | bytes 65536 | tf_op jit(solution)/shard_map/all_to_all | solution.py:117
  36.4 6.8 %copy-start.7 = (bf16[1024,512]{1,0:T(8,128)(2,1)S(1)}, bf16[1024,512]{1,0:T(8,128)(2,1)}, u32[]{:S(2)}) copy-start(bf16[1024,512]{1,0:T(8,128)(2,1)} %param.12) | copy-start | bytes 3145732
  36.4 280.6 %all-to-all-start.1 = ((bf16[64,2,64,512]{3,2,1,0:T(8,128)(2,1)}), bf16[64,2,64,512]{3,2,1,0:T(8,128)(2,1)}, u32[]{:S(2)}, u32[]{:S(2)}) async-start(bf16[64,2,64,512]{3,2,1,0:T(8,128)(2,1)} %gather_fusion), calls=%async_computation.1 | async-start | bytes 16777216 | tf_op jit(solution)/shard_map/all_to_all | solution.py:118
  43.2 1.2 copy-start.8
  43.2 273.8 %all-reduce.2.cloned.1.call-start = ((), (), s32[]{:S(2)}) async-start(), calls=%async_computation.3 | async-start | bytes 262144 | tf_op jit(solution)/shard_map/psum | solution.py:121
  44.9 1.7 copy-start.1
  44.9 3.7 copy-start.5
  46.6 203.8 %collective-permute-start = (bf16[2,1024,512]{1,2,0:T(8,128)(2,1)}, bf16[2,1024,512]{1,2,0:T(8,128)(2,1)}, u32[]{:S(2)}, u32[]{:S(2)}) collective-permute-start(bf16[2,1024,512]{1,2,0:T(8,128)(2,1)} %pad_maximum_fusion.2), channel_id=1, source_target_pairs={{0,4},{4,8},{8,12},{12,16},{16,20},{20,24},{24,28},{28,32},{32,36}... | collective-permute-start | bytes 6291464 | tf_op jit(solution)/shard_map/ppermute | solution.py:21
  48.6 2.3 copy-start
  50.3 2.0 copy-start.11
  50.3 309.1 %all-gather.2.cloned.1.call-start = ((), (), s32[]{:S(2)}) async-start(), calls=%async_computation.4 | async-start | bytes 10485760 | tf_op jit(solution)/shard_map/all_gather | solution.py:101
  53.0 199.1 %copy-start.2 = (bf16[1024,512]{0,1:T(8,128)(2,1)S(1)}, bf16[1024,512]{0,1:T(8,128)(2,1)}, u32[]{:S(2)}) copy-start(bf16[1024,512]{0,1:T(8,128)(2,1)} %copy-done.1) | copy-start | bytes 3145732
  337.9 4.1 %copy-start.4 = (bf16[8,128,4,128]{3,2,1,0:T(4,128)(2,1)S(1)}, bf16[8,128,4,128]{3,2,1,0:T(4,128)(2,1)}, u32[]{:S(2)}) copy-start(bf16[8,128,4,128]{3,2,1,0:T(4,128)(2,1)} %reshape.333) | copy-start | bytes 3145732
  342.7 3.1 copy-start.6
  348.5 3.2 copy-start.3
  348.5 3.2 copy-start.9
  348.5 3.2 copy-start.10
  354.9 17.0 %all-to-all-start.2 = ((bf16[4,256,512]{2,1,0:T(8,128)(2,1)}), bf16[4,256,512]{2,1,0:T(8,128)(2,1)S(1)}, u32[]{:S(2)}, u32[]{:S(2)}) async-start(bf16[4,256,512]{2,1,0:T(8,128)(2,1)} %add_convert_fusion), calls=%async_computation.2 | async-start | bytes 2097152 | tf_op jit(solution)/shard_map/all_to_all | solution.py:140
Sparse Core Ops, SparseCore 0:
  50.4 197.7 all-reduce.1
Sparse Core Ops, SparseCore 1:
  52.6 86.9 all-gather.1

commit v2 on v1

--- a/solution.py
+++ b/solution.py
@@ -114,21 +114,20 @@
         axis=1,
     )
     slot_table = build_table(owner_index, offset, jnp.logical_not(is_last), owners).reshape(owners, 1)
+    edge_rows = jnp.stack((keys, values))
+    before = passed_along(edge_rows, "seq", 1)
     asked_for = lax.all_to_all(slot_table, "seq", split_axis=0, concat_axis=0, tiled=True)
-    returned = lax.all_to_all(
-        memory_store[jnp.maximum(asked_for[:, 0], 0)], "seq", split_axis=0, concat_axis=0, tiled=True
-    )
+    outgoing = memory_store[jnp.maximum(asked_for[:, 0], 0)]
+    before, outgoing = lax.optimization_barrier((before, outgoing))
+    returned = lax.all_to_all(outgoing, "seq", split_axis=0, concat_axis=0, tiled=True)
     shared = lax.psum(
         jnp.where(seq_index == owners - 1, memory_store[mem_dev - 1], jnp.zeros_like(memory_store[0])),
         "seq",
     )
-    edge_rows = jnp.stack((keys, values))
-    before = passed_along(edge_rows, "seq", 1)
     local_part = window_attention(
         queries, jnp.concatenate([before[0], keys]), jnp.concatenate([before[1], values]), first_row
     )
-    pool = jnp.concatenate([returned, shared[None]])
-    fetched = pool[jnp.where(is_last, owners, owner_index)]
+    fetched = jnp.where(is_last[:, None, None, None], shared[None], returned[owner_index])
     remote = memory_attention(queries, fetched)
     mixing = jax.nn.sigmoid(gate_bias)[None, :, None]
     attended = (

time: 387 us -> 326 us (0.84)
  waiting for transfers between devices: 217 us -> 163 us
  other arithmetic: 23.2 us -> 18.4 us
    ppermute x1, waiting for transfers between devices: 197 us -> 0.01 us  [passed_along(): lax.ppermute(value, axis, [(source, source + steps) for source in range(l...]
    all_to_all x1, waiting for transfers between devices: 0.01 us -> 114 us  [on_device(): lax.all_to_all(outgoing, 'seq', split_axis=0, concat_axis=0, tiled=True)]
    psum x1, waiting for transfers between devices: 0.01 us -> 13.7 us  [on_device(): lax.psum(jnp.where(seq_index == owners - 1, memory_store[mem_dev - 1], jn...]
    all_to_all x1, waiting for transfers between devices: 6.8 us -> 18.3 us  [on_device(): lax.all_to_all(slot_table, 'seq', split_axis=0, concat_axis=0, tiled=True)]
    concatenate x1 -> x0, other arithmetic: 7.46 us -> none  [on_device(): pool = jnp.concatenate([returned, shared[None]])]
  transfers between devices with their start and end apart: 6 -> 6, of which waited for: 3 -> 4; matrix products, arithmetic and copies ran while one was open for 29% -> 34% of each run, Pallas kernels for 0% -> 0%
where the time goes in v2:
time: 326 us; the launch traced here: 325 us
  waiting for transfers between devices  163 us (50%)
  local copies, waits for them, and re-layouts  52.8 us (16%)
  matrix products  48.6 us (15%)
  starting transfers between devices  26.2 us (8%)
  other arithmetic  18.4 us (6%)
  between operations  15.1 us (5%)
    all_to_all x1, waiting for transfers between devices, on_device(): lax.all_to_all(outgoing, 'seq', split_axis=0, concat_axis=0, tiled=True)  114 us
    sub x2, matrix products, masked_softmax(): weights = jnp.where(allowed, jnp.exp(scores - row_max), 0.0)  23.2 us
    all_to_all x1, waiting for transfers between devices, on_device(): lax.all_to_all(slot_table, 'seq', split_axis=0, concat_axis=0, tiled=True)  18.3 us
    dot_general x2, matrix products, per_tile(): jnp.einsum('hqk,khd->qhd', attend_weights, value_tile, preferred_element_...  16.9 us
    all_to_all x1, waiting for transfers between devices, on_device(): lax.all_to_all(attended.reshape(groups, out_rows, features), 'head', spli...  16 us
    psum x1, waiting for transfers between devices, on_device(): lax.psum(jnp.where(seq_index == owners - 1, memory_store[mem_dev - 1], jn...  13.7 us
    all_to_all x1, starting transfers between devices, on_device(): lax.all_to_all(slot_table, 'seq', split_axis=0, concat_axis=0, tiled=True)  12.7 us
    dot_general x1, matrix products, on_device(): jnp.einsum('gqf,gfn->gqn', gathered, full_weight.reshape(groups, features...  6.92 us
  transfers between devices with their start and end apart: 6, of which 4 were waited for; matrix products, arithmetic and copies ran while one was open for 34% of the time, Pallas kernels for 0%

profile of v2, /device:TPU:2, one launch (start us, length us, event | category | flops | bytes accessed | tf_op | source)
XLA Modules:
  0.0 325.1 jit_solution(10096298842922641298)
XLA Ops:
  7.4 1.6 copy.88
  9.0 0.5 copy.89
  9.5 0.0 copy-start.1
  9.5 0.0 copy-start.10
  9.5 1.6 pad_maximum_fusion.1
  11.2 1.9 collective-permute-start
  13.1 0.1 copy.85
  13.2 0.1 reshape.325
  13.3 0.1 select_reduce_fusion.1
  13.4 0.7 copy.90
  14.1 12.7 %all-to-all-start = ((s32[64,1,1]{2,1,0:T(1,128)}), s32[64,1,1]{2,1,0:T(1,128)S(1)}, u32[]{:S(2)}, u32[]{:S(2)}) async-start(s32[64,1,1]{2,1,0:T(1,128)} %copy.90), calls=%async_computation | async-start | bytes 65536 | tf_op jit(solution)/shard_map/all_to_all | solution.py:119
  26.8 1.7 pad_maximum_fusion
  28.6 18.3 %all-to-all-done = s32[64,1,1]{2,1,0:T(1,128)S(1)} async-done(((s32[64,1,1]{2,1,0:T(1,128)}), s32[64,1,1]{2,1,0:T(1,128)S(1)}, u32[]{:S(2)}, u32[]{:S(2)}) %all-to-all-start) | async-done | bytes 288 | tf_op jit(solution)/shard_map/all_to_all | solution.py:119
  46.9 1.2 maximum_reduce_fusion
  48.1 5.5 %gather_fusion = bf16[64,2,64,512]{3,2,1,0:T(8,128)(2,1)} fusion(bf16[16,2,64,512]{3,2,1,0:T(8,128)(2,1)S(1)} %pad_maximum_fusion, s32[1024]{0:T(1024)S(1)} %pad_clamp_fusion.1), kind=kCustom, calls=%fused_computation | custom fusion | bytes 16777472 | tf_op jit(solution)/shard_map/gather | solution.py:120
  53.6 6.8 %all-to-all-start.1 = ((bf16[64,2,64,512]{3,2,1,0:T(8,128)(2,1)}), bf16[64,2,64,512]{3,2,1,0:T(8,128)(2,1)}, u32[]{:S(2)}, u32[]{:S(2)}) async-start(bf16[64,2,64,512]{3,2,1,0:T(8,128)(2,1)} %gather_fusion), calls=%async_computation.1 | async-start | bytes 16777216 | tf_op jit(solution)/shard_map/all_to_all | solution.py:122
  60.4 0.0 all-reduce.2.cloned.1.call-start
  60.5 0.0 copy-start
  60.5 1.6 select_bitcast_fusion
  62.1 0.0 all-reduce.2.cloned.1.call-update
  62.2 0.2 all-gather.2.cloned.1.call-start
  62.4 0.3 all-gather.2.cloned.1.call-update
  62.7 0.1 reshape.326
  62.8 1.1 reshape.327
  64.0 0.7 broadcast_bitcast_fusion
  64.6 1.8 slice_bitcast_fusion
  66.4 0.1 copy-done.2
  66.5 1.7 pad_maximum_fusion.2
  68.1 60.6 %while.13 = (s32[]{:T(128)}, f32[2,512,4,128]{3,2,1,0:T(4,128)}, s32[2]{0:T(128)S(1)}, bf16[2048,512]{0,1:T(8,128)(2,1)S(1)}, s32[]{:T(128)}, /*index=5*/bf16[10...) while((s32[]{:T(128)}, f32[2,512,4,128]{3,2,1,0:T(4,128)}, ...), condition=%wide.region_7.8_spmd, body=%wide.region_4.7_spmd.sunk | while | flops 2444237824 | bytes 44080892 | solution.py:64
  68.1 0.6 dynamic_slice.37
  69.4 0.8 and_and_fusion.2
  70.2 3.3 %constant_dynamic-slice_fusion.5 = (bf16[1536,512]{0,1:T(8,128)(2,1)}, bf16[1536,512]{0,1:T(8,128)(2,1)}) fusion(bf16[2048,512]{0,1:T(8,128)(2,1)} %get-tuple-element.284, s32[]{:T(128)S(6)} %select_n.127, bf16[2048,512]{0,1:T(8,128)(2,1)S(1)} %get-tuple-element.281), kind=kLoop, calls=%fused_computation.20.clone.1 | loop fusion | bytes 6291460 | tf_op jit(solution)/shard_map/while/body/eval_jaxpr/dynamic_slice | solution.py:42
  73.6 1.1 constant_dynamic-slice_fusion.6
  74.6 1.0 copy.118
  75.6 11.6 %fusion.57 = (f32[4,512]{1,0:T(4,128)S(1)}, f32[4,512,1536]{2,1,0:T(8,128)}) fusion(pred[512,1536]{1,0:T(8,128)(4,1)S(1)} %and_and_fusion.2, bf16[512,4,128]{0,2,1:T(8,128)(2,1)} %bitcast.77, bf16[1536,4,128]{0,2,1:T(8,128)(2,1)} %bitcast.76), kind=kOutput, calls=%fused_computation.78.clone.1 | convolution fusion | flops 1629488640 | bytes 15474688 | tf_op jit(solution)/shard_map/while/body/eval_jaxpr/sub | solution.py:26
  87.2 8.4 %fusion.58 = f32[1,512,4,128]{1,3,2,0:T(8,128)} fusion(bf16[1536,4,128]{0,2,1:T(8,128)(2,1)} %bitcast.75, f32[4,512,1536]{2,1,0:T(8,128)} %get-tuple-element.250, f32[4,512]{1,0:T(4,128)S(1)} %get-tuple-element.251), kind=kOutput, calls=%fused_computation.14.clone.1 | convolution fusion | flops 811597824 | bytes 15212544 | tf_op jit(solution)/shard_map/while/body/eval_jaxpr/hqk,khd->qhd/dot_general | solution.py:60
  95.7 1.6 copy.119
  97.3 1.1 constant_dynamic-update-slice_fusion.2
  98.4 0.6 dynamic_slice.37
  99.7 0.8 and_and_fusion.2
  100.5 3.3 %constant_dynamic-slice_fusion.5 = (bf16[1536,512]{0,1:T(8,128)(2,1)}, bf16[1536,512]{0,1:T(8,128)(2,1)}) fusion(bf16[2048,512]{0,1:T(8,128)(2,1)} %get-tuple-element.284, s32[]{:T(128)S(6)} %select_n.127, bf16[2048,512]{0,1:T(8,128)(2,1)S(1)} %get-tuple-element.281), kind=kLoop, calls=%fused_computation.20.clone.1 | loop fusion | bytes 6291460 | tf_op jit(solution)/shard_map/while/body/eval_jaxpr/dynamic_slice | solution.py:42
  103.8 1.1 constant_dynamic-slice_fusion.6
  104.9 1.0 copy.118
  105.9 11.6 %fusion.57 = (f32[4,512]{1,0:T(4,128)S(1)}, f32[4,512,1536]{2,1,0:T(8,128)}) fusion(pred[512,1536]{1,0:T(8,128)(4,1)S(1)} %and_and_fusion.2, bf16[512,4,128]{0,2,1:T(8,128)(2,1)} %bitcast.77, bf16[1536,4,128]{0,2,1:T(8,128)(2,1)} %bitcast.76), kind=kOutput, calls=%fused_computation.78.clone.1 | convolution fusion | flops 1629488640 | bytes 15474688 | tf_op jit(solution)/shard_map/while/body/eval_jaxpr/sub | solution.py:26
  117.5 8.5 %fusion.58 = f32[1,512,4,128]{1,3,2,0:T(8,128)} fusion(bf16[1536,4,128]{0,2,1:T(8,128)(2,1)} %bitcast.75, f32[4,512,1536]{2,1,0:T(8,128)} %get-tuple-element.250, f32[4,512]{1,0:T(4,128)S(1)} %get-tuple-element.251), kind=kOutput, calls=%fused_computation.14.clone.1 | convolution fusion | flops 811597824 | bytes 15212544 | tf_op jit(solution)/shard_map/while/body/eval_jaxpr/hqk,khd->qhd/dot_general | solution.py:60
  126.0 1.6 copy.119
  127.6 1.1 constant_dynamic-update-slice_fusion.2
  128.7 3.1 reshape.329
  131.8 114.3 %all-to-all-done.1 = bf16[64,2,64,512]{3,2,1,0:T(8,128)(2,1)} async-done(((bf16[64,2,64,512]{3,2,1,0:T(8,128)(2,1)}), bf16[64,2,64,512]{3,2,1,0:T(8,128)(2,1)}, u32[]{:S(2)}, u32[]{:S(2)}) %all-to-all-start.1) | async-done | bytes 8388640 | tf_op jit(solution)/shard_map/all_to_all | solution.py:122
  246.1 6.1 %gather_fusion.1 = bf16[32,2,64,512]{3,2,1,0:T(8,128)(2,1)} fusion(bf16[64,2,64,512]{3,2,1,0:T(8,128)(2,1)} %all-to-all-done.1, s32[1024]{0:T(1024)S(1)} %pad_clamp_fusion), kind=kCustom, calls=%fused_computation.1 | custom fusion | bytes 8388736 | tf_op jit(solution)/shard_map/gather | solution.py:130
  252.2 13.7 %all-reduce.2.cloned.1.call-done = bf16[2,64,512]{2,1,0:T(8,128)(2,1)} async-done(((bf16[2,64,512]{2,1,0:T(8,128)(2,1)}), bf16[2,64,512]{2,1,0:T(8,128)(2,1)}) %all-reduce.2.cloned.1.call-update) | async-done | bytes 131088 | tf_op jit(solution)/shard_map/psum | solution.py:123
  265.9 2.6 broadcast_select_fusion
  268.5 2.2 fusion.36
  270.7 2.5 reshape_squeeze.7
  273.2 4.0 %reshape_squeeze.6 = bf16[8,256,4,128]{3,2,1,0:T(4,128)(2,1)} reshape(bf16[32,1,64,512]{3,2,1,0:T(8,128)(2,1)} %get-tuple-element.183) | data formatting | bytes 4194304 | tf_op jit(solution)/shard_map/reshape;squeeze | solution.py:76
  277.3 0.7 fusion.22
  278.0 3.1 fusion.37
  281.1 0.9 fusion.25
  282.0 1.8 copy.96
  283.9 3.2 reshape.328
  287.1 3.1 add_convert_fusion
  290.2 4.5 %all-to-all-start.2 = ((bf16[4,256,512]{2,1,0:T(8,128)(2,1)}), bf16[4,256,512]{2,1,0:T(8,128)(2,1)S(1)}, u32[]{:S(2)}, u32[]{:S(2)}) async-start(bf16[4,256,512]{2,1,0:T(8,128)(2,1)} %add_convert_fusion), calls=%async_computation.2 | async-start | bytes 2097152 | tf_op jit(solution)/shard_map/all_to_all | solution.py:139
  294.7 16.0 %all-to-all-done.2 = bf16[4,256,512]{2,1,0:T(8,128)(2,1)S(1)} async-done(((bf16[4,256,512]{2,1,0:T(8,128)(2,1)}), bf16[4,256,512]{2,1,0:T(8,128)(2,1)S(1)}, u32[]{:S(2)}, u32[]{:S(2)}) %all-to-all-start.2) | async-done | bytes 1048608 | tf_op jit(solution)/shard_map/all_to_all | solution.py:139
  310.7 6.9 %convert_reduce_fusion = bf16[256,2048]{1,0:T(8,128)(2,1)} fusion(bf16[4,256,512]{2,1,0:T(8,128)(2,1)S(1)} %all-to-all-done.2, bf16[4,512,2048]{2,1,0:T(8,128)(2,1)} %bitcast.84), kind=kOutput, calls=%fused_computation.30 | convolution fusion | flops 2151153664 | bytes 10485760 | tf_op jit(solution)/shard_map/gqf,gfn->gqn/dot_general | solution.py:142
  (37 shorter events, 0.1 us)
Async XLA Ops:
  7.4 1.6 copy-start.7
  9.5 1.7 copy-start.1
  9.5 3.6 %copy-start.10 = (s32[8,4]{0,1:T(4,128)S(1)}, s32[8,4]{0,1:T(4,128)}, u32[]{:S(2)}) copy-start(s32[8,4]{0,1:T(4,128)} %param.15) | copy-start | bytes 388
  11.2 42.5 %collective-permute-start = (bf16[2,1024,512]{1,2,0:T(8,128)(2,1)}, bf16[2,1024,512]{1,2,0:T(8,128)(2,1)}, u32[]{:S(2)}, u32[]{:S(2)}) collective-permute-start(bf16[2,1024,512]{1,2,0:T(8,128)(2,1)} %pad_maximum_fusion.1), channel_id=1, source_target_pairs={{0,4},{4,8},{8,12},{12,16},{16,20},{20,24},{24,28},{28,32},{32,36}... | collective-permute-start | bytes 6291464 | tf_op jit(solution)/shard_map/ppermute | solution.py:21
  14.1 32.8 %all-to-all-start = ((s32[64,1,1]{2,1,0:T(1,128)}), s32[64,1,1]{2,1,0:T(1,128)S(1)}, u32[]{:S(2)}, u32[]{:S(2)}) async-start(s32[64,1,1]{2,1,0:T(1,128)} %copy.90), calls=%async_computation | async-start | bytes 65536 | tf_op jit(solution)/shard_map/all_to_all | solution.py:119
  53.6 6.9 %copy-start.5 = (bf16[1024,512]{1,0:T(8,128)(2,1)S(1)}, bf16[1024,512]{1,0:T(8,128)(2,1)}, u32[]{:S(2)}) copy-start(bf16[1024,512]{1,0:T(8,128)(2,1)} %param.14) | copy-start | bytes 3145732
  53.6 192.4 %all-to-all-start.1 = ((bf16[64,2,64,512]{3,2,1,0:T(8,128)(2,1)}), bf16[64,2,64,512]{3,2,1,0:T(8,128)(2,1)}, u32[]{:S(2)}, u32[]{:S(2)}) async-start(bf16[64,2,64,512]{3,2,1,0:T(8,128)(2,1)} %gather_fusion), calls=%async_computation.1 | async-start | bytes 16777216 | tf_op jit(solution)/shard_map/all_to_all | solution.py:122
  60.4 205.5 %all-reduce.2.cloned.1.call-start = ((), (), s32[]{:S(2)}) async-start(), calls=%async_computation.3 | async-start | bytes 262144 | tf_op jit(solution)/shard_map/psum | solution.py:123
  60.5 2.3 copy-start
  62.1 1.8 copy-start.11
  62.2 232.5 %all-gather.2.cloned.1.call-start = ((), (), s32[]{:S(2)}) async-start(), calls=%async_computation.4 | async-start | bytes 10485760 | tf_op jit(solution)/shard_map/all_gather | solution.py:101
  64.6 1.9 copy-start.2
  273.2 4.1 %copy-start.4 = (bf16[8,128,4,128]{3,2,1,0:T(4,128)(2,1)S(1)}, bf16[8,128,4,128]{3,2,1,0:T(4,128)(2,1)}, u32[]{:S(2)}) copy-start(bf16[8,128,4,128]{3,2,1,0:T(4,128)(2,1)} %reshape.327) | copy-start | bytes 3145732
  278.0 3.1 copy-start.6
  283.9 3.2 copy-start.3
  283.9 3.2 copy-start.8
  283.9 3.2 copy-start.9
  290.2 20.5 %all-to-all-start.2 = ((bf16[4,256,512]{2,1,0:T(8,128)(2,1)}), bf16[4,256,512]{2,1,0:T(8,128)(2,1)S(1)}, u32[]{:S(2)}, u32[]{:S(2)}) async-start(bf16[4,256,512]{2,1,0:T(8,128)(2,1)} %add_convert_fusion), calls=%async_computation.2 | async-start | bytes 2097152 | tf_op jit(solution)/shard_map/all_to_all | solution.py:139
Sparse Core Ops, SparseCore 0:
  64.7 201.1 all-reduce.1
Sparse Core Ops, SparseCore 1:
  64.4 86.7 all-gather.1

commit v3 on v2

--- a/solution.py
+++ b/solution.py
@@ -113,17 +113,18 @@
         ),
         axis=1,
     )
-    slot_table = build_table(owner_index, offset, jnp.logical_not(is_last), owners).reshape(owners, 1)
     edge_rows = jnp.stack((keys, values))
     before = passed_along(edge_rows, "seq", 1)
-    asked_for = lax.all_to_all(slot_table, "seq", split_axis=0, concat_axis=0, tiled=True)
-    outgoing = memory_store[jnp.maximum(asked_for[:, 0], 0)]
-    before, outgoing = lax.optimization_barrier((before, outgoing))
-    returned = lax.all_to_all(outgoing, "seq", split_axis=0, concat_axis=0, tiled=True)
     shared = lax.psum(
         jnp.where(seq_index == owners - 1, memory_store[mem_dev - 1], jnp.zeros_like(memory_store[0])),
         "seq",
     )
+    every_id = lax.all_gather(block_ids, "seq", axis=0, tiled=True).reshape(owners, request_count)
+    mine = (every_id // mem_dev == seq_index) & (every_id != last_block)
+    asked_for = jnp.sum(jnp.where(mine, every_id % mem_dev + 1, 0), axis=1) - 1
+    outgoing = memory_store[jnp.maximum(asked_for, 0)]
+    before, outgoing, shared = lax.optimization_barrier((before, outgoing, shared))
+    returned = lax.all_to_all(outgoing, "seq", split_axis=0, concat_axis=0, tiled=True)
     local_part = window_attention(
         queries, jnp.concatenate([before[0], keys]), jnp.concatenate([before[1], values]), first_row
     )

time: 326 us -> 454 us (1.39)
  waiting for transfers between devices: 163 us -> 239 us
  blocking collectives: 0 us -> 63 us
  starting transfers between devices: 26.2 us -> 14.5 us
    psum x1, waiting for transfers between devices: 13.7 us -> 109 us  [on_device(): lax.psum(jnp.where(seq_index == owners - 1, memory_store[mem_dev - 1], jn...]
    all_gather x0 -> x1, blocking collectives: none -> 63 us  [on_device(): lax.all_gather(block_ids, 'seq', axis=0, tiled=True)]
    all_to_all x1 -> x0, waiting for transfers between devices: 18.3 us -> none  [on_device(): lax.all_to_all(slot_table, 'seq', split_axis=0, concat_axis=0, tiled=True)]
    all_to_all x1 -> x0, starting transfers between devices: 12.7 us -> none  [on_device(): lax.all_to_all(slot_table, 'seq', split_axis=0, concat_axis=0, tiled=True)]
  transfers between devices with their start and end apart: 6 -> 5, of which waited for: 4 -> 3; matrix products, arithmetic and copies ran while one was open for 34% -> 24% of each run, Pallas kernels for 0% -> 0%
where the time goes in v3:
time: 454 us; the launch traced here: 452 us
  waiting for transfers between devices  239 us (53%)
  blocking collectives  63 us (14%)
  local copies, waits for them, and re-layouts  52.9 us (12%)
  matrix products  48.6 us (11%)
  other arithmetic  17 us (4%)
  between operations  15.1 us (3%)
  starting transfers between devices  14.5 us (3%)
    all_to_all x1, waiting for transfers between devices, on_device(): lax.all_to_all(outgoing, 'seq', split_axis=0, concat_axis=0, tiled=True)  114 us
    psum x1, waiting for transfers between devices, on_device(): lax.psum(jnp.where(seq_index == owners - 1, memory_store[mem_dev - 1], jn...  109 us
    all_gather x1, blocking collectives, on_device(): lax.all_gather(block_ids, 'seq', axis=0, tiled=True)  63 us
    sub x2, matrix products, masked_softmax(): weights = jnp.where(allowed, jnp.exp(scores - row_max), 0.0)  23.2 us
    dot_general x2, matrix products, per_tile(): jnp.einsum('hqk,khd->qhd', attend_weights, value_tile, preferred_element_...  16.9 us
    all_to_all x1, waiting for transfers between devices, on_device(): lax.all_to_all(attended.reshape(groups, out_rows, features), 'head', spli...  16.3 us
  transfers between devices with their start and end apart: 5, of which 3 were waited for; matrix products, arithmetic and copies ran while one was open for 24% of the time, Pallas kernels for 0%

profile of v3, /device:TPU:2, one launch (start us, length us, event | category | flops | bytes accessed | tf_op | source)
XLA Modules:
  0.0 451.7 jit_solution(179319438945823830)
XLA Ops:
  7.4 1.6 copy.52
  9.0 0.5 copy.53
  9.5 1.5 pad_maximum_fusion.1
  11.0 0.1 copy-done.1
  11.2 2.0 collective-permute-start
  13.2 1.5 select_bitcast_fusion
  14.7 0.0 all-reduce.2.cloned.1.call-update
  14.8 63.0 %all-gather = s32[64,8,4]{1,2,0:T(4,128)S(1)} all-gather(s32[1,8,4]{1,2,0:T(4,128)S(1)} %bitcast.85), channel_id=1, replica_groups=mesh['seq'=64,'head'=4] {'seq'}, dimensions={0}, use_global_device_ids=true | all-gather | bytes 8320 | tf_op jit(solution)/shard_map/all_gather | solution.py:122
  77.7 0.1 reshape.283
  77.9 0.1 reduce_sum.51
  78.0 0.1 reduce_sum.52
  78.1 1.7 pad_maximum_fusion
  79.9 5.5 %gather_fusion = bf16[64,2,64,512]{3,2,1,0:T(8,128)(2,1)} fusion(bf16[16,2,64,512]{3,2,1,0:T(8,128)(2,1)S(1)} %pad_maximum_fusion, s32[1024]{0:T(1024)S(1)} %pad_clamp_fusion.1), kind=kCustom, calls=%fused_computation | custom fusion | bytes 16777472 | tf_op jit(solution)/shard_map/gather | solution.py:125
  85.4 108.5 %all-reduce.2.cloned.1.call-done = bf16[2,64,512]{2,1,0:T(8,128)(2,1)} async-done(((bf16[2,64,512]{2,1,0:T(8,128)(2,1)}), bf16[2,64,512]{2,1,0:T(8,128)(2,1)}) %all-reduce.2.cloned.1.call-update) | async-done | bytes 131088 | tf_op jit(solution)/shard_map/psum | solution.py:118
  193.9 8.0 %all-to-all-start = ((bf16[64,2,64,512]{3,2,1,0:T(8,128)(2,1)}), bf16[64,2,64,512]{3,2,1,0:T(8,128)(2,1)}, u32[]{:S(2)}, u32[]{:S(2)}) async-start(bf16[64,2,64,512]{3,2,1,0:T(8,128)(2,1)} %gather_fusion), calls=%async_computation | async-start | bytes 16777216 | tf_op jit(solution)/shard_map/all_to_all | solution.py:127
  201.9 0.0 copy-start
  201.9 0.0 copy-start.12
  201.9 0.2 all-gather.3.cloned.1.call-start
  202.2 0.3 all-gather.3.cloned.1.call-update
  202.5 0.1 copy.57
  202.6 0.1 reshape.260
  202.7 0.1 copy.51
  202.8 0.1 eq.27
  202.9 0.3 copy-done
  203.1 1.1 reshape.261
  204.3 0.7 broadcast_bitcast_fusion
  204.9 1.8 slice_bitcast_fusion
  206.8 0.1 copy-done.2
  206.8 1.7 pad_maximum_fusion.2
  208.5 60.5 %while.13 = (s32[]{:T(128)}, f32[2,512,4,128]{3,2,1,0:T(4,128)}, s32[2]{0:T(128)S(1)}, bf16[2048,512]{0,1:T(8,128)(2,1)S(1)}, s32[]{:T(128)}, /*index=5*/bf16[10...) while((s32[]{:T(128)}, f32[2,512,4,128]{3,2,1,0:T(4,128)}, ...), condition=%wide.region_8.9_spmd, body=%wide.region_5.8_spmd.sunk | while | flops 2444237824 | bytes 44080892 | solution.py:64
  208.5 0.6 dynamic_slice.37
  209.7 0.8 and_and_fusion.2
  210.5 3.3 constant_dynamic-slice_fusion.5
  213.9 1.1 constant_dynamic-slice_fusion.6
  214.9 1.0 copy.84
  215.9 11.6 %fusion.59 = (f32[4,512]{1,0:T(4,128)S(1)}, f32[4,512,1536]{2,1,0:T(8,128)}) fusion(pred[512,1536]{1,0:T(8,128)(4,1)S(1)} %and_and_fusion.2, bf16[512,4,128]{0,2,1:T(8,128)(2,1)} %bitcast.78, bf16[1536,4,128]{0,2,1:T(8,128)(2,1)} %bitcast.77), kind=kOutput, calls=%fused_computation.78.clone.1 | convolution fusion | flops 1629488640 | bytes 15474688 | tf_op jit(solution)/shard_map/while/body/eval_jaxpr/sub | solution.py:26
  227.5 8.5 %fusion.60 = f32[1,512,4,128]{1,3,2,0:T(8,128)} fusion(bf16[1536,4,128]{0,2,1:T(8,128)(2,1)} %bitcast.76, f32[4,512,1536]{2,1,0:T(8,128)} %get-tuple-element.234, f32[4,512]{1,0:T(4,128)S(1)} %get-tuple-element.235), kind=kOutput, calls=%fused_computation.14.clone.1 | convolution fusion | flops 811597824 | bytes 15212544 | tf_op jit(solution)/shard_map/while/body/eval_jaxpr/hqk,khd->qhd/dot_general | solution.py:60
  236.0 1.6 copy.85
  237.6 1.1 constant_dynamic-update-slice_fusion.2
  238.7 0.6 dynamic_slice.37
  240.0 0.8 and_and_fusion.2
  240.8 3.4 constant_dynamic-slice_fusion.5
  244.2 1.1 constant_dynamic-slice_fusion.6
  245.2 1.0 copy.84
  246.2 11.6 %fusion.59 = (f32[4,512]{1,0:T(4,128)S(1)}, f32[4,512,1536]{2,1,0:T(8,128)}) fusion(pred[512,1536]{1,0:T(8,128)(4,1)S(1)} %and_and_fusion.2, bf16[512,4,128]{0,2,1:T(8,128)(2,1)} %bitcast.78, bf16[1536,4,128]{0,2,1:T(8,128)(2,1)} %bitcast.77), kind=kOutput, calls=%fused_computation.78.clone.1 | convolution fusion | flops 1629488640 | bytes 15474688 | tf_op jit(solution)/shard_map/while/body/eval_jaxpr/sub | solution.py:26
  257.8 8.5 %fusion.60 = f32[1,512,4,128]{1,3,2,0:T(8,128)} fusion(bf16[1536,4,128]{0,2,1:T(8,128)(2,1)} %bitcast.76, f32[4,512,1536]{2,1,0:T(8,128)} %get-tuple-element.234, f32[4,512]{1,0:T(4,128)S(1)} %get-tuple-element.235), kind=kOutput, calls=%fused_computation.14.clone.1 | convolution fusion | flops 811597824 | bytes 15212544 | tf_op jit(solution)/shard_map/while/body/eval_jaxpr/hqk,khd->qhd/dot_general | solution.py:60
  266.3 1.6 copy.85
  267.9 1.1 constant_dynamic-update-slice_fusion.2
  269.0 3.1 reshape.263
  272.1 114.0 %all-to-all-done = bf16[64,2,64,512]{3,2,1,0:T(8,128)(2,1)} async-done(((bf16[64,2,64,512]{3,2,1,0:T(8,128)(2,1)}), bf16[64,2,64,512]{3,2,1,0:T(8,128)(2,1)}, u32[]{:S(2)}, u32[]{:S(2)}) %all-to-all-start) | async-done | bytes 8388640 | tf_op jit(solution)/shard_map/all_to_all | solution.py:127
  386.2 6.2 %gather_fusion.1 = bf16[32,2,64,512]{3,2,1,0:T(8,128)(2,1)} fusion(bf16[64,2,64,512]{3,2,1,0:T(8,128)(2,1)} %all-to-all-done, s32[1024]{0:T(1024)S(1)} %pad_clamp_fusion), kind=kCustom, calls=%fused_computation.1 | custom fusion | bytes 8388736 | tf_op jit(solution)/shard_map/gather | solution.py:131
  392.3 2.6 broadcast_select_fusion
  394.9 2.3 fusion.38
  397.2 2.5 reshape_squeeze.7
  399.8 4.1 reshape_squeeze.6
  403.8 0.7 fusion.22
  404.6 3.1 fusion.39
  407.7 0.9 fusion.25
  408.6 1.8 copy.62
  410.4 3.2 reshape.262
  413.7 3.1 add_convert_fusion
  416.8 4.3 all-to-all-start.1
  421.1 16.3 %all-to-all-done.1 = bf16[4,256,512]{2,1,0:T(8,128)(2,1)S(1)} async-done(((bf16[4,256,512]{2,1,0:T(8,128)(2,1)}), bf16[4,256,512]{2,1,0:T(8,128)(2,1)S(1)}, u32[]{:S(2)}, u32[]{:S(2)}) %all-to-all-start.1) | async-done | bytes 1048608 | tf_op jit(solution)/shard_map/all_to_all | solution.py:140
  437.4 6.9 %convert_reduce_fusion = bf16[256,2048]{1,0:T(8,128)(2,1)} fusion(bf16[4,256,512]{2,1,0:T(8,128)(2,1)S(1)} %all-to-all-done.1, bf16[4,512,2048]{2,1,0:T(8,128)(2,1)} %bitcast.86), kind=kOutput, calls=%fused_computation.30 | convolution fusion | flops 2151153664 | bytes 10485760 | tf_op jit(solution)/shard_map/gqf,gfn->gqn/dot_general | solution.py:143
  (40 shorter events, 0.2 us)
Async XLA Ops:
  7.4 1.6 copy-start.7
  7.4 186.5 %all-reduce.2.cloned.1.call-start = ((), (), s32[]{:S(2)}) async-start(), calls=%async_computation.2 | async-start | bytes 262144 | tf_op jit(solution)/shard_map/psum | solution.py:118
  9.5 1.7 copy-start.1
  9.5 3.7 copy-start.5
  11.2 3.6 copy-start.9
  11.2 182.8 %collective-permute-start = (bf16[2,1024,512]{1,2,0:T(8,128)(2,1)}, bf16[2,1024,512]{1,2,0:T(8,128)(2,1)}, u32[]{:S(2)}, u32[]{:S(2)}) collective-permute-start(bf16[2,1024,512]{1,2,0:T(8,128)(2,1)} %pad_maximum_fusion.1), channel_id=1, source_target_pairs={{0,4},{4,8},{8,12},{12,16},{16,20},{20,24},{24,28},{28,32},{32,36}... | collective-permute-start | bytes 6291464 | tf_op jit(solution)/shard_map/ppermute | solution.py:21
  193.9 192.2 %all-to-all-start = ((bf16[64,2,64,512]{3,2,1,0:T(8,128)(2,1)}), bf16[64,2,64,512]{3,2,1,0:T(8,128)(2,1)}, u32[]{:S(2)}, u32[]{:S(2)}) async-start(bf16[64,2,64,512]{3,2,1,0:T(8,128)(2,1)} %gather_fusion), calls=%async_computation | async-start | bytes 16777216 | tf_op jit(solution)/shard_map/all_to_all | solution.py:127
  201.9 1.2 copy-start
  201.9 2.3 copy-start.12
  201.9 219.1 %all-gather.3.cloned.1.call-start = ((), (), s32[]{:S(2)}) async-start(), calls=%async_computation.3 | async-start | bytes 10485760 | tf_op jit(solution)/shard_map/all_gather | solution.py:101
  204.9 1.9 copy-start.2
  272.1 120.2 %copy-start.8 = (bf16[2,64,512]{2,1,0:T(8,128)(2,1)S(1)}, bf16[2,64,512]{2,1,0:T(8,128)(2,1)}, u32[]{:S(2)}) copy-start(bf16[2,64,512]{2,1,0:T(8,128)(2,1)} %all-reduce.2.cloned.1.call-done) | copy-start | bytes 393220
  399.8 4.1 copy-start.4
  404.6 3.1 copy-start.6
  410.4 3.2 copy-start.3
  410.4 3.2 copy-start.10
  410.4 3.2 copy-start.11
  416.8 20.6 %all-to-all-start.1 = ((bf16[4,256,512]{2,1,0:T(8,128)(2,1)}), bf16[4,256,512]{2,1,0:T(8,128)(2,1)S(1)}, u32[]{:S(2)}, u32[]{:S(2)}) async-start(bf16[4,256,512]{2,1,0:T(8,128)(2,1)} %add_convert_fusion), calls=%async_computation.1 | async-start | bytes 2097152 | tf_op jit(solution)/shard_map/all_to_all | solution.py:140
Sparse Core Ops, SparseCore 0:
  14.9 178.9 all-reduce.1
Sparse Core Ops, SparseCore 1:
  204.2 86.5 all-gather.2

commit v4 on v2

--- a/solution.py
+++ b/solution.py
@@ -3,6 +3,8 @@
 import jax
 import jax.numpy as jnp
 from jax import lax
+from jax.experimental import pallas as pl
+from jax.experimental.pallas import tpu as pltpu
 from jax.sharding import PartitionSpec as P
 
 HDIM = 128
@@ -83,6 +85,58 @@
         "bhqk,bkhd->bqhd", attend_weights, value_blocks, preferred_element_type=jnp.float32
     )
     return remote.reshape(tok_rows, heads_here, HDIM)
+
+
+def mixed_memory_attention(queries, returned, shared, local_part, mixing_row, slot_owner, slot_shared):
+    tok_rows, features = queries.shape
+    heads_here = features // HDIM
+    block_count = tok_rows // QBLK
+    score_scale = 1.0 / math.sqrt(HDIM)
+
+    def kernel(owner_ref, flag_ref, q_ref, r0, r1, r2, r3, sh_ref, loc_ref, mix_ref, out_ref):
+        c = pl.program_id(0)
+        fetched = (r0, r1, r2, r3)
+        key_parts = []
+        value_parts = []
+        for j in range(TOPM):
+            use_shared = flag_ref[c * TOPM + j] == 1
+            key_parts.append(jnp.where(use_shared, sh_ref[0], fetched[j][0, 0]))
+            value_parts.append(jnp.where(use_shared, sh_ref[1], fetched[j][0, 1]))
+        key_tile = jnp.concatenate(key_parts, axis=0)
+        value_tile = jnp.concatenate(value_parts, axis=0)
+        query_tile = q_ref[...]
+        for h in range(heads_here):
+            cols = slice(h * HDIM, (h + 1) * HDIM)
+            scores = lax.dot_general(query_tile[:, cols], key_tile[:, cols], (((1,), (1,)), ((), ())),
+                                     preferred_element_type=jnp.float32) * score_scale
+            row_max = jnp.max(scores, axis=-1, keepdims=True)
+            weights = jnp.exp(scores - row_max)
+            weights = (weights / jnp.sum(weights, axis=-1, keepdims=True)).astype(jnp.bfloat16)
+            remote = jnp.dot(weights, value_tile[:, cols], preferred_element_type=jnp.float32)
+            gate = mix_ref[:, cols]
+            out_ref[:, cols] = (gate * remote + (1.0 - gate) * loc_ref[:, cols]).astype(jnp.bfloat16)
+
+    def fetched_spec(j):
+        return pl.BlockSpec((1, 2, MROWS, features), lambda c, owner, flag: (owner[c * TOPM + j], 0, 0, 0))
+
+    grid_spec = pltpu.PrefetchScalarGridSpec(
+        num_scalar_prefetch=2,
+        grid=(block_count,),
+        in_specs=[pl.BlockSpec((QBLK, features), lambda c, owner, flag: (c, 0))]
+        + [fetched_spec(j) for j in range(TOPM)]
+        + [
+            pl.BlockSpec((2, MROWS, features), lambda c, owner, flag: (0, 0, 0)),
+            pl.BlockSpec((QBLK, features), lambda c, owner, flag: (c, 0)),
+            pl.BlockSpec((1, features), lambda c, owner, flag: (0, 0)),
+        ],
+        out_specs=pl.BlockSpec((QBLK, features), lambda c, owner, flag: (c, 0)),
+    )
+    return pl.pallas_call(
+        kernel,
+        grid_spec=grid_spec,
+        out_shape=jax.ShapeDtypeStruct((tok_rows, features), jnp.bfloat16),
+        compiler_params=pltpu.CompilerParams(dimension_semantics=("arbitrary",)),
+    )(slot_owner, slot_shared, queries, returned, returned, returned, returned, shared, local_part, mixing_row)
 
 
 def build_table(slot_index, offset, in_use, total_slots):
@@ -127,13 +181,15 @@
     local_part = window_attention(
         queries, jnp.concatenate([before[0], keys]), jnp.concatenate([before[1], values]), first_row
     )
-    fetched = jnp.where(is_last[:, None, None, None], shared[None], returned[owner_index])
-    remote = memory_attention(queries, fetched)
-    mixing = jax.nn.sigmoid(gate_bias)[None, :, None]
-    attended = (
-        (mixing * remote + (1.0 - mixing) * local_part)
-        .reshape(tok_rows, features)
-        .astype(jnp.bfloat16)
+    mixing_row = jnp.repeat(jax.nn.sigmoid(gate_bias), HDIM)[None, :]
+    attended = mixed_memory_attention(
+        queries,
+        returned,
+        shared,
+        local_part.reshape(tok_rows, features),
+        mixing_row,
+        owner_index,
+        is_last.astype(jnp.int32),
     )
     out_rows = tok_rows // groups
     gathered = lax.all_to_all(

time: 326 us -> 313 us (0.960)
  local copies, waits for them, and re-layouts: 52.8 us -> 31.6 us
  Pallas kernels: 0 us -> 11.1 us
  other arithmetic: 18.4 us -> 9.24 us
  waiting for transfers between devices: 163 us -> 171 us
    psum x1, waiting for transfers between devices: 13.7 us -> 137 us  [on_device(): lax.psum(jnp.where(seq_index == owners - 1, memory_store[mem_dev - 1], jn...]
    all_to_all x1, waiting for transfers between devices: 114 us -> 0.01 us  [on_device(): lax.all_to_all(outgoing, 'seq', split_axis=0, concat_axis=0, tiled=True)]
    pallas_call x0 -> x1, Pallas kernels: none -> 11.1 us  [mixed_memory_attention(): pl.pallas_call(kernel, grid_spec=grid_spec, out_shape=jax.ShapeDtypeStruc...]
    reshape x3 -> x0, local copies, waits for them, and re-layouts: 7.41 us -> none  [the longest x1 3.23 us: memory_attention(): return remote.reshape(tok_rows, heads_here, HDIM)]
    another operation x2 -> x0, local copies, waits for them, and re-layouts: 6.59 us -> none  [the longest x1 4.05 us: memory_attention(): fetched[:, 1].reshape(block_count, TOPM * MROWS, heads_here, HDIM)]
    gather x1 -> x0, local copies, waits for them, and re-layouts: 6.15 us -> none  [on_device(): returned[owner_index]]
  transfers between devices with their start and end apart: 6 -> 6, of which waited for: 4 -> 3; matrix products, arithmetic and copies ran while one was open for 34% -> 25% of each run, Pallas kernels for 0% -> 4%
where the time goes in v4:
time: 313 us
  waiting for transfers between devices  171 us (55%)
  matrix products  46.7 us (15%)
  local copies, waits for them, and re-layouts  31.6 us (10%)
  starting transfers between devices  26.2 us (8%)
  between operations  15 us (5%)
  Pallas kernels  11.1 us (4%)
  other arithmetic  9.24 us (3%)
    psum x1, waiting for transfers between devices, on_device(): lax.psum(jnp.where(seq_index == owners - 1, memory_store[mem_dev - 1], jn...  137 us
    sub x2, matrix products, masked_softmax(): weights = jnp.where(allowed, jnp.exp(scores - row_max), 0.0)  23 us
    all_to_all x1, waiting for transfers between devices, on_device(): lax.all_to_all(slot_table, 'seq', split_axis=0, concat_axis=0, tiled=True)  17.7 us
    dot_general x2, matrix products, per_tile(): jnp.einsum('hqk,khd->qhd', attend_weights, value_tile, preferred_element_...  16.8 us
    all_to_all x1, waiting for transfers between devices, on_device(): lax.all_to_all(attended.reshape(groups, out_rows, features), 'head', spli...  16 us
    all_to_all x1, starting transfers between devices, on_device(): lax.all_to_all(slot_table, 'seq', split_axis=0, concat_axis=0, tiled=True)  12.7 us
    pallas_call x1, Pallas kernels, mixed_memory_attention(): pl.pallas_call(kernel, grid_spec=grid_spec, out_shape=jax.ShapeDtypeStruc...  11.1 us
    dot_general x1, matrix products, on_device(): jnp.einsum('gqf,gfn->gqn', gathered, full_weight.reshape(groups, features...  6.92 us
  transfers between devices with their start and end apart: 6, of which 3 were waited for; matrix products, arithmetic and copies ran while one was open for 25% of the time, Pallas kernels for 4%

profile of v4, /device:TPU:2, one launch (start us, length us, event | category | flops | bytes accessed | tf_op | source)
XLA Modules:
  0.0 312.6 jit_solution(8299052656078200807)
XLA Ops:
  7.4 1.6 copy.44
  8.9 0.0 copy-done.5
  9.0 0.5 copy.45
  9.5 0.0 copy-start.1
  9.5 0.0 copy-start.6
  9.5 1.6 pad_maximum_fusion.1
  11.2 0.0 copy-done.1
  11.2 1.9 collective-permute-start
  13.1 0.0 copy-done.6
  13.1 0.1 copy.43
  13.2 0.1 reshape.209
  13.3 0.0 copy-start.7
  13.3 0.6 compare_not_fusion
  13.9 0.1 select_reduce_fusion.1
  14.0 0.7 copy.46
  14.7 12.7 %all-to-all-start = ((s32[64,1,1]{2,1,0:T(1,128)}), s32[64,1,1]{2,1,0:T(1,128)S(1)}, u32[]{:S(2)}, u32[]{:S(2)}) async-start(s32[64,1,1]{2,1,0:T(1,128)} %copy.46), calls=%async_computation | async-start | bytes 65536 | tf_op jit(solution)/shard_map/all_to_all | solution.py:173
  27.5 1.7 pad_maximum_fusion
  29.2 0.0 copy-done.7
  29.2 17.7 %all-to-all-done = s32[64,1,1]{2,1,0:T(1,128)S(1)} async-done(((s32[64,1,1]{2,1,0:T(1,128)}), s32[64,1,1]{2,1,0:T(1,128)S(1)}, u32[]{:S(2)}, u32[]{:S(2)}) %all-to-all-start) | async-done | bytes 288 | tf_op jit(solution)/shard_map/all_to_all | solution.py:173
  46.9 1.2 maximum_reduce_fusion
  48.1 5.5 %gather_fusion = bf16[64,2,64,512]{3,2,1,0:T(8,128)(2,1)} fusion(bf16[16,2,64,512]{3,2,1,0:T(8,128)(2,1)S(1)} %pad_maximum_fusion, s32[1024]{0:T(1024)S(1)} %pad_clamp_fusion), kind=kCustom, calls=%fused_computation | custom fusion | bytes 16777472 | tf_op jit(solution)/shard_map/gather | solution.py:174
  53.6 0.0 collective-permute-done
  53.6 6.8 %all-to-all-start.1 = ((bf16[64,2,64,512]{3,2,1,0:T(8,128)(2,1)}), bf16[64,2,64,512]{3,2,1,0:T(8,128)(2,1)}, u32[]{:S(2)}, u32[]{:S(2)}) async-start(bf16[64,2,64,512]{3,2,1,0:T(8,128)(2,1)} %gather_fusion), calls=%async_computation.1 | async-start | bytes 16777216 | tf_op jit(solution)/shard_map/all_to_all | solution.py:176
  60.5 0.0 all-reduce.2.cloned.1.call-start
  60.5 0.0 copy-done.3
  60.6 0.0 copy-done.4
  60.6 0.0 copy-start.8
  60.6 0.7 select_bitcast_fusion
  61.2 0.0 all-reduce.2.cloned.1.call-update
  61.3 0.2 all-gather.2.cloned.1.call-start
  61.5 0.3 all-gather.2.cloned.1.call-update
  61.9 0.0 copy-done.8
  61.9 0.0 copy-start.2
  61.9 1.8 slice_bitcast_fusion
  63.7 0.0 copy-done.2
  63.7 1.6 pad_maximum_fusion.2
  65.4 60.2 %while.13 = (s32[]{:T(128)}, f32[2,512,4,128]{3,2,1,0:T(4,128)}, s32[2]{0:T(128)S(1)}, bf16[2048,512]{0,1:T(8,128)(2,1)S(1)}, s32[]{:T(128)}, /*index=5*/bf16[10...) while((s32[]{:T(128)}, f32[2,512,4,128]{3,2,1,0:T(4,128)}, ...), condition=%wide.region_5.6_spmd, body=%wide.region_2.5_spmd.sunk | while | flops 2444237824 | bytes 44080892 | solution.py:66
  65.4 0.6 dynamic_slice.37
  66.7 0.8 and_and_fusion.2
  67.5 3.3 %constant_dynamic-slice_fusion.5 = (bf16[1536,512]{0,1:T(8,128)(2,1)}, bf16[1536,512]{0,1:T(8,128)(2,1)}) fusion(bf16[2048,512]{0,1:T(8,128)(2,1)} %get-tuple-element.269, s32[]{:T(128)S(6)} %select_n.87, bf16[2048,512]{0,1:T(8,128)(2,1)S(1)} %get-tuple-element.266), kind=kLoop, calls=%fused_computation.19.clone.1 | loop fusion | bytes 6291460 | tf_op jit(solution)/shard_map/while/body/eval_jaxpr/dynamic_slice | solution.py:44
  70.8 1.1 constant_dynamic-slice_fusion.6
  71.9 1.0 copy.61
  72.9 11.5 %fusion.37 = (f32[4,512]{1,0:T(4,128)S(1)}, f32[4,512,1536]{2,1,0:T(8,128)}) fusion(pred[512,1536]{1,0:T(8,128)(4,1)S(1)} %and_and_fusion.2, bf16[512,4,128]{0,2,1:T(8,128)(2,1)} %bitcast.57, bf16[1536,4,128]{0,2,1:T(8,128)(2,1)} %bitcast.56), kind=kOutput, calls=%fused_computation.51.clone.1 | convolution fusion | flops 1629488640 | bytes 15474688 | tf_op jit(solution)/shard_map/while/body/eval_jaxpr/sub | solution.py:28
  84.4 8.4 %fusion.38 = f32[1,512,4,128]{1,3,2,0:T(8,128)} fusion(bf16[1536,4,128]{0,2,1:T(8,128)(2,1)} %bitcast.55, f32[4,512,1536]{2,1,0:T(8,128)} %get-tuple-element.235, f32[4,512]{1,0:T(4,128)S(1)} %get-tuple-element.236), kind=kOutput, calls=%fused_computation.13.clone.1 | convolution fusion | flops 811597824 | bytes 15212544 | tf_op jit(solution)/shard_map/while/body/eval_jaxpr/hqk,khd->qhd/dot_general | solution.py:62
  92.7 1.6 copy.62
  94.3 1.1 constant_dynamic-update-slice_fusion.2
  95.4 0.6 dynamic_slice.37
  96.7 0.8 and_and_fusion.2
  97.5 3.3 %constant_dynamic-slice_fusion.5 = (bf16[1536,512]{0,1:T(8,128)(2,1)}, bf16[1536,512]{0,1:T(8,128)(2,1)}) fusion(bf16[2048,512]{0,1:T(8,128)(2,1)} %get-tuple-element.269, s32[]{:T(128)S(6)} %select_n.87, bf16[2048,512]{0,1:T(8,128)(2,1)S(1)} %get-tuple-element.266), kind=kLoop, calls=%fused_computation.19.clone.1 | loop fusion | bytes 6291460 | tf_op jit(solution)/shard_map/while/body/eval_jaxpr/dynamic_slice | solution.py:44
  100.8 1.1 constant_dynamic-slice_fusion.6
  101.9 1.0 copy.61
  102.9 11.5 %fusion.37 = (f32[4,512]{1,0:T(4,128)S(1)}, f32[4,512,1536]{2,1,0:T(8,128)}) fusion(pred[512,1536]{1,0:T(8,128)(4,1)S(1)} %and_and_fusion.2, bf16[512,4,128]{0,2,1:T(8,128)(2,1)} %bitcast.57, bf16[1536,4,128]{0,2,1:T(8,128)(2,1)} %bitcast.56), kind=kOutput, calls=%fused_computation.51.clone.1 | convolution fusion | flops 1629488640 | bytes 15474688 | tf_op jit(solution)/shard_map/while/body/eval_jaxpr/sub | solution.py:28
  114.4 8.4 %fusion.38 = f32[1,512,4,128]{1,3,2,0:T(8,128)} fusion(bf16[1536,4,128]{0,2,1:T(8,128)(2,1)} %bitcast.55, f32[4,512,1536]{2,1,0:T(8,128)} %get-tuple-element.235, f32[4,512]{1,0:T(4,128)S(1)} %get-tuple-element.236), kind=kOutput, calls=%fused_computation.13.clone.1 | convolution fusion | flops 811597824 | bytes 15212544 | tf_op jit(solution)/shard_map/while/body/eval_jaxpr/hqk,khd->qhd/dot_general | solution.py:62
  122.9 1.6 copy.62
  124.5 1.1 constant_dynamic-update-slice_fusion.2
  125.6 3.2 %copy.58 = f32[128,8,4,128]{3,1,2,0:T(8,128)} copy(f32[128,8,4,128]{3,2,1,0:T(4,128)} %bitcast.66) | data formatting | bytes 4194304
  128.8 137.2 %all-reduce.2.cloned.1.call-done.sh_ref = bf16[2,64,512]{2,1,0:T(8,128)(2,1)} async-done(((bf16[2,64,512]{2,1,0:T(8,128)(2,1)}), bf16[2,64,512]{2,1,0:T(8,128)(2,1)}) %all-reduce.2.cloned.1.call-update) | async-done | bytes 131088 | tf_op jit(solution)/shard_map/psum | solution.py:177
  265.9 0.0 all-to-all-done.1.r0.r1.r2.r3
  265.9 0.7 broadcast_in_dim.77
  266.6 0.0 copy-done
  266.6 11.1 %shard_map.82 = bf16[1024,512]{1,0:T(8,128)(2,1)} custom-call(s32[32]{0:T(128)} %copy-done.7, s32[32]{0:T(128)} %get-tuple-element.177.flag_ref, bf16[1024,512]{1,0:T(8,128)(2,1)S(1)} %copy-done, bf16[64,2,64,512]{3,2,1,0:T(8,128)(2,1)} %all-to-all-done.1.r0.r1.r2.r3, bf16[64,2,64,512]{3,2,1,0:T(8,128)(2,1)} %all-to-all-done.1.r0.r1.r2.r3, ...), custom_call_target="tpu_custom_call" | custom-call | tf_op jit(solution)/shard_map/pallas_call | solution.py:134
  277.7 4.5 %all-to-all-start.2 = ((bf16[4,256,512]{2,1,0:T(8,128)(2,1)}), bf16[4,256,512]{2,1,0:T(8,128)(2,1)S(1)}, u32[]{:S(2)}, u32[]{:S(2)}) async-start(bf16[4,256,512]{2,1,0:T(8,128)(2,1)} %bitcast.61), calls=%async_computation.2 | async-start | bytes 2097152 | tf_op jit(solution)/shard_map/all_to_all | solution.py:195
  282.2 16.0 %all-to-all-done.2 = bf16[4,256,512]{2,1,0:T(8,128)(2,1)S(1)} async-done(((bf16[4,256,512]{2,1,0:T(8,128)(2,1)}), bf16[4,256,512]{2,1,0:T(8,128)(2,1)S(1)}, u32[]{:S(2)}, u32[]{:S(2)}) %all-to-all-start.2) | async-done | bytes 1048608 | tf_op jit(solution)/shard_map/all_to_all | solution.py:195
  298.2 6.9 %convert_reduce_fusion = bf16[256,2048]{1,0:T(8,128)(2,1)} fusion(bf16[4,256,512]{2,1,0:T(8,128)(2,1)S(1)} %all-to-all-done.2, bf16[4,512,2048]{2,1,0:T(8,128)(2,1)} %bitcast.68), kind=kOutput, calls=%fused_computation.24 | convolution fusion | flops 2151153664 | bytes 10485760 | tf_op jit(solution)/shard_map/gqf,gfn->gqn/dot_general | solution.py:198
  (17 shorter events, 0.1 us)
Async XLA Ops:
  7.4 1.6 copy-start.5
  9.5 1.7 copy-start.1
  9.5 3.6 %copy-start.6 = (s32[8,4]{0,1:T(4,128)S(1)}, s32[8,4]{0,1:T(4,128)}, u32[]{:S(2)}) copy-start(s32[8,4]{0,1:T(4,128)} %param.15) | copy-start | bytes 388
  11.2 42.5 %collective-permute-start = (bf16[2,1024,512]{1,2,0:T(8,128)(2,1)}, bf16[2,1024,512]{1,2,0:T(8,128)(2,1)}, u32[]{:S(2)}, u32[]{:S(2)}) collective-permute-start(bf16[2,1024,512]{1,2,0:T(8,128)(2,1)} %pad_maximum_fusion.1), channel_id=1, source_target_pairs={{0,4},{4,8},{8,12},{12,16},{16,20},{20,24},{24,28},{28,32},{32,36}... | collective-permute-start | bytes 6291464 | tf_op jit(solution)/shard_map/ppermute | solution.py:23
  13.3 15.9 %copy-start.7 = (s32[32]{0:T(128)}, s32[32]{0:T(128)S(1)}, u32[]{:S(2)}) copy-start(s32[32]{0:T(128)S(1)} %get-tuple-element.179.owner_ref) | copy-start | bytes 388
  14.7 32.2 %all-to-all-start = ((s32[64,1,1]{2,1,0:T(1,128)}), s32[64,1,1]{2,1,0:T(1,128)S(1)}, u32[]{:S(2)}, u32[]{:S(2)}) async-start(s32[64,1,1]{2,1,0:T(1,128)} %copy.46), calls=%async_computation | async-start | bytes 65536 | tf_op jit(solution)/shard_map/all_to_all | solution.py:173
  53.6 6.9 %copy-start.3 = (bf16[1024,512]{1,0:T(8,128)(2,1)S(1)}, bf16[1024,512]{1,0:T(8,128)(2,1)}, u32[]{:S(2)}) copy-start(bf16[1024,512]{1,0:T(8,128)(2,1)} %param.14) | copy-start | bytes 3145732
  53.6 6.9 %copy-start.4 = (bf16[1024,512]{1,0:T(8,128)(2,1)S(1)}, bf16[1024,512]{1,0:T(8,128)(2,1)}, u32[]{:S(2)}) copy-start(bf16[1024,512]{1,0:T(8,128)(2,1)} %param.13) | copy-start | bytes 3145732
  53.6 212.3 %all-to-all-start.1 = ((bf16[64,2,64,512]{3,2,1,0:T(8,128)(2,1)}), bf16[64,2,64,512]{3,2,1,0:T(8,128)(2,1)}, u32[]{:S(2)}, u32[]{:S(2)}) async-start(bf16[64,2,64,512]{3,2,1,0:T(8,128)(2,1)} %gather_fusion), calls=%async_computation.1 | async-start | bytes 16777216 | tf_op jit(solution)/shard_map/all_to_all | solution.py:176
  60.5 205.5 %all-reduce.2.cloned.1.call-start = ((), (), s32[]{:S(2)}) async-start(), calls=%async_computation.3 | async-start | bytes 262144 | tf_op jit(solution)/shard_map/psum | solution.py:177
  60.6 1.3 copy-start.8
  61.3 220.9 %all-gather.2.cloned.1.call-start = ((), (), s32[]{:S(2)}) async-start(), calls=%async_computation.4 | async-start | bytes 10485760 | tf_op jit(solution)/shard_map/all_gather | solution.py:155
  61.9 1.9 copy-start.2
  125.6 141.0 %copy-start = (bf16[1024,512]{1,0:T(8,128)(2,1)S(1)}, bf16[1024,512]{1,0:T(8,128)(2,1)}, u32[]{:S(2)}) copy-start(bf16[1024,512]{1,0:T(8,128)(2,1)} %get-tuple-element.280) | copy-start | bytes 3145732
  277.7 20.5 %all-to-all-start.2 = ((bf16[4,256,512]{2,1,0:T(8,128)(2,1)}), bf16[4,256,512]{2,1,0:T(8,128)(2,1)S(1)}, u32[]{:S(2)}, u32[]{:S(2)}) async-start(bf16[4,256,512]{2,1,0:T(8,128)(2,1)} %bitcast.61), calls=%async_computation.2 | async-start | bytes 2097152 | tf_op jit(solution)/shard_map/all_to_all | solution.py:195
Sparse Core Ops, SparseCore 0:
  64.8 201.1 all-reduce.1
Sparse Core Ops, SparseCore 1:
  63.6 86.7 all-gather.1

commit v5 on v4

--- a/solution.py
+++ b/solution.py
@@ -87,14 +87,14 @@
     return remote.reshape(tok_rows, heads_here, HDIM)
 
 
-def mixed_memory_attention(queries, returned, shared, local_part, mixing_row, slot_owner, slot_shared):
+def mixed_memory_attention(queries, returned, shared, local_part, mixing_row, block_order, slot_owner, slot_shared, written, first, count):
     tok_rows, features = queries.shape
     heads_here = features // HDIM
-    block_count = tok_rows // QBLK
     score_scale = 1.0 / math.sqrt(HDIM)
 
-    def kernel(owner_ref, flag_ref, q_ref, r0, r1, r2, r3, sh_ref, loc_ref, mix_ref, out_ref):
-        c = pl.program_id(0)
+    def kernel(order_ref, owner_ref, flag_ref, q_ref, r0, r1, r2, r3, sh_ref, loc_ref, mix_ref, *rest):
+        out_ref = rest[-1]
+        c = order_ref[first + pl.program_id(0)]
         fetched = (r0, r1, r2, r3)
         key_parts = []
         value_parts = []
@@ -107,8 +107,15 @@
         query_tile = q_ref[...]
         for h in range(heads_here):
             cols = slice(h * HDIM, (h + 1) * HDIM)
-            scores = lax.dot_general(query_tile[:, cols], key_tile[:, cols], (((1,), (1,)), ((), ())),
-                                     preferred_element_type=jnp.float32) * score_scale
+            scores = (
+                lax.dot_general(
+                    query_tile[:, cols],
+                    key_tile[:, cols],
+                    (((1,), (1,)), ((), ())),
+                    preferred_element_type=jnp.float32,
+                )
+                * score_scale
+            )
             row_max = jnp.max(scores, axis=-1, keepdims=True)
             weights = jnp.exp(scores - row_max)
             weights = (weights / jnp.sum(weights, axis=-1, keepdims=True)).astype(jnp.bfloat16)
@@ -116,27 +123,43 @@
             gate = mix_ref[:, cols]
             out_ref[:, cols] = (gate * remote + (1.0 - gate) * loc_ref[:, cols]).astype(jnp.bfloat16)
 
+    def rows_spec():
+        return pl.BlockSpec((QBLK, features), lambda i, order, owner, flag: (order[first + i], 0))
+
     def fetched_spec(j):
-        return pl.BlockSpec((1, 2, MROWS, features), lambda c, owner, flag: (owner[c * TOPM + j], 0, 0, 0))
-
-    grid_spec = pltpu.PrefetchScalarGridSpec(
-        num_scalar_prefetch=2,
-        grid=(block_count,),
-        in_specs=[pl.BlockSpec((QBLK, features), lambda c, owner, flag: (c, 0))]
+        return pl.BlockSpec(
+            (1, 2, MROWS, features),
+            lambda i, order, owner, flag: (owner[order[first + i] * TOPM + j], 0, 0, 0),
+        )
+
+    in_specs = (
+        [rows_spec()]
         + [fetched_spec(j) for j in range(TOPM)]
         + [
-            pl.BlockSpec((2, MROWS, features), lambda c, owner, flag: (0, 0, 0)),
-            pl.BlockSpec((QBLK, features), lambda c, owner, flag: (c, 0)),
-            pl.BlockSpec((1, features), lambda c, owner, flag: (0, 0)),
-        ],
-        out_specs=pl.BlockSpec((QBLK, features), lambda c, owner, flag: (c, 0)),
+            pl.BlockSpec((2, MROWS, features), lambda i, order, owner, flag: (0, 0, 0)),
+            rows_spec(),
+            pl.BlockSpec((1, features), lambda i, order, owner, flag: (0, 0)),
+        ]
+    )
+    operands = [queries, returned, returned, returned, returned, shared, local_part, mixing_row]
+    aliases = {}
+    if written is not None:
+        in_specs.append(pl.BlockSpec(memory_space=pl.ANY))
+        operands.append(written)
+        aliases = {3 + len(operands) - 1: 0}
+    grid_spec = pltpu.PrefetchScalarGridSpec(
+        num_scalar_prefetch=3,
+        grid=(count,),
+        in_specs=in_specs,
+        out_specs=rows_spec(),
     )
     return pl.pallas_call(
         kernel,
         grid_spec=grid_spec,
         out_shape=jax.ShapeDtypeStruct((tok_rows, features), jnp.bfloat16),
+        input_output_aliases=aliases,
         compiler_params=pltpu.CompilerParams(dimension_semantics=("arbitrary",)),
-    )(slot_owner, slot_shared, queries, returned, returned, returned, returned, shared, local_part, mixing_row)
+    )(block_order, slot_owner, slot_shared, *operands)
 
 
 def build_table(slot_index, offset, in_use, total_slots):
@@ -182,14 +205,19 @@
         queries, jnp.concatenate([before[0], keys]), jnp.concatenate([before[1], values]), first_row
     )
     mixing_row = jnp.repeat(jax.nn.sigmoid(gate_bias), HDIM)[None, :]
+    block_count = tok_rows // QBLK
+    uses_shared = jnp.any(is_last.reshape(block_count, TOPM), axis=1)
+    block_order = jnp.argsort(uses_shared.astype(jnp.int32), stable=True).astype(jnp.int32)
+    flags = is_last.astype(jnp.int32)
+    local_rows = local_part.reshape(tok_rows, features)
+    no_shared = jnp.zeros_like(shared)
     attended = mixed_memory_attention(
-        queries,
-        returned,
-        shared,
-        local_part.reshape(tok_rows, features),
-        mixing_row,
-        owner_index,
-        is_last.astype(jnp.int32),
+        queries, returned, no_shared, local_rows, mixing_row, block_order, owner_index, flags,
+        None, 0, block_count - 1,
+    )
+    attended = mixed_memory_attention(
+        queries, returned, shared, local_rows, mixing_row, block_order, owner_index, flags,
+        attended, block_count - 1, 1,
     )
     out_rows = tok_rows // groups
     gathered = lax.all_to_all(

time: 313 us -> 305 us (0.974)
  waiting for transfers between devices: 171 us -> 159 us
    psum x1, waiting for transfers between devices: 137 us -> 8.51 us  [on_device(): lax.psum(jnp.where(seq_index == owners - 1, memory_store[mem_dev - 1], jn...]
    all_to_all x1, waiting for transfers between devices: 0.01 us -> 116 us  [on_device(): lax.all_to_all(outgoing, 'seq', split_axis=0, concat_axis=0, tiled=True)]
    pallas_call x1 -> x2, Pallas kernels: 11.1 us -> 13.6 us  [mixed_memory_attention(): pl.pallas_call(kernel, grid_spec=grid_spec, out_shape=jax.ShapeDtypeStruc...]
  transfers between devices with their start and end apart: 6 -> 6, of which waited for: 3 -> 4; matrix products, arithmetic and copies ran while one was open for 25% -> 26% of each run, Pallas kernels for 4% -> 4%
where the time goes in v5:
time: 305 us; the launch traced here: 304 us
  waiting for transfers between devices  159 us (52%)
  matrix products  46.8 us (15%)
  local copies, waits for them, and re-layouts  32.4 us (11%)
  starting transfers between devices  26.2 us (9%)
  between operations  15 us (5%)
  Pallas kernels  13.6 us (4%)
  other arithmetic  10.2 us (3%)
    all_to_all x1, waiting for transfers between devices, on_device(): lax.all_to_all(outgoing, 'seq', split_axis=0, concat_axis=0, tiled=True)  116 us
    sub x2, matrix products, masked_softmax(): weights = jnp.where(allowed, jnp.exp(scores - row_max), 0.0)  23 us
    all_to_all x1, waiting for transfers between devices, on_device(): lax.all_to_all(slot_table, 'seq', split_axis=0, concat_axis=0, tiled=True)  17.7 us
    dot_general x2, matrix products, per_tile(): jnp.einsum('hqk,khd->qhd', attend_weights, value_tile, preferred_element_...  16.9 us
    all_to_all x1, waiting for transfers between devices, on_device(): lax.all_to_all(attended.reshape(groups, out_rows, features), 'head', spli...  15.9 us
    pallas_call x2, Pallas kernels, mixed_memory_attention(): pl.pallas_call(kernel, grid_spec=grid_spec, out_shape=jax.ShapeDtypeStruc...  13.6 us
    all_to_all x1, starting transfers between devices, on_device(): lax.all_to_all(slot_table, 'seq', split_axis=0, concat_axis=0, tiled=True)  12.7 us
    psum x1, waiting for transfers between devices, on_device(): lax.psum(jnp.where(seq_index == owners - 1, memory_store[mem_dev - 1], jn...  8.51 us
  transfers between devices with their start and end apart: 6, of which 4 were waited for; matrix products, arithmetic and copies ran while one was open for 26% of the time, Pallas kernels for 4%

profile of v5, /device:TPU:2, one launch (start us, length us, event | category | flops | bytes accessed | tf_op | source)
XLA Modules:
  0.0 304.2 jit_solution(16989268354619205127)
XLA Ops:
  7.4 1.6 copy.45
  8.9 0.0 copy-done.5
  9.0 0.5 copy.46
  9.5 0.0 copy-start.1
  9.5 0.0 copy-start.6
  9.5 1.6 pad_maximum_fusion.1
  11.2 0.0 copy-done.1
  11.2 1.9 collective-permute-start
  13.1 0.0 copy-done.6
  13.1 0.1 copy.44
  13.2 0.1 reshape.210
  13.3 0.0 copy-start.7
  13.3 0.5 compare_not_fusion
  13.8 0.1 select_reduce_fusion.1
  13.9 0.7 copy.47
  14.6 12.7 %all-to-all-start = ((s32[64,1,1]{2,1,0:T(1,128)}), s32[64,1,1]{2,1,0:T(1,128)S(1)}, u32[]{:S(2)}, u32[]{:S(2)}) async-start(s32[64,1,1]{2,1,0:T(1,128)} %copy.47), calls=%async_computation | async-start | bytes 65536 | tf_op jit(solution)/shard_map/all_to_all | solution.py:196
  27.4 1.7 pad_maximum_fusion
  29.1 0.0 copy-done.7
  29.1 17.7 %all-to-all-done = s32[64,1,1]{2,1,0:T(1,128)S(1)} async-done(((s32[64,1,1]{2,1,0:T(1,128)}), s32[64,1,1]{2,1,0:T(1,128)S(1)}, u32[]{:S(2)}, u32[]{:S(2)}) %all-to-all-start) | async-done | bytes 288 | tf_op jit(solution)/shard_map/all_to_all | solution.py:196
  46.9 1.2 maximum_reduce_fusion
  48.1 5.5 %gather_fusion = bf16[64,2,64,512]{3,2,1,0:T(8,128)(2,1)} fusion(bf16[16,2,64,512]{3,2,1,0:T(8,128)(2,1)S(1)} %pad_maximum_fusion, s32[1024]{0:T(1024)S(1)} %pad_clamp_fusion), kind=kCustom, calls=%fused_computation | custom fusion | bytes 16777472 | tf_op jit(solution)/shard_map/gather | solution.py:197
  53.6 0.0 collective-permute-done
  53.6 6.8 %all-to-all-start.1 = ((bf16[64,2,64,512]{3,2,1,0:T(8,128)(2,1)}), bf16[64,2,64,512]{3,2,1,0:T(8,128)(2,1)}, u32[]{:S(2)}, u32[]{:S(2)}) async-start(bf16[64,2,64,512]{3,2,1,0:T(8,128)(2,1)} %gather_fusion), calls=%async_computation.1 | async-start | bytes 16777216 | tf_op jit(solution)/shard_map/all_to_all | solution.py:199
  60.4 0.0 all-reduce.2.cloned.1.call-start
  60.5 0.0 copy-done.3
  60.5 0.0 copy-start.8
  60.5 0.7 select_bitcast_fusion
  61.2 0.0 all-reduce.2.cloned.1.call-update
  61.2 0.2 all-gather.2.cloned.1.call-start
  61.4 0.3 all-gather.2.cloned.1.call-update
  61.8 1.0 sort.17
  62.9 0.0 copy-start.2
  62.9 1.8 slice_bitcast_fusion
  64.7 0.0 copy-done.2
  64.8 1.7 pad_maximum_fusion.2
  66.4 60.4 %while.13 = (s32[]{:T(128)}, f32[2,512,4,128]{3,2,1,0:T(4,128)}, s32[2]{0:T(128)S(1)}, bf16[2048,512]{0,1:T(8,128)(2,1)S(1)}, s32[]{:T(128)}, /*index=5*/bf16[10...) while((s32[]{:T(128)}, f32[2,512,4,128]{3,2,1,0:T(4,128)}, ...), condition=%wide.region_7.8_spmd, body=%wide.region_4.7_spmd.sunk | while | flops 2444237824 | bytes 44080892 | solution.py:66
  66.4 0.6 dynamic_slice.37
  67.7 0.8 and_and_fusion.2
  68.5 3.3 %constant_dynamic-slice_fusion.5 = (bf16[1536,512]{0,1:T(8,128)(2,1)}, bf16[1536,512]{0,1:T(8,128)(2,1)}) fusion(bf16[2048,512]{0,1:T(8,128)(2,1)} %get-tuple-element.271, s32[]{:T(128)S(6)} %select_n.87, bf16[2048,512]{0,1:T(8,128)(2,1)S(1)} %get-tuple-element.268), kind=kLoop, calls=%fused_computation.19.clone.1 | loop fusion | bytes 6291460 | tf_op jit(solution)/shard_map/while/body/eval_jaxpr/dynamic_slice | solution.py:44
  71.8 1.1 constant_dynamic-slice_fusion.6
  72.9 1.0 copy.62
  73.9 11.5 %fusion.37 = (f32[4,512]{1,0:T(4,128)S(1)}, f32[4,512,1536]{2,1,0:T(8,128)}) fusion(pred[512,1536]{1,0:T(8,128)(4,1)S(1)} %and_and_fusion.2, bf16[512,4,128]{0,2,1:T(8,128)(2,1)} %bitcast.59, bf16[1536,4,128]{0,2,1:T(8,128)(2,1)} %bitcast.56), kind=kOutput, calls=%fused_computation.52.clone.1 | convolution fusion | flops 1629488640 | bytes 15474688 | tf_op jit(solution)/shard_map/while/body/eval_jaxpr/sub | solution.py:28
  85.4 8.4 %fusion.38 = f32[1,512,4,128]{1,3,2,0:T(8,128)} fusion(bf16[1536,4,128]{0,2,1:T(8,128)(2,1)} %bitcast.55, f32[4,512,1536]{2,1,0:T(8,128)} %get-tuple-element.237, f32[4,512]{1,0:T(4,128)S(1)} %get-tuple-element.238), kind=kOutput, calls=%fused_computation.13.clone.1 | convolution fusion | flops 811597824 | bytes 15212544 | tf_op jit(solution)/shard_map/while/body/eval_jaxpr/hqk,khd->qhd/dot_general | solution.py:62
  93.8 1.6 copy.63
  95.4 1.1 constant_dynamic-update-slice_fusion.2
  96.5 0.6 dynamic_slice.37
  97.8 0.8 and_and_fusion.2
  98.6 3.4 %constant_dynamic-slice_fusion.5 = (bf16[1536,512]{0,1:T(8,128)(2,1)}, bf16[1536,512]{0,1:T(8,128)(2,1)}) fusion(bf16[2048,512]{0,1:T(8,128)(2,1)} %get-tuple-element.271, s32[]{:T(128)S(6)} %select_n.87, bf16[2048,512]{0,1:T(8,128)(2,1)S(1)} %get-tuple-element.268), kind=kLoop, calls=%fused_computation.19.clone.1 | loop fusion | bytes 6291460 | tf_op jit(solution)/shard_map/while/body/eval_jaxpr/dynamic_slice | solution.py:44
  102.0 1.1 constant_dynamic-slice_fusion.6
  103.1 1.0 copy.62
  104.1 11.5 %fusion.37 = (f32[4,512]{1,0:T(4,128)S(1)}, f32[4,512,1536]{2,1,0:T(8,128)}) fusion(pred[512,1536]{1,0:T(8,128)(4,1)S(1)} %and_and_fusion.2, bf16[512,4,128]{0,2,1:T(8,128)(2,1)} %bitcast.59, bf16[1536,4,128]{0,2,1:T(8,128)(2,1)} %bitcast.56), kind=kOutput, calls=%fused_computation.52.clone.1 | convolution fusion | flops 1629488640 | bytes 15474688 | tf_op jit(solution)/shard_map/while/body/eval_jaxpr/sub | solution.py:28
  115.6 8.5 %fusion.38 = f32[1,512,4,128]{1,3,2,0:T(8,128)} fusion(bf16[1536,4,128]{0,2,1:T(8,128)(2,1)} %bitcast.55, f32[4,512,1536]{2,1,0:T(8,128)} %get-tuple-element.237, f32[4,512]{1,0:T(4,128)S(1)} %get-tuple-element.238), kind=kOutput, calls=%fused_computation.13.clone.1 | convolution fusion | flops 811597824 | bytes 15212544 | tf_op jit(solution)/shard_map/while/body/eval_jaxpr/hqk,khd->qhd/dot_general | solution.py:62
  124.1 1.6 copy.63
  125.7 1.1 constant_dynamic-update-slice_fusion.2
  126.8 3.2 %copy.59 = f32[128,8,4,128]{3,1,2,0:T(8,128)} copy(f32[128,8,4,128]{3,2,1,0:T(4,128)} %bitcast.67) | data formatting | bytes 4194304
  130.0 116.1 %all-to-all-done.1.r0.r1.r2.r3 = bf16[64,2,64,512]{3,2,1,0:T(8,128)(2,1)} async-done(((bf16[64,2,64,512]{3,2,1,0:T(8,128)(2,1)}), bf16[64,2,64,512]{3,2,1,0:T(8,128)(2,1)}, u32[]{:S(2)}, u32[]{:S(2)}) %all-to-all-start.1) | async-done | bytes 8388640 | tf_op jit(solution)/shard_map/all_to_all | solution.py:199
  246.1 0.7 broadcast_in_dim.73
  246.7 0.7 broadcast_12_sh_ref.2.sh_ref
  247.4 10.1 %shard_map.82.rest_0_ = bf16[1024,512]{1,0:T(8,128)(2,1)} custom-call(s32[8]{0:T(128)} %get-tuple-element.117.order_ref, s32[32]{0:T(128)} %copy-done.7, s32[32]{0:T(128)} %get-tuple-element.179.flag_ref, bf16[1024,512]{1,0:T(8,128)(2,1)S(1)} %copy-done, bf16[64,2,64,512]{3,2,1,0:T(8,128)(2,1)} %all-to-all-done.1.r0.r1.r2.r3, ...), custom_call_target="tpu_custom_call" | custom-call | tf_op jit(solution)/shard_map/pallas_call | solution.py:156
  257.5 8.5 %all-reduce.2.cloned.1.call-done.sh_ref = bf16[2,64,512]{2,1,0:T(8,128)(2,1)} async-done(((bf16[2,64,512]{2,1,0:T(8,128)(2,1)}), bf16[2,64,512]{2,1,0:T(8,128)(2,1)}) %all-reduce.2.cloned.1.call-update) | async-done | bytes 131088 | tf_op jit(solution)/shard_map/psum | solution.py:200
  266.0 3.4 %shard_map.83 = bf16[1024,512]{1,0:T(8,128)(2,1)} custom-call(s32[8]{0:T(128)} %get-tuple-element.117.order_ref, s32[32]{0:T(128)} %copy-done.7, s32[32]{0:T(128)} %get-tuple-element.179.flag_ref, bf16[1024,512]{1,0:T(8,128)(2,1)S(1)} %copy-done, bf16[64,2,64,512]{3,2,1,0:T(8,128)(2,1)} %all-to-all-done.1.r0.r1.r2.r3, ...), custom_call_target="tpu_custom_call", output_to_operand_aliasing={{}: (11, {})} | custom-call | tf_op jit(solution)/shard_map/pallas_call | solution.py:156
  269.5 4.5 %all-to-all-start.2 = ((bf16[4,256,512]{2,1,0:T(8,128)(2,1)}), bf16[4,256,512]{2,1,0:T(8,128)(2,1)S(1)}, u32[]{:S(2)}, u32[]{:S(2)}) async-start(bf16[4,256,512]{2,1,0:T(8,128)(2,1)} %bitcast.60), calls=%async_computation.2 | async-start | bytes 2097152 | tf_op jit(solution)/shard_map/all_to_all | solution.py:223
  273.9 15.9 %all-to-all-done.2 = bf16[4,256,512]{2,1,0:T(8,128)(2,1)S(1)} async-done(((bf16[4,256,512]{2,1,0:T(8,128)(2,1)}), bf16[4,256,512]{2,1,0:T(8,128)(2,1)S(1)}, u32[]{:S(2)}, u32[]{:S(2)}) %all-to-all-start.2) | async-done | bytes 1048608 | tf_op jit(solution)/shard_map/all_to_all | solution.py:223
  289.8 6.9 %convert_reduce_fusion = bf16[256,2048]{1,0:T(8,128)(2,1)} fusion(bf16[4,256,512]{2,1,0:T(8,128)(2,1)S(1)} %all-to-all-done.2, bf16[4,512,2048]{2,1,0:T(8,128)(2,1)} %bitcast.70), kind=kOutput, calls=%fused_computation.24 | convolution fusion | flops 2151153664 | bytes 10485760 | tf_op jit(solution)/shard_map/gqf,gfn->gqn/dot_general | solution.py:226
  (23 shorter events, 0.1 us)
Async XLA Ops:
  7.4 1.6 copy-start.5
  9.5 1.7 copy-start.1
  9.5 3.6 %copy-start.6 = (s32[8,4]{0,1:T(4,128)S(1)}, s32[8,4]{0,1:T(4,128)}, u32[]{:S(2)}) copy-start(s32[8,4]{0,1:T(4,128)} %param.15) | copy-start | bytes 388
  11.2 42.5 %collective-permute-start = (bf16[2,1024,512]{1,2,0:T(8,128)(2,1)}, bf16[2,1024,512]{1,2,0:T(8,128)(2,1)}, u32[]{:S(2)}, u32[]{:S(2)}) collective-permute-start(bf16[2,1024,512]{1,2,0:T(8,128)(2,1)} %pad_maximum_fusion.1), channel_id=1, source_target_pairs={{0,4},{4,8},{8,12},{12,16},{16,20},{20,24},{24,28},{28,32},{32,36}... | collective-permute-start | bytes 6291464 | tf_op jit(solution)/shard_map/ppermute | solution.py:23
  13.3 15.9 %copy-start.7 = (s32[32]{0:T(128)}, s32[32]{0:T(128)S(1)}, u32[]{:S(2)}) copy-start(s32[32]{0:T(128)S(1)} %get-tuple-element.181.owner_ref) | copy-start | bytes 388
  14.6 32.2 %all-to-all-start = ((s32[64,1,1]{2,1,0:T(1,128)}), s32[64,1,1]{2,1,0:T(1,128)S(1)}, u32[]{:S(2)}, u32[]{:S(2)}) async-start(s32[64,1,1]{2,1,0:T(1,128)} %copy.47), calls=%async_computation | async-start | bytes 65536 | tf_op jit(solution)/shard_map/all_to_all | solution.py:196
  53.6 6.9 %copy-start.3 = (bf16[1024,512]{1,0:T(8,128)(2,1)S(1)}, bf16[1024,512]{1,0:T(8,128)(2,1)}, u32[]{:S(2)}) copy-start(bf16[1024,512]{1,0:T(8,128)(2,1)} %param.14) | copy-start | bytes 3145732
  53.6 6.9 %copy-start.4 = (bf16[1024,512]{1,0:T(8,128)(2,1)S(1)}, bf16[1024,512]{1,0:T(8,128)(2,1)}, u32[]{:S(2)}) copy-start(bf16[1024,512]{1,0:T(8,128)(2,1)} %param.13) | copy-start | bytes 3145732
  53.6 192.4 %all-to-all-start.1 = ((bf16[64,2,64,512]{3,2,1,0:T(8,128)(2,1)}), bf16[64,2,64,512]{3,2,1,0:T(8,128)(2,1)}, u32[]{:S(2)}, u32[]{:S(2)}) async-start(bf16[64,2,64,512]{3,2,1,0:T(8,128)(2,1)} %gather_fusion), calls=%async_computation.1 | async-start | bytes 16777216 | tf_op jit(solution)/shard_map/all_to_all | solution.py:199
  60.4 205.6 %all-reduce.2.cloned.1.call-start = ((), (), s32[]{:S(2)}) async-start(), calls=%async_computation.3 | async-start | bytes 262144 | tf_op jit(solution)/shard_map/psum | solution.py:200
  60.5 2.4 copy-start.8
  61.2 212.7 %all-gather.2.cloned.1.call-start = ((), (), s32[]{:S(2)}) async-start(), calls=%async_computation.4 | async-start | bytes 10485760 | tf_op jit(solution)/shard_map/all_gather | solution.py:178
  62.9 1.9 copy-start.2
  126.8 120.6 %copy-start = (bf16[1024,512]{1,0:T(8,128)(2,1)S(1)}, bf16[1024,512]{1,0:T(8,128)(2,1)}, u32[]{:S(2)}) copy-start(bf16[1024,512]{1,0:T(8,128)(2,1)} %get-tuple-element.282) | copy-start | bytes 3145732
  269.5 20.4 %all-to-all-start.2 = ((bf16[4,256,512]{2,1,0:T(8,128)(2,1)}), bf16[4,256,512]{2,1,0:T(8,128)(2,1)S(1)}, u32[]{:S(2)}, u32[]{:S(2)}) async-start(bf16[4,256,512]{2,1,0:T(8,128)(2,1)} %bitcast.60), calls=%async_computation.2 | async-start | bytes 2097152 | tf_op jit(solution)/shard_map/all_to_all | solution.py:223
Sparse Core Ops, SparseCore 0:
  64.7 201.2 all-reduce.1
Sparse Core Ops, SparseCore 1:
  63.5 86.7 all-gather.1

commit v6 on v5

--- a/solution.py
+++ b/solution.py
@@ -7,6 +7,7 @@
 from jax.experimental.pallas import tpu as pltpu
 from jax.sharding import PartitionSpec as P
 
+
 HDIM = 128
 WINDOW = 1024
 QBLK = 128
@@ -66,25 +67,6 @@
     return lax.map(per_tile, jnp.arange(tok_rows // tile_rows, dtype=jnp.int32)).reshape(
         tok_rows, heads_here, HDIM
     )
-
-
-def memory_attention(queries, fetched):
-    tok_rows, features = queries.shape
-    heads_here = features // HDIM
-    block_count = tok_rows // QBLK
-    score_scale = 1.0 / math.sqrt(HDIM)
-    query_blocks = queries.reshape(block_count, QBLK, heads_here, HDIM)
-    key_blocks = fetched[:, 0].reshape(block_count, TOPM * MROWS, heads_here, HDIM)
-    value_blocks = fetched[:, 1].reshape(block_count, TOPM * MROWS, heads_here, HDIM)
-    scores = (
-        jnp.einsum("bqhd,bkhd->bhqk", query_blocks, key_blocks, preferred_element_type=jnp.float32)
-        * score_scale
-    )
-    attend_weights = masked_softmax(scores, jnp.ones(scores.shape, dtype=bool))
-    remote = jnp.einsum(
-        "bhqk,bkhd->bqhd", attend_weights, value_blocks, preferred_element_type=jnp.float32
-    )
-    return remote.reshape(tok_rows, heads_here, HDIM)
 
 
 def mixed_memory_attention(queries, returned, shared, local_part, mixing_row, block_order, slot_owner, slot_shared, written, first, count):
@@ -169,7 +151,7 @@
     return jnp.sum(jnp.where(matches, offset[None, :] + 1, 0), axis=1) - 1
 
 
-def on_device(queries, keys, values, memory_keys, memory_values, block_ids, gate_bias, out_weight):
+def layer(queries, keys, values, memory_keys, memory_values, block_ids, gate_bias, out_weight):
     tok_rows, features = queries.shape
     owners = lax.axis_size("seq")
     groups = lax.axis_size("head")
@@ -198,8 +180,8 @@
     before, outgoing = lax.optimization_barrier((before, outgoing))
     returned = lax.all_to_all(outgoing, "seq", split_axis=0, concat_axis=0, tiled=True)
     shared = lax.psum(
-        jnp.where(seq_index == owners - 1, memory_store[mem_dev - 1], jnp.zeros_like(memory_store[0])),
-        "seq",
+      jnp.where(seq_index == owners - 1, memory_store[mem_dev - 1], jnp.zeros_like(memory_store[0])),
+      "seq",
     )
     local_part = window_attention(
         queries, jnp.concatenate([before[0], keys]), jnp.concatenate([before[1], values]), first_row
@@ -244,6 +226,4 @@
         P("head", None),
     )
     out_specs = P(("seq", "head"), None)
-    return jax.shard_map(
-        on_device, mesh=mesh, in_specs=in_specs, out_specs=out_specs, check_vma=False
-    )
+    return jax.shard_map(layer, mesh=mesh, in_specs=in_specs, out_specs=out_specs, check_vma=False)

time: 305 us -> 305 us (level)
  no operation moved by 1% of the time
where the time goes in v6:
time: 305 us; the launch traced here: 304 us
  waiting for transfers between devices  158 us (52%)
  matrix products  46.8 us (15%)
  local copies, waits for them, and re-layouts  32.4 us (11%)
  starting transfers between devices  26.2 us (9%)
  between operations  15 us (5%)
  Pallas kernels  13.6 us (4%)
  other arithmetic  10.2 us (3%)
    all_to_all x1, waiting for transfers between devices, layer(): lax.all_to_all(outgoing, 'seq', split_axis=0, concat_axis=0, tiled=True)  116 us
    sub x2, matrix products, masked_softmax(): weights = jnp.where(allowed, jnp.exp(scores - row_max), 0.0)  23 us
    all_to_all x1, waiting for transfers between devices, layer(): lax.all_to_all(slot_table, 'seq', split_axis=0, concat_axis=0, tiled=True)  17.7 us
    dot_general x2, matrix products, per_tile(): jnp.einsum('hqk,khd->qhd', attend_weights, value_tile, preferred_element_...  16.9 us
    all_to_all x1, waiting for transfers between devices, layer(): lax.all_to_all(attended.reshape(groups, out_rows, features), 'head', spli...  15.8 us
    pallas_call x2, Pallas kernels, mixed_memory_attention(): pl.pallas_call(kernel, grid_spec=grid_spec, out_shape=jax.ShapeDtypeStruc...  13.6 us
    all_to_all x1, starting transfers between devices, layer(): lax.all_to_all(slot_table, 'seq', split_axis=0, concat_axis=0, tiled=True)  12.7 us
    psum x1, waiting for transfers between devices, layer(): lax.psum(jnp.where(seq_index == owners - 1, memory_store[mem_dev - 1], jn...  8.51 us
  transfers between devices with their start and end apart: 6, of which 4 were waited for; matrix products, arithmetic and copies ran while one was open for 26% of the time, Pallas kernels for 4%

profile of v6, /device:TPU:2, one launch (start us, length us, event | category | flops | bytes accessed | tf_op | source)
XLA Modules:
  0.0 304.1 jit_solution(16989268354619205127)
XLA Ops:
  7.4 1.6 copy.45
  8.9 0.0 copy-done.5
  9.0 0.5 copy.46
  9.5 0.0 copy-start.1
  9.5 0.0 copy-start.6
  9.5 1.6 pad_maximum_fusion.1
  11.2 0.0 copy-done.1
  11.2 1.9 collective-permute-start
  13.1 0.0 copy-done.6
  13.1 0.1 copy.44
  13.2 0.1 reshape.210
  13.3 0.0 copy-start.7
  13.3 0.5 compare_not_fusion
  13.8 0.1 select_reduce_fusion.1
  13.9 0.7 copy.47
  14.6 12.7 %all-to-all-start = ((s32[64,1,1]{2,1,0:T(1,128)}), s32[64,1,1]{2,1,0:T(1,128)S(1)}, u32[]{:S(2)}, u32[]{:S(2)}) async-start(s32[64,1,1]{2,1,0:T(1,128)} %copy.47), calls=%async_computation | async-start | bytes 65536 | tf_op jit(solution)/shard_map/all_to_all | solution.py:178
  27.4 1.7 pad_maximum_fusion
  29.1 0.0 copy-done.7
  29.1 17.7 %all-to-all-done = s32[64,1,1]{2,1,0:T(1,128)S(1)} async-done(((s32[64,1,1]{2,1,0:T(1,128)}), s32[64,1,1]{2,1,0:T(1,128)S(1)}, u32[]{:S(2)}, u32[]{:S(2)}) %all-to-all-start) | async-done | bytes 288 | tf_op jit(solution)/shard_map/all_to_all | solution.py:178
  46.9 1.2 maximum_reduce_fusion
  48.1 5.5 %gather_fusion = bf16[64,2,64,512]{3,2,1,0:T(8,128)(2,1)} fusion(bf16[16,2,64,512]{3,2,1,0:T(8,128)(2,1)S(1)} %pad_maximum_fusion, s32[1024]{0:T(1024)S(1)} %pad_clamp_fusion), kind=kCustom, calls=%fused_computation | custom fusion | bytes 16777472 | tf_op jit(solution)/shard_map/gather | solution.py:179
  53.6 0.0 collective-permute-done
  53.6 6.8 %all-to-all-start.1 = ((bf16[64,2,64,512]{3,2,1,0:T(8,128)(2,1)}), bf16[64,2,64,512]{3,2,1,0:T(8,128)(2,1)}, u32[]{:S(2)}, u32[]{:S(2)}) async-start(bf16[64,2,64,512]{3,2,1,0:T(8,128)(2,1)} %gather_fusion), calls=%async_computation.1 | async-start | bytes 16777216 | tf_op jit(solution)/shard_map/all_to_all | solution.py:181
  60.4 0.0 all-reduce.2.cloned.1.call-start
  60.5 0.0 copy-start.8
  60.5 0.7 select_bitcast_fusion
  61.2 0.0 all-reduce.2.cloned.1.call-update
  61.2 0.2 all-gather.2.cloned.1.call-start
  61.4 0.3 all-gather.2.cloned.1.call-update
  61.8 1.0 sort.17
  62.9 0.0 copy-start.2
  62.9 1.8 slice_bitcast_fusion
  64.7 0.0 copy-done.2
  64.8 1.7 pad_maximum_fusion.2
  66.4 60.4 %while.13 = (s32[]{:T(128)}, f32[2,512,4,128]{3,2,1,0:T(4,128)}, s32[2]{0:T(128)S(1)}, bf16[2048,512]{0,1:T(8,128)(2,1)S(1)}, s32[]{:T(128)}, /*index=5*/bf16[10...) while((s32[]{:T(128)}, f32[2,512,4,128]{3,2,1,0:T(4,128)}, ...), condition=%wide.region_7.8_spmd, body=%wide.region_4.7_spmd.sunk | while | flops 2444237824 | bytes 44080892 | solution.py:67
  66.4 0.6 dynamic_slice.37
  67.7 0.8 and_and_fusion.2
  68.5 3.3 %constant_dynamic-slice_fusion.5 = (bf16[1536,512]{0,1:T(8,128)(2,1)}, bf16[1536,512]{0,1:T(8,128)(2,1)}) fusion(bf16[2048,512]{0,1:T(8,128)(2,1)} %get-tuple-element.271, s32[]{:T(128)S(6)} %select_n.87, bf16[2048,512]{0,1:T(8,128)(2,1)S(1)} %get-tuple-element.268), kind=kLoop, calls=%fused_computation.19.clone.1 | loop fusion | bytes 6291460 | tf_op jit(solution)/shard_map/while/body/eval_jaxpr/dynamic_slice | solution.py:45
  71.8 1.1 constant_dynamic-slice_fusion.6
  72.9 1.0 copy.62
  73.9 11.5 %fusion.37 = (f32[4,512]{1,0:T(4,128)S(1)}, f32[4,512,1536]{2,1,0:T(8,128)}) fusion(pred[512,1536]{1,0:T(8,128)(4,1)S(1)} %and_and_fusion.2, bf16[512,4,128]{0,2,1:T(8,128)(2,1)} %bitcast.59, bf16[1536,4,128]{0,2,1:T(8,128)(2,1)} %bitcast.56), kind=kOutput, calls=%fused_computation.52.clone.1 | convolution fusion | flops 1629488640 | bytes 15474688 | tf_op jit(solution)/shard_map/while/body/eval_jaxpr/sub | solution.py:29
  85.4 8.4 %fusion.38 = f32[1,512,4,128]{1,3,2,0:T(8,128)} fusion(bf16[1536,4,128]{0,2,1:T(8,128)(2,1)} %bitcast.55, f32[4,512,1536]{2,1,0:T(8,128)} %get-tuple-element.237, f32[4,512]{1,0:T(4,128)S(1)} %get-tuple-element.238), kind=kOutput, calls=%fused_computation.13.clone.1 | convolution fusion | flops 811597824 | bytes 15212544 | tf_op jit(solution)/shard_map/while/body/eval_jaxpr/hqk,khd->qhd/dot_general | solution.py:63
  93.8 1.6 copy.63
  95.4 1.1 constant_dynamic-update-slice_fusion.2
  96.5 0.6 dynamic_slice.37
  97.8 0.8 and_and_fusion.2
  98.6 3.4 %constant_dynamic-slice_fusion.5 = (bf16[1536,512]{0,1:T(8,128)(2,1)}, bf16[1536,512]{0,1:T(8,128)(2,1)}) fusion(bf16[2048,512]{0,1:T(8,128)(2,1)} %get-tuple-element.271, s32[]{:T(128)S(6)} %select_n.87, bf16[2048,512]{0,1:T(8,128)(2,1)S(1)} %get-tuple-element.268), kind=kLoop, calls=%fused_computation.19.clone.1 | loop fusion | bytes 6291460 | tf_op jit(solution)/shard_map/while/body/eval_jaxpr/dynamic_slice | solution.py:45
  102.0 1.1 constant_dynamic-slice_fusion.6
  103.1 1.0 copy.62
  104.1 11.5 %fusion.37 = (f32[4,512]{1,0:T(4,128)S(1)}, f32[4,512,1536]{2,1,0:T(8,128)}) fusion(pred[512,1536]{1,0:T(8,128)(4,1)S(1)} %and_and_fusion.2, bf16[512,4,128]{0,2,1:T(8,128)(2,1)} %bitcast.59, bf16[1536,4,128]{0,2,1:T(8,128)(2,1)} %bitcast.56), kind=kOutput, calls=%fused_computation.52.clone.1 | convolution fusion | flops 1629488640 | bytes 15474688 | tf_op jit(solution)/shard_map/while/body/eval_jaxpr/sub | solution.py:29
  115.6 8.5 %fusion.38 = f32[1,512,4,128]{1,3,2,0:T(8,128)} fusion(bf16[1536,4,128]{0,2,1:T(8,128)(2,1)} %bitcast.55, f32[4,512,1536]{2,1,0:T(8,128)} %get-tuple-element.237, f32[4,512]{1,0:T(4,128)S(1)} %get-tuple-element.238), kind=kOutput, calls=%fused_computation.13.clone.1 | convolution fusion | flops 811597824 | bytes 15212544 | tf_op jit(solution)/shard_map/while/body/eval_jaxpr/hqk,khd->qhd/dot_general | solution.py:63
  124.1 1.6 copy.63
  125.7 1.1 constant_dynamic-update-slice_fusion.2
  126.8 3.2 %copy.59 = f32[128,8,4,128]{3,1,2,0:T(8,128)} copy(f32[128,8,4,128]{3,2,1,0:T(4,128)} %bitcast.67) | data formatting | bytes 4194304
  130.0 116.1 %all-to-all-done.1.r0.r1.r2.r3 = bf16[64,2,64,512]{3,2,1,0:T(8,128)(2,1)} async-done(((bf16[64,2,64,512]{3,2,1,0:T(8,128)(2,1)}), bf16[64,2,64,512]{3,2,1,0:T(8,128)(2,1)}, u32[]{:S(2)}, u32[]{:S(2)}) %all-to-all-start.1) | async-done | bytes 8388640 | tf_op jit(solution)/shard_map/all_to_all | solution.py:181
  246.1 0.7 broadcast_in_dim.73
  246.7 0.7 broadcast_12_sh_ref.2.sh_ref
  247.4 0.0 copy-done
  247.4 10.1 %shard_map.82.rest_0_ = bf16[1024,512]{1,0:T(8,128)(2,1)} custom-call(s32[8]{0:T(128)} %get-tuple-element.117.order_ref, s32[32]{0:T(128)} %copy-done.7, s32[32]{0:T(128)} %get-tuple-element.179.flag_ref, bf16[1024,512]{1,0:T(8,128)(2,1)S(1)} %copy-done, bf16[64,2,64,512]{3,2,1,0:T(8,128)(2,1)} %all-to-all-done.1.r0.r1.r2.r3, ...), custom_call_target="tpu_custom_call" | custom-call | tf_op jit(solution)/shard_map/pallas_call | solution.py:138
  257.5 8.5 %all-reduce.2.cloned.1.call-done.sh_ref = bf16[2,64,512]{2,1,0:T(8,128)(2,1)} async-done(((bf16[2,64,512]{2,1,0:T(8,128)(2,1)}), bf16[2,64,512]{2,1,0:T(8,128)(2,1)}) %all-reduce.2.cloned.1.call-update) | async-done | bytes 131088 | tf_op jit(solution)/shard_map/psum | solution.py:182
  266.0 3.4 %shard_map.83 = bf16[1024,512]{1,0:T(8,128)(2,1)} custom-call(s32[8]{0:T(128)} %get-tuple-element.117.order_ref, s32[32]{0:T(128)} %copy-done.7, s32[32]{0:T(128)} %get-tuple-element.179.flag_ref, bf16[1024,512]{1,0:T(8,128)(2,1)S(1)} %copy-done, bf16[64,2,64,512]{3,2,1,0:T(8,128)(2,1)} %all-to-all-done.1.r0.r1.r2.r3, ...), custom_call_target="tpu_custom_call", output_to_operand_aliasing={{}: (11, {})} | custom-call | tf_op jit(solution)/shard_map/pallas_call | solution.py:138
  269.4 4.5 %all-to-all-start.2 = ((bf16[4,256,512]{2,1,0:T(8,128)(2,1)}), bf16[4,256,512]{2,1,0:T(8,128)(2,1)S(1)}, u32[]{:S(2)}, u32[]{:S(2)}) async-start(bf16[4,256,512]{2,1,0:T(8,128)(2,1)} %bitcast.60), calls=%async_computation.2 | async-start | bytes 2097152 | tf_op jit(solution)/shard_map/all_to_all | solution.py:205
  273.9 15.8 %all-to-all-done.2 = bf16[4,256,512]{2,1,0:T(8,128)(2,1)S(1)} async-done(((bf16[4,256,512]{2,1,0:T(8,128)(2,1)}), bf16[4,256,512]{2,1,0:T(8,128)(2,1)S(1)}, u32[]{:S(2)}, u32[]{:S(2)}) %all-to-all-start.2) | async-done | bytes 1048608 | tf_op jit(solution)/shard_map/all_to_all | solution.py:205
  289.8 6.9 %convert_reduce_fusion = bf16[256,2048]{1,0:T(8,128)(2,1)} fusion(bf16[4,256,512]{2,1,0:T(8,128)(2,1)S(1)} %all-to-all-done.2, bf16[4,512,2048]{2,1,0:T(8,128)(2,1)} %bitcast.70), kind=kOutput, calls=%fused_computation.24 | convolution fusion | flops 2151153664 | bytes 10485760 | tf_op jit(solution)/shard_map/gqf,gfn->gqn/dot_general | solution.py:208
  (23 shorter events, 0.1 us)
Async XLA Ops:
  7.4 1.6 copy-start.5
  9.5 1.7 copy-start.1
  9.5 3.6 %copy-start.6 = (s32[8,4]{0,1:T(4,128)S(1)}, s32[8,4]{0,1:T(4,128)}, u32[]{:S(2)}) copy-start(s32[8,4]{0,1:T(4,128)} %param.15) | copy-start | bytes 388
  11.2 42.5 %collective-permute-start = (bf16[2,1024,512]{1,2,0:T(8,128)(2,1)}, bf16[2,1024,512]{1,2,0:T(8,128)(2,1)}, u32[]{:S(2)}, u32[]{:S(2)}) collective-permute-start(bf16[2,1024,512]{1,2,0:T(8,128)(2,1)} %pad_maximum_fusion.1), channel_id=1, source_target_pairs={{0,4},{4,8},{8,12},{12,16},{16,20},{20,24},{24,28},{28,32},{32,36}... | collective-permute-start | bytes 6291464 | tf_op jit(solution)/shard_map/ppermute | solution.py:24
  13.3 15.9 %copy-start.7 = (s32[32]{0:T(128)}, s32[32]{0:T(128)S(1)}, u32[]{:S(2)}) copy-start(s32[32]{0:T(128)S(1)} %get-tuple-element.181.owner_ref) | copy-start | bytes 388
  14.6 32.2 %all-to-all-start = ((s32[64,1,1]{2,1,0:T(1,128)}), s32[64,1,1]{2,1,0:T(1,128)S(1)}, u32[]{:S(2)}, u32[]{:S(2)}) async-start(s32[64,1,1]{2,1,0:T(1,128)} %copy.47), calls=%async_computation | async-start | bytes 65536 | tf_op jit(solution)/shard_map/all_to_all | solution.py:178
  53.6 6.9 %copy-start.3 = (bf16[1024,512]{1,0:T(8,128)(2,1)S(1)}, bf16[1024,512]{1,0:T(8,128)(2,1)}, u32[]{:S(2)}) copy-start(bf16[1024,512]{1,0:T(8,128)(2,1)} %param.14) | copy-start | bytes 3145732
  53.6 6.9 %copy-start.4 = (bf16[1024,512]{1,0:T(8,128)(2,1)S(1)}, bf16[1024,512]{1,0:T(8,128)(2,1)}, u32[]{:S(2)}) copy-start(bf16[1024,512]{1,0:T(8,128)(2,1)} %param.13) | copy-start | bytes 3145732
  53.6 192.4 %all-to-all-start.1 = ((bf16[64,2,64,512]{3,2,1,0:T(8,128)(2,1)}), bf16[64,2,64,512]{3,2,1,0:T(8,128)(2,1)}, u32[]{:S(2)}, u32[]{:S(2)}) async-start(bf16[64,2,64,512]{3,2,1,0:T(8,128)(2,1)} %gather_fusion), calls=%async_computation.1 | async-start | bytes 16777216 | tf_op jit(solution)/shard_map/all_to_all | solution.py:181
  60.4 205.6 %all-reduce.2.cloned.1.call-start = ((), (), s32[]{:S(2)}) async-start(), calls=%async_computation.3 | async-start | bytes 262144 | tf_op jit(solution)/shard_map/psum | solution.py:182
  60.5 2.4 copy-start.8
  61.2 212.7 %all-gather.2.cloned.1.call-start = ((), (), s32[]{:S(2)}) async-start(), calls=%async_computation.4 | async-start | bytes 10485760 | tf_op jit(solution)/shard_map/all_gather | solution.py:160
  62.9 1.9 copy-start.2
  126.8 120.6 %copy-start = (bf16[1024,512]{1,0:T(8,128)(2,1)S(1)}, bf16[1024,512]{1,0:T(8,128)(2,1)}, u32[]{:S(2)}) copy-start(bf16[1024,512]{1,0:T(8,128)(2,1)} %get-tuple-element.282) | copy-start | bytes 3145732
  269.4 20.3 %all-to-all-start.2 = ((bf16[4,256,512]{2,1,0:T(8,128)(2,1)}), bf16[4,256,512]{2,1,0:T(8,128)(2,1)S(1)}, u32[]{:S(2)}, u32[]{:S(2)}) async-start(bf16[4,256,512]{2,1,0:T(8,128)(2,1)} %bitcast.60), calls=%async_computation.2 | async-start | bytes 2097152 | tf_op jit(solution)/shard_map/all_to_all | solution.py:205
Sparse Core Ops, SparseCore 0:
  64.7 201.2 all-reduce.1
Sparse Core Ops, SparseCore 1:
  63.5 86.7 all-gather.1

commit v7 on v6

--- a/solution.py
+++ b/solution.py
@@ -188,18 +188,10 @@
     )
     mixing_row = jnp.repeat(jax.nn.sigmoid(gate_bias), HDIM)[None, :]
     block_count = tok_rows // QBLK
-    uses_shared = jnp.any(is_last.reshape(block_count, TOPM), axis=1)
-    block_order = jnp.argsort(uses_shared.astype(jnp.int32), stable=True).astype(jnp.int32)
-    flags = is_last.astype(jnp.int32)
-    local_rows = local_part.reshape(tok_rows, features)
-    no_shared = jnp.zeros_like(shared)
+    block_order = jnp.arange(block_count, dtype=jnp.int32)
     attended = mixed_memory_attention(
-        queries, returned, no_shared, local_rows, mixing_row, block_order, owner_index, flags,
-        None, 0, block_count - 1,
-    )
-    attended = mixed_memory_attention(
-        queries, returned, shared, local_rows, mixing_row, block_order, owner_index, flags,
-        attended, block_count - 1, 1,
+        queries, returned, shared, local_part.reshape(tok_rows, features), mixing_row, block_order,
+        owner_index, is_last.astype(jnp.int32), None, 0, block_count,
     )
     out_rows = tok_rows // groups
     gathered = lax.all_to_all(

time: 305 us -> 314 us (1.030)
  waiting for transfers between devices: 158 us -> 171 us
    psum x1, waiting for transfers between devices: 8.51 us -> 137 us  [layer(): lax.psum(jnp.where(seq_index == owners - 1, memory_store[mem_dev - 1], jn...]
    all_to_all x1, waiting for transfers between devices: 116 us -> 0.01 us  [layer(): lax.all_to_all(outgoing, 'seq', split_axis=0, concat_axis=0, tiled=True)]
    pallas_call x2 -> x1, Pallas kernels: 13.6 us -> 11.1 us  [mixed_memory_attention(): pl.pallas_call(kernel, grid_spec=grid_spec, out_shape=jax.ShapeDtypeStruc...]
  transfers between devices with their start and end apart: 6 -> 6, of which waited for: 4 -> 3; matrix products, arithmetic and copies ran while one was open for 26% -> 25% of each run, Pallas kernels for 4% -> 4%
where the time goes in v7:
time: 314 us; the launch traced here: 313 us
  waiting for transfers between devices  171 us (54%)
  matrix products  46.7 us (15%)
  local copies, waits for them, and re-layouts  32.2 us (10%)
  starting transfers between devices  26.2 us (8%)
  between operations  15 us (5%)
  Pallas kernels  11.1 us (4%)
  other arithmetic  9.24 us (3%)
    psum x1, waiting for transfers between devices, layer(): lax.psum(jnp.where(seq_index == owners - 1, memory_store[mem_dev - 1], jn...  137 us
    sub x2, matrix products, masked_softmax(): weights = jnp.where(allowed, jnp.exp(scores - row_max), 0.0)  23 us
    all_to_all x1, waiting for transfers between devices, layer(): lax.all_to_all(slot_table, 'seq', split_axis=0, concat_axis=0, tiled=True)  17.7 us
    dot_general x2, matrix products, per_tile(): jnp.einsum('hqk,khd->qhd', attend_weights, value_tile, preferred_element_...  16.8 us
    all_to_all x1, waiting for transfers between devices, layer(): lax.all_to_all(attended.reshape(groups, out_rows, features), 'head', spli...  16 us
    all_to_all x1, starting transfers between devices, layer(): lax.all_to_all(slot_table, 'seq', split_axis=0, concat_axis=0, tiled=True)  12.7 us
    pallas_call x1, Pallas kernels, mixed_memory_attention(): pl.pallas_call(kernel, grid_spec=grid_spec, out_shape=jax.ShapeDtypeStruc...  11.1 us
    dot_general x1, matrix products, layer(): jnp.einsum('gqf,gfn->gqn', gathered, full_weight.reshape(groups, features...  6.92 us
  transfers between devices with their start and end apart: 6, of which 3 were waited for; matrix products, arithmetic and copies ran while one was open for 25% of the time, Pallas kernels for 4%

profile of v7, /device:TPU:2, one launch (start us, length us, event | category | flops | bytes accessed | tf_op | source)
XLA Modules:
  0.0 313.1 jit_solution(7322521721803911010)
XLA Ops:
  7.4 1.6 copy.44
  8.9 0.0 copy-done.5
  9.0 0.5 copy.45
  9.5 0.0 copy-start.1
  9.5 0.0 copy-start.7
  9.5 1.6 pad_maximum_fusion.1
  11.2 0.0 copy-done.1
  11.2 1.9 collective-permute-start
  13.1 0.0 copy-done.7
  13.1 0.1 copy.43
  13.2 0.1 reshape.209
  13.3 0.0 copy-start.6
  13.3 0.6 compare_not_fusion
  13.9 0.1 select_reduce_fusion.1
  14.0 0.7 copy.46
  14.7 12.7 %all-to-all-start = ((s32[64,1,1]{2,1,0:T(1,128)}), s32[64,1,1]{2,1,0:T(1,128)S(1)}, u32[]{:S(2)}, u32[]{:S(2)}) async-start(s32[64,1,1]{2,1,0:T(1,128)} %copy.46), calls=%async_computation | async-start | bytes 65536 | tf_op jit(solution)/shard_map/all_to_all | solution.py:178
  27.5 1.7 pad_maximum_fusion
  29.2 0.0 copy-done.6
  29.2 17.7 %all-to-all-done = s32[64,1,1]{2,1,0:T(1,128)S(1)} async-done(((s32[64,1,1]{2,1,0:T(1,128)}), s32[64,1,1]{2,1,0:T(1,128)S(1)}, u32[]{:S(2)}, u32[]{:S(2)}) %all-to-all-start) | async-done | bytes 288 | tf_op jit(solution)/shard_map/all_to_all | solution.py:178
  46.9 1.2 maximum_reduce_fusion
  48.1 5.6 %gather_fusion = bf16[64,2,64,512]{3,2,1,0:T(8,128)(2,1)} fusion(bf16[16,2,64,512]{3,2,1,0:T(8,128)(2,1)S(1)} %pad_maximum_fusion, s32[1024]{0:T(1024)S(1)} %pad_clamp_fusion), kind=kCustom, calls=%fused_computation | custom fusion | bytes 16777472 | tf_op jit(solution)/shard_map/gather | solution.py:179
  53.7 0.0 collective-permute-done
  53.7 6.8 %all-to-all-start.1 = ((bf16[64,2,64,512]{3,2,1,0:T(8,128)(2,1)}), bf16[64,2,64,512]{3,2,1,0:T(8,128)(2,1)}, u32[]{:S(2)}, u32[]{:S(2)}) async-start(bf16[64,2,64,512]{3,2,1,0:T(8,128)(2,1)} %gather_fusion), calls=%async_computation.1 | async-start | bytes 16777216 | tf_op jit(solution)/shard_map/all_to_all | solution.py:181
  60.5 0.0 all-reduce.2.cloned.1.call-start
  60.5 0.0 copy-done.3
  60.5 0.0 copy-done.4
  60.6 0.0 copy-start.8
  60.6 0.7 select_bitcast_fusion
  61.2 0.0 all-reduce.2.cloned.1.call-update
  61.3 0.2 all-gather.2.cloned.1.call-start
  61.5 0.3 all-gather.2.cloned.1.call-update
  61.9 0.0 copy-start.2
  61.9 1.8 slice_bitcast_fusion
  63.7 0.0 copy-done.2
  63.7 1.6 pad_maximum_fusion.2
  65.4 60.2 %while.13 = (s32[]{:T(128)}, f32[2,512,4,128]{3,2,1,0:T(4,128)}, s32[2]{0:T(128)S(1)}, bf16[2048,512]{0,1:T(8,128)(2,1)S(1)}, s32[]{:T(128)}, /*index=5*/bf16[10...) while((s32[]{:T(128)}, f32[2,512,4,128]{3,2,1,0:T(4,128)}, ...), condition=%wide.region_5.6_spmd, body=%wide.region_2.5_spmd.sunk | while | flops 2444237824 | bytes 44080892 | solution.py:67
  65.4 0.6 dynamic_slice.37
  66.7 0.8 and_and_fusion.2
  67.5 3.3 %constant_dynamic-slice_fusion.5 = (bf16[1536,512]{0,1:T(8,128)(2,1)}, bf16[1536,512]{0,1:T(8,128)(2,1)}) fusion(bf16[2048,512]{0,1:T(8,128)(2,1)} %get-tuple-element.269, s32[]{:T(128)S(6)} %select_n.87, bf16[2048,512]{0,1:T(8,128)(2,1)S(1)} %get-tuple-element.266), kind=kLoop, calls=%fused_computation.19.clone.1 | loop fusion | bytes 6291460 | tf_op jit(solution)/shard_map/while/body/eval_jaxpr/dynamic_slice | solution.py:45
  70.8 1.1 constant_dynamic-slice_fusion.6
  71.9 1.0 copy.61
  72.9 11.5 %fusion.37 = (f32[4,512]{1,0:T(4,128)S(1)}, f32[4,512,1536]{2,1,0:T(8,128)}) fusion(pred[512,1536]{1,0:T(8,128)(4,1)S(1)} %and_and_fusion.2, bf16[512,4,128]{0,2,1:T(8,128)(2,1)} %bitcast.57, bf16[1536,4,128]{0,2,1:T(8,128)(2,1)} %bitcast.56), kind=kOutput, calls=%fused_computation.51.clone.1 | convolution fusion | flops 1629488640 | bytes 15474688 | tf_op jit(solution)/shard_map/while/body/eval_jaxpr/sub | solution.py:29
  84.4 8.4 %fusion.38 = f32[1,512,4,128]{1,3,2,0:T(8,128)} fusion(bf16[1536,4,128]{0,2,1:T(8,128)(2,1)} %bitcast.55, f32[4,512,1536]{2,1,0:T(8,128)} %get-tuple-element.235, f32[4,512]{1,0:T(4,128)S(1)} %get-tuple-element.236), kind=kOutput, calls=%fused_computation.13.clone.1 | convolution fusion | flops 811597824 | bytes 15212544 | tf_op jit(solution)/shard_map/while/body/eval_jaxpr/hqk,khd->qhd/dot_general | solution.py:63
  92.7 1.6 copy.62
  94.3 1.1 constant_dynamic-update-slice_fusion.2
  95.4 0.6 dynamic_slice.37
  96.7 0.8 and_and_fusion.2
  97.5 3.3 %constant_dynamic-slice_fusion.5 = (bf16[1536,512]{0,1:T(8,128)(2,1)}, bf16[1536,512]{0,1:T(8,128)(2,1)}) fusion(bf16[2048,512]{0,1:T(8,128)(2,1)} %get-tuple-element.269, s32[]{:T(128)S(6)} %select_n.87, bf16[2048,512]{0,1:T(8,128)(2,1)S(1)} %get-tuple-element.266), kind=kLoop, calls=%fused_computation.19.clone.1 | loop fusion | bytes 6291460 | tf_op jit(solution)/shard_map/while/body/eval_jaxpr/dynamic_slice | solution.py:45
  100.8 1.1 constant_dynamic-slice_fusion.6
  101.9 1.0 copy.61
  102.9 11.5 %fusion.37 = (f32[4,512]{1,0:T(4,128)S(1)}, f32[4,512,1536]{2,1,0:T(8,128)}) fusion(pred[512,1536]{1,0:T(8,128)(4,1)S(1)} %and_and_fusion.2, bf16[512,4,128]{0,2,1:T(8,128)(2,1)} %bitcast.57, bf16[1536,4,128]{0,2,1:T(8,128)(2,1)} %bitcast.56), kind=kOutput, calls=%fused_computation.51.clone.1 | convolution fusion | flops 1629488640 | bytes 15474688 | tf_op jit(solution)/shard_map/while/body/eval_jaxpr/sub | solution.py:29
  114.4 8.4 %fusion.38 = f32[1,512,4,128]{1,3,2,0:T(8,128)} fusion(bf16[1536,4,128]{0,2,1:T(8,128)(2,1)} %bitcast.55, f32[4,512,1536]{2,1,0:T(8,128)} %get-tuple-element.235, f32[4,512]{1,0:T(4,128)S(1)} %get-tuple-element.236), kind=kOutput, calls=%fused_computation.13.clone.1 | convolution fusion | flops 811597824 | bytes 15212544 | tf_op jit(solution)/shard_map/while/body/eval_jaxpr/hqk,khd->qhd/dot_general | solution.py:63
  122.9 1.6 copy.62
  124.5 1.1 constant_dynamic-update-slice_fusion.2
  125.6 3.2 %copy.58 = f32[128,8,4,128]{3,1,2,0:T(8,128)} copy(f32[128,8,4,128]{3,2,1,0:T(4,128)} %bitcast.66) | data formatting | bytes 4194304
  128.8 137.2 %all-reduce.2.cloned.1.call-done.sh_ref = bf16[2,64,512]{2,1,0:T(8,128)(2,1)} async-done(((bf16[2,64,512]{2,1,0:T(8,128)(2,1)}), bf16[2,64,512]{2,1,0:T(8,128)(2,1)}) %all-reduce.2.cloned.1.call-update) | async-done | bytes 131088 | tf_op jit(solution)/shard_map/psum | solution.py:182
  265.9 0.0 all-to-all-done.1.r0.r1.r2.r3
  265.9 0.7 broadcast_in_dim.77
  266.6 0.5 iota.38.order_ref
  267.1 0.0 copy-done
  267.1 11.1 %shard_map.82 = bf16[1024,512]{1,0:T(8,128)(2,1)} custom-call(s32[8]{0:T(128)} %iota.38.order_ref, s32[32]{0:T(128)} %copy-done.6, s32[32]{0:T(128)} %get-tuple-element.177.flag_ref, bf16[1024,512]{1,0:T(8,128)(2,1)S(1)} %copy-done, bf16[64,2,64,512]{3,2,1,0:T(8,128)(2,1)} %all-to-all-done.1.r0.r1.r2.r3, ...), custom_call_target="tpu_custom_call" | custom-call | tf_op jit(solution)/shard_map/pallas_call | solution.py:138
  278.3 4.5 %all-to-all-start.2 = ((bf16[4,256,512]{2,1,0:T(8,128)(2,1)}), bf16[4,256,512]{2,1,0:T(8,128)(2,1)S(1)}, u32[]{:S(2)}, u32[]{:S(2)}) async-start(bf16[4,256,512]{2,1,0:T(8,128)(2,1)} %bitcast.61), calls=%async_computation.2 | async-start | bytes 2097152 | tf_op jit(solution)/shard_map/all_to_all | solution.py:197
  282.7 16.0 %all-to-all-done.2 = bf16[4,256,512]{2,1,0:T(8,128)(2,1)S(1)} async-done(((bf16[4,256,512]{2,1,0:T(8,128)(2,1)}), bf16[4,256,512]{2,1,0:T(8,128)(2,1)S(1)}, u32[]{:S(2)}, u32[]{:S(2)}) %all-to-all-start.2) | async-done | bytes 1048608 | tf_op jit(solution)/shard_map/all_to_all | solution.py:197
  298.7 6.9 %convert_reduce_fusion = bf16[256,2048]{1,0:T(8,128)(2,1)} fusion(bf16[4,256,512]{2,1,0:T(8,128)(2,1)S(1)} %all-to-all-done.2, bf16[4,512,2048]{2,1,0:T(8,128)(2,1)} %bitcast.68), kind=kOutput, calls=%fused_computation.24 | convolution fusion | flops 2151153664 | bytes 10485760 | tf_op jit(solution)/shard_map/gqf,gfn->gqn/dot_general | solution.py:200
  (18 shorter events, 0.1 us)
Async XLA Ops:
  7.4 1.6 copy-start.5
  9.5 1.7 copy-start.1
  9.5 3.6 %copy-start.7 = (s32[8,4]{0,1:T(4,128)S(1)}, s32[8,4]{0,1:T(4,128)}, u32[]{:S(2)}) copy-start(s32[8,4]{0,1:T(4,128)} %param.15) | copy-start | bytes 388
  11.2 42.5 %collective-permute-start = (bf16[2,1024,512]{1,2,0:T(8,128)(2,1)}, bf16[2,1024,512]{1,2,0:T(8,128)(2,1)}, u32[]{:S(2)}, u32[]{:S(2)}) collective-permute-start(bf16[2,1024,512]{1,2,0:T(8,128)(2,1)} %pad_maximum_fusion.1), channel_id=1, source_target_pairs={{0,4},{4,8},{8,12},{12,16},{16,20},{20,24},{24,28},{28,32},{32,36}... | collective-permute-start | bytes 6291464 | tf_op jit(solution)/shard_map/ppermute | solution.py:24
  13.3 15.9 %copy-start.6 = (s32[32]{0:T(128)}, s32[32]{0:T(128)S(1)}, u32[]{:S(2)}) copy-start(s32[32]{0:T(128)S(1)} %get-tuple-element.179.owner_ref) | copy-start | bytes 388
  14.7 32.2 %all-to-all-start = ((s32[64,1,1]{2,1,0:T(1,128)}), s32[64,1,1]{2,1,0:T(1,128)S(1)}, u32[]{:S(2)}, u32[]{:S(2)}) async-start(s32[64,1,1]{2,1,0:T(1,128)} %copy.46), calls=%async_computation | async-start | bytes 65536 | tf_op jit(solution)/shard_map/all_to_all | solution.py:178
  53.7 6.9 %copy-start.3 = (bf16[1024,512]{1,0:T(8,128)(2,1)S(1)}, bf16[1024,512]{1,0:T(8,128)(2,1)}, u32[]{:S(2)}) copy-start(bf16[1024,512]{1,0:T(8,128)(2,1)} %param.14) | copy-start | bytes 3145732
  53.7 6.9 %copy-start.4 = (bf16[1024,512]{1,0:T(8,128)(2,1)S(1)}, bf16[1024,512]{1,0:T(8,128)(2,1)}, u32[]{:S(2)}) copy-start(bf16[1024,512]{1,0:T(8,128)(2,1)} %param.13) | copy-start | bytes 3145732
  53.7 212.3 %all-to-all-start.1 = ((bf16[64,2,64,512]{3,2,1,0:T(8,128)(2,1)}), bf16[64,2,64,512]{3,2,1,0:T(8,128)(2,1)}, u32[]{:S(2)}, u32[]{:S(2)}) async-start(bf16[64,2,64,512]{3,2,1,0:T(8,128)(2,1)} %gather_fusion), calls=%async_computation.1 | async-start | bytes 16777216 | tf_op jit(solution)/shard_map/all_to_all | solution.py:181
  60.5 205.5 %all-reduce.2.cloned.1.call-start = ((), (), s32[]{:S(2)}) async-start(), calls=%async_computation.3 | async-start | bytes 262144 | tf_op jit(solution)/shard_map/psum | solution.py:182
  60.6 1.3 copy-start.8
  61.3 221.5 %all-gather.2.cloned.1.call-start = ((), (), s32[]{:S(2)}) async-start(), calls=%async_computation.4 | async-start | bytes 10485760 | tf_op jit(solution)/shard_map/all_gather | solution.py:160
  61.9 1.9 copy-start.2
  125.6 141.5 %copy-start = (bf16[1024,512]{1,0:T(8,128)(2,1)S(1)}, bf16[1024,512]{1,0:T(8,128)(2,1)}, u32[]{:S(2)}) copy-start(bf16[1024,512]{1,0:T(8,128)(2,1)} %get-tuple-element.280) | copy-start | bytes 3145732
  278.3 20.4 %all-to-all-start.2 = ((bf16[4,256,512]{2,1,0:T(8,128)(2,1)}), bf16[4,256,512]{2,1,0:T(8,128)(2,1)S(1)}, u32[]{:S(2)}, u32[]{:S(2)}) async-start(bf16[4,256,512]{2,1,0:T(8,128)(2,1)} %bitcast.61), calls=%async_computation.2 | async-start | bytes 2097152 | tf_op jit(solution)/shard_map/all_to_all | solution.py:197
Sparse Core Ops, SparseCore 0:
  64.8 201.1 all-reduce.1
Sparse Core Ops, SparseCore 1:
  63.6 86.7 all-gather.1

commit v8 on v7

--- a/solution.py
+++ b/solution.py
@@ -144,6 +144,31 @@
     )(block_order, slot_owner, slot_shared, *operands)
 
 
+def grouped_projection(gathered, weight):
+    groups, rows, features = gathered.shape
+    width = weight.shape[2]
+    tile = math.gcd(width, 512)
+
+    def kernel(a_ref, w_ref, o_ref):
+        total = jnp.zeros((rows, tile), jnp.float32)
+        for g in range(groups):
+            part = jnp.dot(a_ref[g], w_ref[g], preferred_element_type=jnp.float32)
+            total = total + part.astype(jnp.bfloat16).astype(jnp.float32)
+        o_ref[...] = total.astype(jnp.bfloat16)
+
+    return pl.pallas_call(
+        kernel,
+        grid=(width // tile,),
+        in_specs=[
+            pl.BlockSpec((groups, rows, features), lambda n: (0, 0, 0)),
+            pl.BlockSpec((groups, features, tile), lambda n: (0, 0, n)),
+        ],
+        out_specs=pl.BlockSpec((rows, tile), lambda n: (0, n)),
+        out_shape=jax.ShapeDtypeStruct((rows, width), jnp.bfloat16),
+        compiler_params=pltpu.CompilerParams(dimension_semantics=("arbitrary",)),
+    )(gathered, weight)
+
+
 def build_table(slot_index, offset, in_use, total_slots):
     matches = (jnp.arange(total_slots, dtype=jnp.int32)[:, None] == slot_index[None, :]) & in_use[
         None, :
@@ -197,13 +222,7 @@
     gathered = lax.all_to_all(
         attended.reshape(groups, out_rows, features), "head", split_axis=0, concat_axis=0, tiled=True
     )
-    partials = jnp.einsum(
-        "gqf,gfn->gqn",
-        gathered,
-        full_weight.reshape(groups, features, full_weight.shape[1]),
-        preferred_element_type=jnp.float32,
-    ).astype(jnp.bfloat16)
-    return jnp.sum(partials.astype(jnp.float32), axis=0).astype(jnp.bfloat16)
+    return grouped_projection(gathered, full_weight.reshape(groups, features, full_weight.shape[1]))
 
 
 def solution(mesh):

time: 314 us -> 315 us (level)
  matrix products: 46.7 us -> 39.7 us
  Pallas kernels: 11.1 us -> 17.7 us
    dot_general x1 -> x0, matrix products: 6.92 us -> none  [layer(): jnp.einsum('gqf,gfn->gqn', gathered, full_weight.reshape(groups, features...]
    pallas_call x0 -> x1, Pallas kernels: none -> 6.59 us  [grouped_projection(): pl.pallas_call(kernel, grid=(width // tile,), in_specs=[pl.BlockSpec((gro...]
    unnamed x22 -> x24, local copies, waits for them, and re-layouts: 5.45 us -> 6.43 us
where the time goes in v8:
time: 315 us; the launch traced here: 314 us
  waiting for transfers between devices  171 us (54%)
  matrix products  39.7 us (13%)
  local copies, waits for them, and re-layouts  33.2 us (11%)
  starting transfers between devices  26.2 us (8%)
  Pallas kernels  17.7 us (6%)
  between operations  15 us (5%)
  other arithmetic  9.24 us (3%)
    psum x1, waiting for transfers between devices, layer(): lax.psum(jnp.where(seq_index == owners - 1, memory_store[mem_dev - 1], jn...  137 us
    sub x2, matrix products, masked_softmax(): weights = jnp.where(allowed, jnp.exp(scores - row_max), 0.0)  22.9 us
    all_to_all x1, waiting for transfers between devices, layer(): lax.all_to_all(slot_table, 'seq', split_axis=0, concat_axis=0, tiled=True)  17.7 us
    dot_general x2, matrix products, per_tile(): jnp.einsum('hqk,khd->qhd', attend_weights, value_tile, preferred_element_...  16.8 us
    all_to_all x1, waiting for transfers between devices, layer(): lax.all_to_all(attended.reshape(groups, out_rows, features), 'head', spli...  16 us
    all_to_all x1, starting transfers between devices, layer(): lax.all_to_all(slot_table, 'seq', split_axis=0, concat_axis=0, tiled=True)  12.7 us
    pallas_call x1, Pallas kernels, mixed_memory_attention(): pl.pallas_call(kernel, grid_spec=grid_spec, out_shape=jax.ShapeDtypeStruc...  11.1 us
    all_to_all x1, starting transfers between devices, layer(): lax.all_to_all(outgoing, 'seq', split_axis=0, concat_axis=0, tiled=True)  6.81 us
  transfers between devices with their start and end apart: 6, of which 3 were waited for; matrix products, arithmetic and copies ran while one was open for 25% of the time, Pallas kernels for 4%

profile of v8, /device:TPU:2, one launch (start us, length us, event | category | flops | bytes accessed | tf_op | source)
XLA Modules:
  0.0 313.7 jit_solution(10531894970375825385)
XLA Ops:
  7.4 1.6 copy.44
  8.9 0.0 copy-done.6
  9.0 0.5 copy.45
  9.5 0.0 copy-start.1
  9.5 0.0 copy-start.8
  9.5 1.7 pad_maximum_fusion.1
  11.2 0.0 copy-done.1
  11.2 1.9 collective-permute-start
  13.1 0.0 copy-done.8
  13.1 0.1 copy.43
  13.2 0.1 reshape.209
  13.3 0.0 copy-start.7
  13.3 0.5 compare_not_fusion
  13.8 0.1 select_reduce_fusion.1
  13.9 0.7 copy.46
  14.6 12.7 %all-to-all-start = ((s32[64,1,1]{2,1,0:T(1,128)}), s32[64,1,1]{2,1,0:T(1,128)S(1)}, u32[]{:S(2)}, u32[]{:S(2)}) async-start(s32[64,1,1]{2,1,0:T(1,128)} %copy.46), calls=%async_computation | async-start | bytes 65536 | tf_op jit(solution)/shard_map/all_to_all | solution.py:203
  27.4 1.7 pad_maximum_fusion
  29.1 0.0 copy-done.7
  29.2 17.7 %all-to-all-done = s32[64,1,1]{2,1,0:T(1,128)S(1)} async-done(((s32[64,1,1]{2,1,0:T(1,128)}), s32[64,1,1]{2,1,0:T(1,128)S(1)}, u32[]{:S(2)}, u32[]{:S(2)}) %all-to-all-start) | async-done | bytes 288 | tf_op jit(solution)/shard_map/all_to_all | solution.py:203
  46.9 1.2 maximum_reduce_fusion
  48.1 5.5 %gather_fusion = bf16[64,2,64,512]{3,2,1,0:T(8,128)(2,1)} fusion(bf16[16,2,64,512]{3,2,1,0:T(8,128)(2,1)S(1)} %pad_maximum_fusion, s32[1024]{0:T(1024)S(1)} %pad_clamp_fusion), kind=kCustom, calls=%fused_computation | custom fusion | bytes 16777472 | tf_op jit(solution)/shard_map/gather | solution.py:204
  53.7 0.0 collective-permute-done
  53.7 6.8 %all-to-all-start.1 = ((bf16[64,2,64,512]{3,2,1,0:T(8,128)(2,1)}), bf16[64,2,64,512]{3,2,1,0:T(8,128)(2,1)}, u32[]{:S(2)}, u32[]{:S(2)}) async-start(bf16[64,2,64,512]{3,2,1,0:T(8,128)(2,1)} %gather_fusion), calls=%async_computation.1 | async-start | bytes 16777216 | tf_op jit(solution)/shard_map/all_to_all | solution.py:206
  60.5 0.0 all-reduce.2.cloned.1.call-start
  60.5 0.0 copy-done.4
  60.6 0.0 copy-start.9
  60.6 0.7 select_bitcast_fusion
  61.3 0.0 all-reduce.2.cloned.1.call-update
  61.3 0.2 all-gather.2.cloned.1.call-start
  61.5 0.3 all-gather.2.cloned.1.call-update
  61.9 0.0 copy-start.2
  61.9 1.8 slice_bitcast_fusion
  63.7 0.0 copy-done.2
  63.8 1.7 pad_maximum_fusion.2
  65.4 60.2 %while.13 = (s32[]{:T(128)}, f32[2,512,4,128]{3,2,1,0:T(4,128)}, s32[2]{0:T(128)S(1)}, bf16[2048,512]{0,1:T(8,128)(2,1)S(1)}, s32[]{:T(128)}, /*index=5*/bf16[10...) while((s32[]{:T(128)}, f32[2,512,4,128]{3,2,1,0:T(4,128)}, ...), condition=%wide.region_5.6_spmd, body=%wide.region_2.5_spmd.sunk | while | flops 2444237824 | bytes 44080892 | solution.py:67
  65.4 0.6 dynamic_slice.37
  66.7 0.8 and_and_fusion.2
  67.5 3.3 %constant_dynamic-slice_fusion.5 = (bf16[1536,512]{0,1:T(8,128)(2,1)}, bf16[1536,512]{0,1:T(8,128)(2,1)}) fusion(bf16[2048,512]{0,1:T(8,128)(2,1)} %get-tuple-element.269, s32[]{:T(128)S(6)} %select_n.87, bf16[2048,512]{0,1:T(8,128)(2,1)S(1)} %get-tuple-element.266), kind=kLoop, calls=%fused_computation.19.clone.1 | loop fusion | bytes 6291460 | tf_op jit(solution)/shard_map/while/body/eval_jaxpr/dynamic_slice | solution.py:45
  70.9 1.1 constant_dynamic-slice_fusion.6
  71.9 1.0 copy.61
  72.9 11.5 %fusion.35 = (f32[4,512]{1,0:T(4,128)S(1)}, f32[4,512,1536]{2,1,0:T(8,128)}) fusion(pred[512,1536]{1,0:T(8,128)(4,1)S(1)} %and_and_fusion.2, bf16[512,4,128]{0,2,1:T(8,128)(2,1)} %bitcast.55, bf16[1536,4,128]{0,2,1:T(8,128)(2,1)} %bitcast.54), kind=kOutput, calls=%fused_computation.50.clone.1 | convolution fusion | flops 1629488640 | bytes 15474688 | tf_op jit(solution)/shard_map/while/body/eval_jaxpr/sub | solution.py:29
  84.4 8.4 %fusion.36 = f32[1,512,4,128]{1,3,2,0:T(8,128)} fusion(bf16[1536,4,128]{0,2,1:T(8,128)(2,1)} %bitcast.53, f32[4,512,1536]{2,1,0:T(8,128)} %get-tuple-element.235, f32[4,512]{1,0:T(4,128)S(1)} %get-tuple-element.236), kind=kOutput, calls=%fused_computation.13.clone.1 | convolution fusion | flops 811597824 | bytes 15212544 | tf_op jit(solution)/shard_map/while/body/eval_jaxpr/hqk,khd->qhd/dot_general | solution.py:63
  92.8 1.6 copy.62
  94.4 1.1 constant_dynamic-update-slice_fusion.2
  95.5 0.6 dynamic_slice.37
  96.7 0.8 and_and_fusion.2
  97.5 3.4 %constant_dynamic-slice_fusion.5 = (bf16[1536,512]{0,1:T(8,128)(2,1)}, bf16[1536,512]{0,1:T(8,128)(2,1)}) fusion(bf16[2048,512]{0,1:T(8,128)(2,1)} %get-tuple-element.269, s32[]{:T(128)S(6)} %select_n.87, bf16[2048,512]{0,1:T(8,128)(2,1)S(1)} %get-tuple-element.266), kind=kLoop, calls=%fused_computation.19.clone.1 | loop fusion | bytes 6291460 | tf_op jit(solution)/shard_map/while/body/eval_jaxpr/dynamic_slice | solution.py:45
  100.9 1.1 constant_dynamic-slice_fusion.6
  102.0 1.0 copy.61
  103.0 11.5 %fusion.35 = (f32[4,512]{1,0:T(4,128)S(1)}, f32[4,512,1536]{2,1,0:T(8,128)}) fusion(pred[512,1536]{1,0:T(8,128)(4,1)S(1)} %and_and_fusion.2, bf16[512,4,128]{0,2,1:T(8,128)(2,1)} %bitcast.55, bf16[1536,4,128]{0,2,1:T(8,128)(2,1)} %bitcast.54), kind=kOutput, calls=%fused_computation.50.clone.1 | convolution fusion | flops 1629488640 | bytes 15474688 | tf_op jit(solution)/shard_map/while/body/eval_jaxpr/sub | solution.py:29
  114.4 8.4 %fusion.36 = f32[1,512,4,128]{1,3,2,0:T(8,128)} fusion(bf16[1536,4,128]{0,2,1:T(8,128)(2,1)} %bitcast.53, f32[4,512,1536]{2,1,0:T(8,128)} %get-tuple-element.235, f32[4,512]{1,0:T(4,128)S(1)} %get-tuple-element.236), kind=kOutput, calls=%fused_computation.13.clone.1 | convolution fusion | flops 811597824 | bytes 15212544 | tf_op jit(solution)/shard_map/while/body/eval_jaxpr/hqk,khd->qhd/dot_general | solution.py:63
  122.9 1.6 copy.62
  124.5 1.1 constant_dynamic-update-slice_fusion.2
  125.6 3.2 %copy.58 = f32[128,8,4,128]{3,1,2,0:T(8,128)} copy(f32[128,8,4,128]{3,2,1,0:T(4,128)} %bitcast.65) | data formatting | bytes 4194304
  128.8 137.1 %all-reduce.2.cloned.1.call-done.sh_ref = bf16[2,64,512]{2,1,0:T(8,128)(2,1)} async-done(((bf16[2,64,512]{2,1,0:T(8,128)(2,1)}), bf16[2,64,512]{2,1,0:T(8,128)(2,1)}) %all-reduce.2.cloned.1.call-update) | async-done | bytes 131088 | tf_op jit(solution)/shard_map/psum | solution.py:207
  265.9 0.0 all-to-all-done.1.r0.r1.r2.r3
  265.9 0.7 broadcast_in_dim.77
  266.6 0.5 iota.38.order_ref
  267.1 0.0 copy-done
  267.1 11.1 %shard_map.82 = bf16[1024,512]{1,0:T(8,128)(2,1)} custom-call(s32[8]{0:T(128)} %iota.38.order_ref, s32[32]{0:T(128)} %copy-done.7, s32[32]{0:T(128)} %get-tuple-element.177.flag_ref, bf16[1024,512]{1,0:T(8,128)(2,1)S(1)} %copy-done, bf16[64,2,64,512]{3,2,1,0:T(8,128)(2,1)} %all-to-all-done.1.r0.r1.r2.r3, ...), custom_call_target="tpu_custom_call" | custom-call | tf_op jit(solution)/shard_map/pallas_call | solution.py:138
  278.2 4.5 %all-to-all-start.2 = ((bf16[4,256,512]{2,1,0:T(8,128)(2,1)}), bf16[4,256,512]{2,1,0:T(8,128)(2,1)S(1)}, u32[]{:S(2)}, u32[]{:S(2)}) async-start(bf16[4,256,512]{2,1,0:T(8,128)(2,1)} %bitcast.60), calls=%async_computation.2 | async-start | bytes 2097152 | tf_op jit(solution)/shard_map/all_to_all | solution.py:222
  282.7 16.0 %all-to-all-done.2.a_ref = bf16[4,256,512]{2,1,0:T(8,128)(2,1)S(1)} async-done(((bf16[4,256,512]{2,1,0:T(8,128)(2,1)}), bf16[4,256,512]{2,1,0:T(8,128)(2,1)S(1)}, u32[]{:S(2)}, u32[]{:S(2)}) %all-to-all-start.2) | async-done | bytes 1048608 | tf_op jit(solution)/shard_map/all_to_all | solution.py:222
  298.7 1.0 copy-done.3
  299.7 6.6 %shard_map.83 = bf16[256,2048]{1,0:T(8,128)(2,1)} custom-call(bf16[4,256,512]{2,1,0:T(8,128)(2,1)} %copy-done.3, bf16[4,512,2048]{2,1,0:T(8,128)(2,1)} %bitcast.58), custom_call_target="tpu_custom_call" | custom-call | tf_op jit(solution)/shard_map/pallas_call | solution.py:159
  (20 shorter events, 0.1 us)
Async XLA Ops:
  7.4 1.6 copy-start.6
  9.5 1.7 copy-start.1
  9.5 3.6 %copy-start.8 = (s32[8,4]{0,1:T(4,128)S(1)}, s32[8,4]{0,1:T(4,128)}, u32[]{:S(2)}) copy-start(s32[8,4]{0,1:T(4,128)} %param.15) | copy-start | bytes 388
  11.2 42.5 %collective-permute-start = (bf16[2,1024,512]{1,2,0:T(8,128)(2,1)}, bf16[2,1024,512]{1,2,0:T(8,128)(2,1)}, u32[]{:S(2)}, u32[]{:S(2)}) collective-permute-start(bf16[2,1024,512]{1,2,0:T(8,128)(2,1)} %pad_maximum_fusion.1), channel_id=1, source_target_pairs={{0,4},{4,8},{8,12},{12,16},{16,20},{20,24},{24,28},{28,32},{32,36}... | collective-permute-start | bytes 6291464 | tf_op jit(solution)/shard_map/ppermute | solution.py:24
  13.3 15.9 %copy-start.7 = (s32[32]{0:T(128)}, s32[32]{0:T(128)S(1)}, u32[]{:S(2)}) copy-start(s32[32]{0:T(128)S(1)} %get-tuple-element.179.owner_ref) | copy-start | bytes 388
  14.6 32.2 %all-to-all-start = ((s32[64,1,1]{2,1,0:T(1,128)}), s32[64,1,1]{2,1,0:T(1,128)S(1)}, u32[]{:S(2)}, u32[]{:S(2)}) async-start(s32[64,1,1]{2,1,0:T(1,128)} %copy.46), calls=%async_computation | async-start | bytes 65536 | tf_op jit(solution)/shard_map/all_to_all | solution.py:203
  53.7 6.9 %copy-start.4 = (bf16[1024,512]{1,0:T(8,128)(2,1)S(1)}, bf16[1024,512]{1,0:T(8,128)(2,1)}, u32[]{:S(2)}) copy-start(bf16[1024,512]{1,0:T(8,128)(2,1)} %param.14) | copy-start | bytes 3145732
  53.7 6.9 %copy-start.5 = (bf16[1024,512]{1,0:T(8,128)(2,1)S(1)}, bf16[1024,512]{1,0:T(8,128)(2,1)}, u32[]{:S(2)}) copy-start(bf16[1024,512]{1,0:T(8,128)(2,1)} %param.13) | copy-start | bytes 3145732
  53.7 212.3 %all-to-all-start.1 = ((bf16[64,2,64,512]{3,2,1,0:T(8,128)(2,1)}), bf16[64,2,64,512]{3,2,1,0:T(8,128)(2,1)}, u32[]{:S(2)}, u32[]{:S(2)}) async-start(bf16[64,2,64,512]{3,2,1,0:T(8,128)(2,1)} %gather_fusion), calls=%async_computation.1 | async-start | bytes 16777216 | tf_op jit(solution)/shard_map/all_to_all | solution.py:206
  60.5 205.5 %all-reduce.2.cloned.1.call-start = ((), (), s32[]{:S(2)}) async-start(), calls=%async_computation.3 | async-start | bytes 262144 | tf_op jit(solution)/shard_map/psum | solution.py:207
  60.6 1.3 copy-start.9
  61.3 221.4 %all-gather.2.cloned.1.call-start = ((), (), s32[]{:S(2)}) async-start(), calls=%async_computation.4 | async-start | bytes 10485760 | tf_op jit(solution)/shard_map/all_gather | solution.py:185
  61.9 1.9 copy-start.2
  125.6 141.5 %copy-start = (bf16[1024,512]{1,0:T(8,128)(2,1)S(1)}, bf16[1024,512]{1,0:T(8,128)(2,1)}, u32[]{:S(2)}) copy-start(bf16[1024,512]{1,0:T(8,128)(2,1)} %get-tuple-element.280) | copy-start | bytes 3145732
  278.2 20.5 %all-to-all-start.2 = ((bf16[4,256,512]{2,1,0:T(8,128)(2,1)}), bf16[4,256,512]{2,1,0:T(8,128)(2,1)S(1)}, u32[]{:S(2)}, u32[]{:S(2)}) async-start(bf16[4,256,512]{2,1,0:T(8,128)(2,1)} %bitcast.60), calls=%async_computation.2 | async-start | bytes 2097152 | tf_op jit(solution)/shard_map/all_to_all | solution.py:222
  298.7 1.0 copy-start.3
Sparse Core Ops, SparseCore 0:
  64.8 201.1 all-reduce.1
Sparse Core Ops, SparseCore 1:
  63.6 86.7 all-gather.1

commit v9 on v7

--- a/solution.py
+++ b/solution.py
@@ -144,6 +144,44 @@
     )(block_order, slot_owner, slot_shared, *operands)
 
 
+def grouped_projection(own_part, gathered, weight, head_index):
+    groups, rows, features = gathered.shape
+    width = weight.shape[2]
+    tile = math.gcd(width, 512)
+
+    def kernel(head_ref, own_ref, *refs):
+        parts = refs[: groups - 1]
+        weights = refs[groups - 1 : 2 * (groups - 1)]
+        o_ref = refs[-1]
+        total = own_ref[...].astype(jnp.float32)
+        for a_ref, w_ref in zip(parts, weights):
+            part = jnp.dot(a_ref[0], w_ref[0], preferred_element_type=jnp.float32)
+            total = total + part.astype(jnp.bfloat16).astype(jnp.float32)
+        o_ref[...] = total.astype(jnp.bfloat16)
+
+    def part_spec(k):
+        return pl.BlockSpec((1, rows, features), lambda n, h: ((h[0] + k) % groups, 0, 0))
+
+    def weight_spec(k):
+        return pl.BlockSpec((1, features, tile), lambda n, h: ((h[0] + k) % groups, 0, n))
+
+    others = range(1, groups)
+    grid_spec = pltpu.PrefetchScalarGridSpec(
+        num_scalar_prefetch=1,
+        grid=(width // tile,),
+        in_specs=[pl.BlockSpec((rows, tile), lambda n, h: (0, n))]
+        + [part_spec(k) for k in others]
+        + [weight_spec(k) for k in others],
+        out_specs=pl.BlockSpec((rows, tile), lambda n, h: (0, n)),
+    )
+    return pl.pallas_call(
+        kernel,
+        grid_spec=grid_spec,
+        out_shape=jax.ShapeDtypeStruct((rows, width), jnp.bfloat16),
+        compiler_params=pltpu.CompilerParams(dimension_semantics=("arbitrary",)),
+    )(head_index, own_part, *([gathered] * (groups - 1)), *([weight] * (groups - 1)))
+
+
 def build_table(slot_index, offset, in_use, total_slots):
     matches = (jnp.arange(total_slots, dtype=jnp.int32)[:, None] == slot_index[None, :]) & in_use[
         None, :
@@ -197,13 +235,17 @@
     gathered = lax.all_to_all(
         attended.reshape(groups, out_rows, features), "head", split_axis=0, concat_axis=0, tiled=True
     )
-    partials = jnp.einsum(
-        "gqf,gfn->gqn",
+    head_index = lax.axis_index("head")
+    own_rows = lax.dynamic_index_in_dim(
+        attended.reshape(groups, out_rows, features), head_index, 0, keepdims=False
+    )
+    own_part = jnp.dot(own_rows, out_weight, preferred_element_type=jnp.float32).astype(jnp.bfloat16)
+    return grouped_projection(
+        own_part,
         gathered,
         full_weight.reshape(groups, features, full_weight.shape[1]),
-        preferred_element_type=jnp.float32,
-    ).astype(jnp.bfloat16)
-    return jnp.sum(partials.astype(jnp.float32), axis=0).astype(jnp.bfloat16)
+        head_index.astype(jnp.int32).reshape(1),
+    )
 
 
 def solution(mesh):

time: 314 us -> 314 us (level)
  Pallas kernels: 11.1 us -> 17.3 us
  matrix products: 46.7 us -> 42.4 us
    pallas_call x0 -> x1, Pallas kernels: none -> 6.11 us  [grouped_projection(): pl.pallas_call(kernel, grid_spec=grid_spec, out_shape=jax.ShapeDtypeStruc...]
    dot_general x1, matrix products: 6.92 us -> 2.65 us  [layer(): jnp.dot(own_rows, out_weight, preferred_element_type=jnp.float32)]
    unnamed x22 -> x26, local copies, waits for them, and re-layouts: 5.45 us -> 6.47 us
  transfers between devices with their start and end apart: 6 -> 6, of which waited for: 3 -> 3; matrix products, arithmetic and copies ran while one was open for 25% -> 26% of each run, Pallas kernels for 4% -> 4%
where the time goes in v9:
time: 314 us; the launch traced here: 313 us
  waiting for transfers between devices  169 us (54%)
  matrix products  42.4 us (14%)
  local copies, waits for them, and re-layouts  33.2 us (11%)
  starting transfers between devices  26.3 us (8%)
  Pallas kernels  17.3 us (6%)
  between operations  15 us (5%)
  other arithmetic  9.25 us (3%)
    psum x1, waiting for transfers between devices, layer(): lax.psum(jnp.where(seq_index == owners - 1, memory_store[mem_dev - 1], jn...  137 us
    sub x2, matrix products, masked_softmax(): weights = jnp.where(allowed, jnp.exp(scores - row_max), 0.0)  22.9 us
    all_to_all x1, waiting for transfers between devices, layer(): lax.all_to_all(slot_table, 'seq', split_axis=0, concat_axis=0, tiled=True)  17.7 us
    dot_general x2, matrix products, per_tile(): jnp.einsum('hqk,khd->qhd', attend_weights, value_tile, preferred_element_...  16.8 us
    all_to_all x1, waiting for transfers between devices, layer(): lax.all_to_all(attended.reshape(groups, out_rows, features), 'head', spli...  13.3 us
    all_to_all x1, starting transfers between devices, layer(): lax.all_to_all(slot_table, 'seq', split_axis=0, concat_axis=0, tiled=True)  12.7 us
    pallas_call x1, Pallas kernels, mixed_memory_attention(): pl.pallas_call(kernel, grid_spec=grid_spec, out_shape=jax.ShapeDtypeStruc...  11.1 us
    all_to_all x1, starting transfers between devices, layer(): lax.all_to_all(outgoing, 'seq', split_axis=0, concat_axis=0, tiled=True)  6.8 us
  transfers between devices with their start and end apart: 6, of which 3 were waited for; matrix products, arithmetic and copies ran while one was open for 26% of the time, Pallas kernels for 4%

profile of v9, /device:TPU:2, one launch (start us, length us, event | category | flops | bytes accessed | tf_op | source)
XLA Modules:
  0.0 313.4 jit_solution(4130741767075240469)
XLA Ops:
  7.4 1.6 copy.44
  9.0 0.5 copy.45
  9.5 0.0 copy-start.2
  9.5 0.0 copy-start.9
  9.5 1.6 pad_maximum_fusion.1
  11.2 1.9 collective-permute-start
  13.1 0.0 copy-done.9
  13.1 0.1 copy.43
  13.2 0.1 reshape.214
  13.3 0.0 copy-start.8
  13.3 0.6 compare_not_fusion
  13.9 0.1 select_reduce_fusion.1
  14.0 0.7 copy.46
  14.7 12.7 %all-to-all-start = ((s32[64,1,1]{2,1,0:T(1,128)}), s32[64,1,1]{2,1,0:T(1,128)S(1)}, u32[]{:S(2)}, u32[]{:S(2)}) async-start(s32[64,1,1]{2,1,0:T(1,128)} %copy.46), calls=%async_computation | async-start | bytes 65536 | tf_op jit(solution)/shard_map/all_to_all | solution.py:216
  27.4 1.7 pad_maximum_fusion
  29.2 17.7 %all-to-all-done = s32[64,1,1]{2,1,0:T(1,128)S(1)} async-done(((s32[64,1,1]{2,1,0:T(1,128)}), s32[64,1,1]{2,1,0:T(1,128)S(1)}, u32[]{:S(2)}, u32[]{:S(2)}) %all-to-all-start) | async-done | bytes 288 | tf_op jit(solution)/shard_map/all_to_all | solution.py:216
  46.9 1.2 maximum_reduce_fusion
  48.1 5.6 %gather_fusion = bf16[64,2,64,512]{3,2,1,0:T(8,128)(2,1)} fusion(bf16[16,2,64,512]{3,2,1,0:T(8,128)(2,1)S(1)} %pad_maximum_fusion, s32[1024]{0:T(1024)S(1)} %pad_clamp_fusion), kind=kCustom, calls=%fused_computation | custom fusion | bytes 16777472 | tf_op jit(solution)/shard_map/gather | solution.py:217
  53.7 0.0 collective-permute-done
  53.7 6.8 %all-to-all-start.1 = ((bf16[64,2,64,512]{3,2,1,0:T(8,128)(2,1)}), bf16[64,2,64,512]{3,2,1,0:T(8,128)(2,1)}, u32[]{:S(2)}, u32[]{:S(2)}) async-start(bf16[64,2,64,512]{3,2,1,0:T(8,128)(2,1)} %gather_fusion), calls=%async_computation.1 | async-start | bytes 16777216 | tf_op jit(solution)/shard_map/all_to_all | solution.py:219
  60.5 0.0 all-reduce.2.cloned.1.call-start
  60.5 0.0 copy-done.5
  60.5 0.0 copy-done.6
  60.6 0.0 copy-start.10
  60.6 0.7 select_bitcast_fusion
  61.2 0.0 all-reduce.2.cloned.1.call-update
  61.3 0.2 all-gather.2.cloned.1.call-start
  61.5 0.3 all-gather.2.cloned.1.call-update
  61.9 0.0 copy-start.3
  61.9 1.8 slice_bitcast_fusion
  63.7 0.0 copy-done.3
  63.7 1.7 pad_maximum_fusion.2
  65.4 60.2 %while.13 = (s32[]{:T(128)}, f32[2,512,4,128]{3,2,1,0:T(4,128)}, s32[2]{0:T(128)S(1)}, bf16[2048,512]{0,1:T(8,128)(2,1)S(1)}, s32[]{:T(128)}, /*index=5*/bf16[10...) while((s32[]{:T(128)}, f32[2,512,4,128]{3,2,1,0:T(4,128)}, ...), condition=%wide.region_5.6_spmd, body=%wide.region_2.5_spmd.sunk | while | flops 2444237824 | bytes 44080892 | solution.py:67
  65.4 0.6 dynamic_slice.46
  66.7 0.8 and_and_fusion.2
  67.5 3.3 %constant_dynamic-slice_fusion.5 = (bf16[1536,512]{0,1:T(8,128)(2,1)}, bf16[1536,512]{0,1:T(8,128)(2,1)}) fusion(bf16[2048,512]{0,1:T(8,128)(2,1)} %get-tuple-element.269, s32[]{:T(128)S(6)} %select_n.92, bf16[2048,512]{0,1:T(8,128)(2,1)S(1)} %get-tuple-element.266), kind=kLoop, calls=%fused_computation.19.clone.1 | loop fusion | bytes 6291460 | tf_op jit(solution)/shard_map/while/body/eval_jaxpr/dynamic_slice | solution.py:45
  70.8 1.1 constant_dynamic-slice_fusion.6
  71.9 1.0 copy.61
  72.9 11.5 %fusion.39 = (f32[4,512]{1,0:T(4,128)S(1)}, f32[4,512,1536]{2,1,0:T(8,128)}) fusion(pred[512,1536]{1,0:T(8,128)(4,1)S(1)} %and_and_fusion.2, bf16[512,4,128]{0,2,1:T(8,128)(2,1)} %bitcast.63, bf16[1536,4,128]{0,2,1:T(8,128)(2,1)} %bitcast.62), kind=kOutput, calls=%fused_computation.54.clone.1 | convolution fusion | flops 1629488640 | bytes 15474688 | tf_op jit(solution)/shard_map/while/body/eval_jaxpr/sub | solution.py:29
  84.4 8.4 %fusion.40 = f32[1,512,4,128]{1,3,2,0:T(8,128)} fusion(bf16[1536,4,128]{0,2,1:T(8,128)(2,1)} %bitcast.61, f32[4,512,1536]{2,1,0:T(8,128)} %get-tuple-element.235, f32[4,512]{1,0:T(4,128)S(1)} %get-tuple-element.236), kind=kOutput, calls=%fused_computation.13.clone.1 | convolution fusion | flops 811597824 | bytes 15212544 | tf_op jit(solution)/shard_map/while/body/eval_jaxpr/hqk,khd->qhd/dot_general | solution.py:63
  92.7 1.6 copy.62
  94.4 1.1 constant_dynamic-update-slice_fusion.2
  95.4 0.6 dynamic_slice.46
  96.7 0.8 and_and_fusion.2
  97.5 3.4 %constant_dynamic-slice_fusion.5 = (bf16[1536,512]{0,1:T(8,128)(2,1)}, bf16[1536,512]{0,1:T(8,128)(2,1)}) fusion(bf16[2048,512]{0,1:T(8,128)(2,1)} %get-tuple-element.269, s32[]{:T(128)S(6)} %select_n.92, bf16[2048,512]{0,1:T(8,128)(2,1)S(1)} %get-tuple-element.266), kind=kLoop, calls=%fused_computation.19.clone.1 | loop fusion | bytes 6291460 | tf_op jit(solution)/shard_map/while/body/eval_jaxpr/dynamic_slice | solution.py:45
  100.8 1.1 constant_dynamic-slice_fusion.6
  101.9 1.0 copy.61
  102.9 11.5 %fusion.39 = (f32[4,512]{1,0:T(4,128)S(1)}, f32[4,512,1536]{2,1,0:T(8,128)}) fusion(pred[512,1536]{1,0:T(8,128)(4,1)S(1)} %and_and_fusion.2, bf16[512,4,128]{0,2,1:T(8,128)(2,1)} %bitcast.63, bf16[1536,4,128]{0,2,1:T(8,128)(2,1)} %bitcast.62), kind=kOutput, calls=%fused_computation.54.clone.1 | convolution fusion | flops 1629488640 | bytes 15474688 | tf_op jit(solution)/shard_map/while/body/eval_jaxpr/sub | solution.py:29
  114.4 8.4 %fusion.40 = f32[1,512,4,128]{1,3,2,0:T(8,128)} fusion(bf16[1536,4,128]{0,2,1:T(8,128)(2,1)} %bitcast.61, f32[4,512,1536]{2,1,0:T(8,128)} %get-tuple-element.235, f32[4,512]{1,0:T(4,128)S(1)} %get-tuple-element.236), kind=kOutput, calls=%fused_computation.13.clone.1 | convolution fusion | flops 811597824 | bytes 15212544 | tf_op jit(solution)/shard_map/while/body/eval_jaxpr/hqk,khd->qhd/dot_general | solution.py:63
  122.8 1.6 copy.62
  124.5 1.1 constant_dynamic-update-slice_fusion.2
  125.6 3.2 %copy.58 = f32[128,8,4,128]{3,1,2,0:T(8,128)} copy(f32[128,8,4,128]{3,2,1,0:T(4,128)} %bitcast.73) | data formatting | bytes 4194304
  128.8 137.2 %all-reduce.2.cloned.1.call-done.sh_ref = bf16[2,64,512]{2,1,0:T(8,128)(2,1)} async-done(((bf16[2,64,512]{2,1,0:T(8,128)(2,1)}), bf16[2,64,512]{2,1,0:T(8,128)(2,1)}) %all-reduce.2.cloned.1.call-update) | async-done | bytes 131088 | tf_op jit(solution)/shard_map/psum | solution.py:220
  265.9 0.0 all-to-all-done.1.r0.r1.r2.r3
  265.9 0.7 broadcast_in_dim.77
  266.6 0.5 iota.38.order_ref
  267.1 0.0 copy-done.1
  267.1 11.1 %shard_map.82 = bf16[1024,512]{1,0:T(8,128)(2,1)} custom-call(s32[8]{0:T(128)} %iota.38.order_ref, s32[32]{0:T(128)} %copy-done.8, s32[32]{0:T(128)} %get-tuple-element.177.flag_ref, bf16[1024,512]{1,0:T(8,128)(2,1)S(1)} %copy-done.1, bf16[64,2,64,512]{3,2,1,0:T(8,128)(2,1)} %all-to-all-done.1.r0.r1.r2.r3, ...), custom_call_target="tpu_custom_call" | custom-call | tf_op jit(solution)/shard_map/pallas_call | solution.py:138
  278.2 4.6 %all-to-all-start.2 = ((bf16[4,256,512]{2,1,0:T(8,128)(2,1)}), bf16[4,256,512]{2,1,0:T(8,128)(2,1)S(1)}, u32[]{:S(2)}, u32[]{:S(2)}) async-start(bf16[4,256,512]{2,1,0:T(8,128)(2,1)} %bitcast.67), calls=%async_computation.2 | async-start | bytes 2097152 | tf_op jit(solution)/shard_map/all_to_all | solution.py:235
  282.8 0.0 copy-done.4
  282.8 2.6 convolution_convert_fusion.own_ref
  285.5 13.3 %all-to-all-done.2.refs_0_.refs_1_.refs_2_ = bf16[4,256,512]{2,1,0:T(8,128)(2,1)S(1)} async-done(((bf16[4,256,512]{2,1,0:T(8,128)(2,1)}), bf16[4,256,512]{2,1,0:T(8,128)(2,1)S(1)}, u32[]{:S(2)}, u32[]{:S(2)}) %all-to-all-start.2) | async-done | bytes 1048608 | tf_op jit(solution)/shard_map/all_to_all | solution.py:235
  298.8 1.0 copy-done
  299.8 6.1 %shard_map.83 = bf16[256,2048]{1,0:T(8,128)(2,1)} custom-call(s32[1]{0:T(128)} %bitcast.6.head_ref, bf16[256,2048]{1,0:T(8,128)(2,1)} %convolution_convert_fusion.own_ref, bf16[4,256,512]{2,1,0:T(8,128)(2,1)} %copy-done, bf16[4,256,512]{2,1,0:T(8,128)(2,1)} %copy-done, bf16[4,256,512]{2,1,0:T(8,128)(2,1)} %copy-done, bf16[4,512,2048]{2,1,0:T(8,128)(2,1)} %bitcast.58, ...), custom_call_target="tpu_custom_call" | custom-call | tf_op jit(solution)/shard_map/pallas_call | solution.py:177
  (23 shorter events, 0.1 us)
Async XLA Ops:
  7.4 1.6 copy-start.7
  9.5 1.7 copy-start.2
  9.5 3.6 %copy-start.9 = (s32[8,4]{0,1:T(4,128)S(1)}, s32[8,4]{0,1:T(4,128)}, u32[]{:S(2)}) copy-start(s32[8,4]{0,1:T(4,128)} %param.15) | copy-start | bytes 388
  11.2 42.5 %collective-permute-start = (bf16[2,1024,512]{1,2,0:T(8,128)(2,1)}, bf16[2,1024,512]{1,2,0:T(8,128)(2,1)}, u32[]{:S(2)}, u32[]{:S(2)}) collective-permute-start(bf16[2,1024,512]{1,2,0:T(8,128)(2,1)} %pad_maximum_fusion.1), channel_id=1, source_target_pairs={{0,4},{4,8},{8,12},{12,16},{16,20},{20,24},{24,28},{28,32},{32,36}... | collective-permute-start | bytes 6291464 | tf_op jit(solution)/shard_map/ppermute | solution.py:24
  13.3 15.9 %copy-start.8 = (s32[32]{0:T(128)}, s32[32]{0:T(128)S(1)}, u32[]{:S(2)}) copy-start(s32[32]{0:T(128)S(1)} %get-tuple-element.179.owner_ref) | copy-start | bytes 388
  14.7 32.2 %all-to-all-start = ((s32[64,1,1]{2,1,0:T(1,128)}), s32[64,1,1]{2,1,0:T(1,128)S(1)}, u32[]{:S(2)}, u32[]{:S(2)}) async-start(s32[64,1,1]{2,1,0:T(1,128)} %copy.46), calls=%async_computation | async-start | bytes 65536 | tf_op jit(solution)/shard_map/all_to_all | solution.py:216
  53.7 6.9 %copy-start.5 = (bf16[1024,512]{1,0:T(8,128)(2,1)S(1)}, bf16[1024,512]{1,0:T(8,128)(2,1)}, u32[]{:S(2)}) copy-start(bf16[1024,512]{1,0:T(8,128)(2,1)} %param.14) | copy-start | bytes 3145732
  53.7 6.9 %copy-start.6 = (bf16[1024,512]{1,0:T(8,128)(2,1)S(1)}, bf16[1024,512]{1,0:T(8,128)(2,1)}, u32[]{:S(2)}) copy-start(bf16[1024,512]{1,0:T(8,128)(2,1)} %param.13) | copy-start | bytes 3145732
  53.7 212.3 %all-to-all-start.1 = ((bf16[64,2,64,512]{3,2,1,0:T(8,128)(2,1)}), bf16[64,2,64,512]{3,2,1,0:T(8,128)(2,1)}, u32[]{:S(2)}, u32[]{:S(2)}) async-start(bf16[64,2,64,512]{3,2,1,0:T(8,128)(2,1)} %gather_fusion), calls=%async_computation.1 | async-start | bytes 16777216 | tf_op jit(solution)/shard_map/all_to_all | solution.py:219
  60.5 205.5 %all-reduce.2.cloned.1.call-start = ((), (), s32[]{:S(2)}) async-start(), calls=%async_computation.3 | async-start | bytes 262144 | tf_op jit(solution)/shard_map/psum | solution.py:220
  60.6 1.3 copy-start.10
  61.3 224.2 %all-gather.2.cloned.1.call-start = ((), (), s32[]{:S(2)}) async-start(), calls=%async_computation.4 | async-start | bytes 10485760 | tf_op jit(solution)/shard_map/all_gather | solution.py:198
  61.9 1.9 copy-start.3
  125.6 141.5 %copy-start.1 = (bf16[1024,512]{1,0:T(8,128)(2,1)S(1)}, bf16[1024,512]{1,0:T(8,128)(2,1)}, u32[]{:S(2)}) copy-start(bf16[1024,512]{1,0:T(8,128)(2,1)} %get-tuple-element.282) | copy-start | bytes 3145732
  278.2 4.6 %copy-start.4 = (bf16[512,2048]{1,0:T(8,128)(2,1)S(1)}, bf16[512,2048]{1,0:T(8,128)(2,1)}, u32[]{:S(2)}) copy-start(bf16[512,2048]{1,0:T(8,128)(2,1)} %param.17) | copy-start | bytes 6291460
  278.2 20.6 %all-to-all-start.2 = ((bf16[4,256,512]{2,1,0:T(8,128)(2,1)}), bf16[4,256,512]{2,1,0:T(8,128)(2,1)S(1)}, u32[]{:S(2)}, u32[]{:S(2)}) async-start(bf16[4,256,512]{2,1,0:T(8,128)(2,1)} %bitcast.67), calls=%async_computation.2 | async-start | bytes 2097152 | tf_op jit(solution)/shard_map/all_to_all | solution.py:235
  298.8 1.0 copy-start
Sparse Core Ops, SparseCore 0:
  64.8 201.1 all-reduce.1
Sparse Core Ops, SparseCore 1:
  63.6 86.7 all-gather.1
